TPU v7x, 256 devices: a whole 4x4x8 slice. The times are simulated.
256 devices in a mesh: tm: 16 (over y, x), space: 16 (over z, core).
Axes of the slice: x: 4, y: 4, z: 8, core: 2. Of those that a mesh axis runs over, the one named last changes fastest.
Arguments:
- query_heads: bfloat16 [32, 64, 64, 2240], P('tm', 'space'), may hold values from -10.5 to 10.5
- key_heads: bfloat16 [32, 64, 64, 2240], P('tm', 'space'), may hold values from -10.5 to 10.5
- value_heads: bfloat16 [32, 64, 64, 2240], P('tm', 'space'), may hold values from -12 to 12
- head_gain: float32 [2240], replicated, may hold values from 0.1 to 1.9
- spatial_kernel: float32 [9, 2240], replicated, may hold values from -2 to 2
- temporal_kernel: float32 [3, 2240], replicated, may hold values from -3.5 to 3.5
- out_weight: bfloat16 [2240, 2240], P('space', 'tm'), may hold values from -0.125 to 0.125
Outputs:
- mixed_out: bfloat16 [32, 64, 64, 2240], P('tm', 'space')
All inputs are finite; a program needn't handle non-finite values.
Results may differ from a plain program's by a relative error of at most 0.0057.
Values may be sent and summed in bfloat16 or wider, within the bound.
No kernel may reach another device: no remote copies, remote signals or barrier semaphores. Data moves between devices by JAX's collectives and lax.ppermute only.
A program may use at most 128 MiB of HBM per device.

v0:
```python
import jax
import jax.numpy as jnp
from jax import lax
from jax.sharding import PartitionSpec as P

HEADS = 20
HEAD_DIM = 112


epsilon = 1e-06


def entering(part, axis, combine, identity):
    place = lax.axis_index(axis)
    gathered = lax.all_gather(part, axis)
    state = jnp.zeros_like(part) + jnp.asarray(identity, part.dtype)

    def one(hop, state):
        return combine(state, lax.dynamic_index_in_dim(gathered, hop, 0, False))

    return lax.fori_loop(0, place, one, state)


def extended(block, sides, width):
    for axis, dim in sides:
        count = lax.axis_size(axis)
        forward = [(i, i + 1) for i in range(count - 1)]
        backward = [(target, source) for source, target in forward]
        low = lax.ppermute(
            lax.slice_in_dim(block, block.shape[dim] - width, None, axis=dim), axis, forward
        )
        high = lax.ppermute(lax.slice_in_dim(block, 0, width, axis=dim), axis, backward)
        block = jnp.concatenate([low, block, high], axis=dim)
    return block


def from_behind(block, axis, distance):
    devices = range(lax.axis_size(axis))
    route = [(i - distance, i) for i in devices if i - distance in devices]
    return lax.ppermute(block, axis, route)


def add_states(earlier, latter):
    return earlier + latter


def spatial_conv(padded, spatial_kernel):
    frame_count = padded.shape[0]
    row_count = padded.shape[1] - 2
    col_count = padded.shape[2]
    widened = jnp.pad(padded, ((0, 0), (0, 0), (1, 1), (0, 0)))
    summed = jnp.zeros((frame_count, row_count, col_count, padded.shape[3]), jnp.float32)
    for row_step in range(3):
        for col_step in range(3):
            summed = summed + spatial_kernel[3 * row_step + col_step] * widened[
                :, row_step : row_step + row_count, col_step : col_step + col_count
            ].astype(jnp.float32)
    return summed.astype(jnp.bfloat16)


def per_device(
    query_heads, key_heads, value_heads, head_gain, spatial_kernel, temporal_kernel, out_weight
):
    frame_count, row_count, col_count, model_width = query_heads.shape
    token_count = frame_count * row_count * col_count
    queries = query_heads.reshape(token_count, HEADS, HEAD_DIM)
    key_rows = key_heads.reshape(token_count, HEADS, HEAD_DIM)
    value_rows = value_heads.reshape(token_count, HEADS, HEAD_DIM)
    local_state = jnp.einsum(
        "thd,the->hde", jnp.maximum(key_rows, 0), value_rows, preferred_element_type=jnp.float32
    )
    summed = lax.psum(local_state, "space")
    earlier = entering(summed, "tm", add_states, jnp.zeros_like(summed))
    state_low = (earlier + summed).astype(jnp.bfloat16)
    attended = jnp.einsum(
        "thd,hde->the", jnp.maximum(queries, 0), state_low, preferred_element_type=jnp.float32
    )
    mean_square = jnp.mean(attended * attended, axis=-1, keepdims=True)
    normed = (attended * lax.rsqrt(mean_square + epsilon)).reshape(
        frame_count, row_count, col_count, model_width
    ) * head_gain
    padded = extended(value_heads, (("space", 1),), 1)
    spatial = spatial_conv(padded, spatial_kernel)
    earlier_frames = from_behind(spatial, "tm", 1)
    window = jnp.concatenate([earlier_frames, spatial], axis=0)
    temporal = jnp.zeros(normed.shape, jnp.float32)
    for back_step in range(3):
        temporal = temporal + temporal_kernel[back_step] * window[
            2 - back_step : 2 - back_step + frame_count
        ].astype(jnp.float32)
    mixed = (normed + temporal).astype(jnp.bfloat16).reshape(token_count, model_width)
    weight_band = lax.all_gather(out_weight, "tm", axis=1, tiled=True)
    projected = jnp.dot(
        mixed,
        lax.all_gather(weight_band, "space", axis=0, tiled=True),
        preferred_element_type=jnp.float32,
    )
    return projected.astype(jnp.bfloat16).reshape(frame_count, row_count, col_count, model_width)


def solution(mesh):
    placed = (
        P("tm", "space", None, None),
        P("tm", "space", None, None),
        P("tm", "space", None, None),
        P(),
        P(),
        P(),
        P("space", "tm"),
    )
    return jax.shard_map(
        per_device,
        mesh=mesh,
        in_specs=placed,
        out_specs=P("tm", "space", None, None),
        check_vma=False,
    )
```

profile of v0, /device:TPU:30, one launch (start us, length us, event | category | flops | bytes accessed | tf_op | source)
XLA Modules:
  0.0 405.4 jit_solution(10233113582889997337)
XLA Ops:
  6.5 3.4 broadcast_maximum_fusion.1
  9.9 6.5 %max.13 = bf16[512,20,112]{2,1,0:T(8,128)(2,1)} reshape(bf16[2,4,64,2240]{3,2,1,0:T(8,128)(2,1)} %broadcast_maximum_fusion.1) | data formatting | bytes 4587520 | tf_op jit(solution)/shard_map/max | solution.py:70
  16.5 4.3 %reshape.39 = bf16[512,20,112]{2,1,0:T(8,128)(2,1)} reshape(bf16[2,4,64,2240]{3,2,1,0:T(8,128)(2,1)S(1)} %copy-done) | data formatting | bytes 4587520 | tf_op jit(solution)/shard_map/reshape | solution.py:68
  20.7 5.1 %fusion.9 = f32[20,112,112]{2,1,0:T(8,128)} fusion(bf16[512,20,112]{2,1,0:T(8,128)(2,1)} %reshape.39, bf16[512,20,112]{2,1,0:T(8,128)(2,1)} %max.13), kind=kOutput, calls=%fused_computation.17 | convolution fusion | flops 256901120 | bytes 5591040 | tf_op jit(solution)/shard_map/thd,the->hde/dot_general | solution.py:69
  26.6 22.9 %all-gather.1 = bf16[16,140,140]{2,1,0:T(8,128)(2,1)S(1)} all-gather(bf16[1,140,140]{2,1,0:T(8,128)(2,1)} %bitcast.29), channel_id=1, replica_groups=mesh['tm'=16,'space'=16] {'tm'}, dimensions={0}, use_global_device_ids=true | all-gather | bytes 666400 | tf_op jit(solution)/shard_map/all_gather | solution.py:92
  50.7 2.3 copy.30
  53.1 87.8 %all-reduce.3.cloned.1.call-done = f32[20,112,112]{2,1,0:T(8,128)} async-done(((f32[20,112,112]{2,1,0:T(8,128)}), f32[20,112,112]{2,1,0:T(8,128)}) %all-reduce.3.cloned.1.call-update) | async-done | bytes 1003536 | tf_op jit(solution)/shard_map/psum | solution.py:72
  141.0 2.2 collective-permute-start
  144.8 1.6 broadcast_maximum_fusion
  148.5 5.9 %add_convert_fusion.1 = bf16[2,4,64,2240]{3,2,1,0:T(8,128)(2,1)} fusion(bf16[2,4,64,2240]{3,2,1,0:T(8,128)(2,1)S(1)} %copy-done, bf16[2,6,66,2240]{3,2,1,0:T(8,128)(2,1)S(1)} %fusion.6, bf16[2,1,64,2240]{3,2,1,0:T(8,128)(2,1)S(1)} %collective-permute-done.1, bf16[2,1,64,2240]{3,2,1,0:T(8,128)(2,1)S(1)} %collective-permute-done, ...), kind=kLoop, calls=%fused_computation.5 | loop fusion | flops 33259520 | bytes 19577600 | tf_op jit(solution)/shard_map/convert_element_type | solution.py:58
  155.7 6.6 %max.15 = bf16[512,20,112]{2,1,0:T(8,128)(2,1)} reshape(bf16[2,4,64,2240]{3,2,1,0:T(8,128)(2,1)} %broadcast_maximum_fusion) | data formatting | bytes 4587520 | tf_op jit(solution)/shard_map/max | solution.py:76
  162.3 47.6 %all-gather.8.cloned.1.call-done = bf16[16,140,2240]{2,1,0:T(8,128)(2,1)} async-done(((bf16[1,140,2240]{2,1,0:T(8,128)(2,1)}), bf16[16,140,2240]{2,1,0:T(8,128)(2,1)}) %all-gather.8.cloned.1.call-update) | async-done | bytes 10035216 | tf_op jit(solution)/shard_map/all_gather | solution.py:95
  209.9 11.9 %reshape.47 = bf16[2240,2240]{1,0:T(8,128)(2,1)} reshape(bf16[16,140,2240]{2,1,0:T(8,128)(2,1)} %all-gather.8.cloned.1.call-done) | data formatting | bytes 20070400
  221.8 111.6 %all-gather.6.cloned.1.call-done = f32[320,112,112]{2,1,0:T(8,128)} async-done(((f32[20,112,112]{2,1,0:T(8,128)}), f32[320,112,112]{2,1,0:T(8,128)}) %all-gather.6.cloned.1.call-update) | async-done | bytes 16056336 | tf_op jit(solution)/shard_map/all_gather | solution.py:15
  333.4 23.2 %while.10 = (s32[]{:T(128)}, f32[20,112,112]{2,1,0:T(8,128)S(1)}, s32[]{:T(128)}, f32[16,20,112,112]{3,2,1,0:T(8,128)}, s32[]{:T(128)}, /*index=5*/s32[]{:T(128)}, s32[]{:T(128)}) while((s32[]{:T(128)}, f32[20,112,112]{2,1,0:T(8,128)S(1)}, s32[]{:T(128)}, f32[16,20,112,112]{3,2,1,0:T(8,128)}, s32[]{:T(128)}, /*index=5*/s32[]{:T(128)}, ...), condition=%wide.region_2.3_spmd, body=%wide.region_1.2_spmd.sunk | while | flops 250885 | bytes 3010675 | solution.py:21
  333.4 1.6 bitcast_add_fusion.2
  335.0 1.5 bitcast_add_fusion.2
  356.6 2.9 fusion.4
  359.6 2.8 bitcast_multiply_fusion
  362.4 6.2 %copy.25 = f32[512,20,112]{2,1,0:T(8,128)} copy(f32[512,20,112]{0,2,1:T(8,128)} %bitcast_multiply_fusion) | data formatting | bytes 9175040 | tf_op jit(solution)/shard_map/mul | solution.py:79
  368.6 7.3 %reshape.40 = f32[2,4,64,2240]{3,2,1,0:T(8,128)} reshape(f32[512,20,112]{2,1,0:T(8,128)} %copy.25) | data formatting | bytes 9175040 | tf_op jit(solution)/shard_map/reshape | solution.py:79
  375.9 5.4 %add_convert_fusion = bf16[2,4,64,2240]{3,2,1,0:T(8,128)(2,1)S(1)} fusion(bf16[2,4,64,2240]{3,2,1,0:T(8,128)(2,1)} %collective-permute-done.2, bf16[2,4,64,2240]{3,2,1,0:T(8,128)(2,1)} %add_convert_fusion.1, f32[2,4,64,2240]{3,2,1,0:T(8,128)} %reshape.40, f32[2240]{0:T(1024)S(1)} %get-tuple-element.39, f32[2240]{0:T(1024)S(1)} %get-tuple-element.40, ...), kind=kLoop, calls=%fused_computation.4 | loop fusion | flops 13762560 | bytes 11504640 | tf_op jit(solution)/shard_map/convert_element_type | solution.py:91
  381.3 13.4 %convolution_convert_fusion = bf16[512,2240]{0,1:T(8,128)(2,1)} fusion(bf16[512,2240]{1,0:T(8,128)(2,1)S(1)} %bitcast.27, bf16[2240,2240]{1,0:T(8,128)(2,1)} %reshape.47), kind=kOutput, calls=%fused_computation.12 | convolution fusion | flops 5139169280 | bytes 14622720 | tf_op jit(solution)/shard_map/dot_general | solution.py:93
  394.7 4.2 %copy.28 = bf16[512,2240]{1,0:T(8,128)(2,1)} copy(bf16[512,2240]{0,1:T(8,128)(2,1)} %convolution_convert_fusion) | data formatting | bytes 4587520 | tf_op jit(solution)/shard_map/convert_element_type | solution.py:98
  (46 shorter events, 26.7 us)
Async XLA Ops:
  6.5 9.9 %copy-start = (bf16[2,4,64,2240]{3,2,1,0:T(8,128)(2,1)S(1)}, bf16[2,4,64,2240]{3,2,1,0:T(8,128)(2,1)}, u32[]{:S(2)}) copy-start(bf16[2,4,64,2240]{3,2,1,0:T(8,128)(2,1)} %param.11) | copy-start | bytes 6881284
  6.5 134.3 %all-reduce.3.cloned.1.call-start = ((), (), s32[]{:S(2)}) async-start(), calls=%async_computation | async-start | bytes 2293760 | tf_op jit(solution)/shard_map/psum | solution.py:72
  20.7 5.1 %copy-start.3 = (bf16[140,140]{1,0:T(8,128)(2,1)S(1)}, bf16[140,140]{1,0:T(8,128)(2,1)}, u32[]{:S(2)}) copy-start(bf16[140,140]{1,0:T(8,128)(2,1)} %param.15) | copy-start | bytes 117604
  25.8 184.0 %all-gather.8.cloned.1.call-start = ((), (), s32[]{:S(2)}) async-start(), calls=%async_computation.2 | async-start | bytes 11280384 | tf_op jit(solution)/shard_map/all_gather | solution.py:95
  50.7 93.8 %copy-start.4 = (f32[9,2240]{1,0:T(8,128)S(1)}, f32[9,2240]{1,0:T(8,128)}, u32[]{:S(2)}) copy-start(f32[9,2240]{1,0:T(8,128)} %param.13) | copy-start | bytes 241924
  53.0 280.3 %all-gather.6.cloned.1.call-start = ((), (), s32[]{:S(2)}) async-start(), calls=%async_computation.1 | async-start | bytes 19496960 | tf_op jit(solution)/shard_map/all_gather | solution.py:15
  140.9 3.9 copy-start.2
  141.0 5.4 %collective-permute-start = (bf16[2,1,64,2240]{3,2,1,0:T(8,128)(2,1)S(1)}, bf16[2,1,64,2240]{3,2,1,0:T(8,128)(2,1)S(1)}, u32[]{:S(2)}, u32[]{:S(2)}) collective-permute-start(bf16[2,1,64,2240]{3,2,1,0:T(8,128)(2,1)S(1)} %get-tuple-element.49), channel_id=1, source_target_pairs={{0,1},{1,2},{2,3},{3,4},{4,5},{5,6},{6,7},{7,8},{8,9},{9,10},{10,1... | collective-permute-start | bytes 1720328 | tf_op jit(solution)/shard_map/ppermute | solution.py:29
  143.3 3.9 collective-permute-start.1
  148.4 7.2 %copy-start.5 = (f32[3,2240]{1,0:T(4,128)S(1)}, f32[3,2240]{1,0:T(4,128)}, u32[]{:S(2)}) copy-start(f32[3,2240]{1,0:T(4,128)} %param.14) | copy-start | bytes 80644
  154.3 221.6 %collective-permute-start.2 = (bf16[2,4,64,2240]{3,2,1,0:T(8,128)(2,1)}, bf16[2,4,64,2240]{3,2,1,0:T(8,128)(2,1)}, u32[]{:S(2)}, u32[]{:S(2)}) collective-permute-start(bf16[2,4,64,2240]{3,2,1,0:T(8,128)(2,1)} %add_convert_fusion.1), channel_id=1, source_target_pairs={{0,16},{16,32},{32,48},{48,64},{64,80},{80,96},{96,112},{112,128},... | collective-permute-start | bytes 6881288 | tf_op jit(solution)/shard_map/ppermute | solution.py:40
  333.4 23.2 %copy-start.1 = (f32[20,112,112]{2,1,0:T(8,128)S(1)}, f32[20,112,112]{2,1,0:T(8,128)}, u32[]{:S(2)}) copy-start(f32[20,112,112]{2,1,0:T(8,128)} %all-reduce.3.cloned.1.call-done) | copy-start | bytes 3010564
  368.6 7.3 %copy-start.6 = (f32[2240]{0:T(1024)S(1)}, f32[2240]{0:T(1024)}, u32[]{:S(2)}) copy-start(f32[2240]{0:T(1024)} %param.12) | copy-start | bytes 26884
Sparse Core Ops, SparseCore 0:
  25.9 114.9 all-reduce.2
  142.7 67.0 all-gather.7
  212.3 120.9 all-gather.5
where the time goes:
time: 407 us; the launch traced here: 405 us
  waiting for transfers between devices  248 us (61%)
  local copies, waits for them, and re-layouts  51.7 us (13%)
  other arithmetic  42.9 us (11%)
  blocking collectives  22.9 us (6%)
  matrix products  21.4 us (5%)
  between operations  13.3 us (3%)
  starting transfers between devices  4.89 us (1%)
    all_gather x1, waiting for transfers between devices, entering(): gathered = lax.all_gather(part, axis)  112 us
    psum x1, waiting for transfers between devices, per_device(): summed = lax.psum(local_state, 'space')  87.8 us
    all_gather x1, waiting for transfers between devices, per_device(): lax.all_gather(weight_band, 'space', axis=0, tiled=True)  47.6 us
    all_gather x1, blocking collectives, per_device(): weight_band = lax.all_gather(out_weight, 'tm', axis=1, tiled=True)  22.9 us
    add x15, other arithmetic, add_states(): return earlier + latter  22.6 us
    unnamed x18, local copies, waits for them, and re-layouts  16.2 us
    dot_general x1, matrix products, per_device(): jnp.dot(mixed, lax.all_gather(weight_band, 'space', axis=0, tiled=True),...  13.4 us
  transfers between devices with their start and end apart: 6, of which 4 were waited for; matrix products, arithmetic and copies ran while one was open for 18% of the time, Pallas kernels for 0%

commit v1 on v0

--- a/solution.py
+++ b/solution.py
@@ -8,17 +8,6 @@
 
 
 epsilon = 1e-06
-
-
-def entering(part, axis, combine, identity):
-    place = lax.axis_index(axis)
-    gathered = lax.all_gather(part, axis)
-    state = jnp.zeros_like(part) + jnp.asarray(identity, part.dtype)
-
-    def one(hop, state):
-        return combine(state, lax.dynamic_index_in_dim(gathered, hop, 0, False))
-
-    return lax.fori_loop(0, place, one, state)
 
 
 def extended(block, sides, width):
@@ -40,8 +29,18 @@
     return lax.ppermute(block, axis, route)
 
 
-def add_states(earlier, latter):
-    return earlier + latter
+def prefix_state(local_state):
+    axes = ("tm", "space")
+    blocks, bands = lax.axis_size("tm"), lax.axis_size("space")
+    devices = blocks * bands
+    flat = local_state.reshape(devices, -1)
+    chunk = flat.shape[1]
+    mine = lax.all_to_all(flat, axes, 0, 0, tiled=True)
+    block_sums = mine.reshape(blocks, bands, chunk).sum(axis=1)
+    prefixes = jnp.cumsum(block_sums, axis=0).astype(jnp.bfloat16)
+    outgoing = jnp.broadcast_to(prefixes[:, None, :], (blocks, bands, chunk)).reshape(devices, chunk)
+    gathered = lax.all_to_all(outgoing, axes, 0, 0, tiled=True)
+    return gathered.reshape(local_state.shape)
 
 
 def spatial_conv(padded, spatial_kernel):
@@ -62,6 +61,8 @@
     query_heads, key_heads, value_heads, head_gain, spatial_kernel, temporal_kernel, out_weight
 ):
     frame_count, row_count, col_count, model_width = query_heads.shape
+    weight_band = lax.all_gather(out_weight, "tm", axis=1, tiled=True)
+    weight_stack = lax.all_gather(weight_band, "space", axis=0)
     token_count = frame_count * row_count * col_count
     queries = query_heads.reshape(token_count, HEADS, HEAD_DIM)
     key_rows = key_heads.reshape(token_count, HEADS, HEAD_DIM)
@@ -69,9 +70,7 @@
     local_state = jnp.einsum(
         "thd,the->hde", jnp.maximum(key_rows, 0), value_rows, preferred_element_type=jnp.float32
     )
-    summed = lax.psum(local_state, "space")
-    earlier = entering(summed, "tm", add_states, jnp.zeros_like(summed))
-    state_low = (earlier + summed).astype(jnp.bfloat16)
+    state_low = prefix_state(local_state)
     attended = jnp.einsum(
         "thd,hde->the", jnp.maximum(queries, 0), state_low, preferred_element_type=jnp.float32
     )
@@ -89,10 +88,11 @@
             2 - back_step : 2 - back_step + frame_count
         ].astype(jnp.float32)
     mixed = (normed + temporal).astype(jnp.bfloat16).reshape(token_count, model_width)
-    weight_band = lax.all_gather(out_weight, "tm", axis=1, tiled=True)
-    projected = jnp.dot(
-        mixed,
-        lax.all_gather(weight_band, "space", axis=0, tiled=True),
+    space_count = lax.axis_size("space")
+    projected = jnp.einsum(
+        "tsk,skc->tc",
+        mixed.reshape(token_count, space_count, model_width // space_count),
+        weight_stack,
         preferred_element_type=jnp.float32,
     )
     return projected.astype(jnp.bfloat16).reshape(frame_count, row_count, col_count, model_width)

time: 407 us -> 238 us (0.58)
  the two profiles are of different devices: /device:TPU:30 before, /device:TPU:1 now
where the time goes in v1:
time: 238 us; the launch traced here: 237 us
  local copies, waits for them, and re-layouts  66.5 us (28%)
  waiting for transfers between devices  48.2 us (20%)
  starting transfers between devices  35.7 us (15%)
  other arithmetic  30.2 us (13%)
  blocking collectives  21.5 us (9%)
  matrix products  21.1 us (9%)
  between operations  13.6 us (6%)
    all_to_all x1, waiting for transfers between devices, prefix_state(): mine = lax.all_to_all(flat, axes, 0, 0, tiled=True)  28.4 us
    all_gather x1, blocking collectives, per_device(): weight_band = lax.all_gather(out_weight, 'tm', axis=1, tiled=True)  21.5 us
    all_to_all x1, waiting for transfers between devices, prefix_state(): gathered = lax.all_to_all(outgoing, axes, 0, 0, tiled=True)  19.7 us
    dot_general x1, matrix products, per_device(): jnp.einsum('tsk,skc->tc', mixed.reshape(token_count, space_count, model_w...  14.9 us
    all_to_all x1, starting transfers between devices, prefix_state(): mine = lax.all_to_all(flat, axes, 0, 0, tiled=True)  13.3 us
    another operation x1, local copies, waits for them, and re-layouts, per_device(): mixed.reshape(token_count, space_count, model_width // space_count)  12.7 us
    unnamed x12, local copies, waits for them, and re-layouts  11.5 us
    ppermute x1, starting transfers between devices, extended(): lax.ppermute(lax.slice_in_dim(block, block.shape[dim] - width, None, axis...  8.79 us
  transfers between devices with their start and end apart: 6, of which 2 were waited for; matrix products, arithmetic and copies ran while one was open for 39% of the time, Pallas kernels for 0%

profile of v1, /device:TPU:1, one launch (start us, length us, event | category | flops | bytes accessed | tf_op | source)
XLA Modules:
  0.0 236.7 jit_solution(13361809974933311926)
XLA Ops:
  8.3 21.5 %all-gather.1 = bf16[16,140,140]{2,1,0:T(8,128)(2,1)S(1)} all-gather(bf16[1,140,140]{2,1,0:T(8,128)(2,1)} %bitcast.31), channel_id=1, replica_groups=mesh['tm'=16,'space'=16] {'tm'}, dimensions={0}, use_global_device_ids=true | all-gather | bytes 666400 | tf_op jit(solution)/shard_map/all_gather | solution.py:64
  34.4 8.8 %collective-permute-start = (bf16[2,1,64,2240]{3,2,1,0:T(8,128)(2,1)}, bf16[2,1,64,2240]{3,2,1,0:T(8,128)(2,1)}, u32[]{:S(2)}, u32[]{:S(2)}) collective-permute-start(bf16[2,1,64,2240]{3,2,1,0:T(8,128)(2,1)} %get-tuple-element.17), channel_id=1, source_target_pairs={{0,1},{1,2},{2,3},{3,4},{4,5},{5,6},{6,7},{7,8},{8,9},{9,10},{10,1... | collective-permute-start | bytes 1720328 | tf_op jit(solution)/shard_map/ppermute | solution.py:18
  45.2 3.2 %broadcast_maximum_fusion.1 = bf16[2,4,64,2240]{3,2,1,0:T(8,128)(2,1)} fusion(bf16[2,4,64,2240]{3,2,1,0:T(8,128)(2,1)} %param.8), kind=kLoop, calls=%fused_computation.25 | loop fusion | flops 1146880 | bytes 4587520 | tf_op jit(solution)/shard_map/max | solution.py:71
  48.4 4.3 %reshape.59 = bf16[512,20,112]{2,1,0:T(8,128)(2,1)} reshape(bf16[2,4,64,2240]{3,2,1,0:T(8,128)(2,1)S(1)} %copy-done) | data formatting | bytes 4587520 | tf_op jit(solution)/shard_map/reshape | solution.py:69
  52.7 6.5 %max.13 = bf16[512,20,112]{2,1,0:T(8,128)(2,1)} reshape(bf16[2,4,64,2240]{3,2,1,0:T(8,128)(2,1)} %broadcast_maximum_fusion.1) | data formatting | bytes 4587520 | tf_op jit(solution)/shard_map/max | solution.py:71
  59.2 4.1 %fusion.11 = f32[20,112,112]{2,1,0:T(8,128)S(1)} fusion(bf16[512,20,112]{2,1,0:T(8,128)(2,1)} %reshape.59, bf16[512,20,112]{2,1,0:T(8,128)(2,1)} %max.13), kind=kOutput, calls=%fused_computation.18 | convolution fusion | flops 256901120 | bytes 5591040 | tf_op jit(solution)/shard_map/thd,the->hde/dot_general | solution.py:70
  63.4 3.6 %all_to_all.16 = f32[256,1,980]{2,1,0:T(1,128)} reshape(f32[20,112,112]{2,1,0:T(8,128)S(1)} %fusion.11) | data formatting | bytes 2007040 | tf_op jit(solution)/shard_map/all_to_all | solution.py:38
  67.0 13.3 %all-to-all-start = ((f32[256,1,980]{2,1,0:T(1,128)}), f32[256,1,980]{2,1,0:T(1,128)S(1)}, u32[]{:S(2)}, u32[]{:S(2)}) async-start(f32[256,1,980]{2,1,0:T(1,128)} %all_to_all.16), calls=%async_computation | async-start | bytes 2097152 | tf_op jit(solution)/shard_map/all_to_all | solution.py:38
  84.5 6.8 %add_convert_fusion.1 = bf16[2,4,64,2240]{3,2,1,0:T(8,128)(2,1)} fusion(bf16[2,4,64,2240]{3,2,1,0:T(8,128)(2,1)S(1)} %copy-done, bf16[2,6,66,2240]{3,2,1,0:T(8,128)(2,1)S(1)} %fusion.8, bf16[2,1,64,2240]{3,2,1,0:T(8,128)(2,1)} %collective-permute-done.1, bf16[2,1,64,2240]{3,2,1,0:T(8,128)(2,1)} %collective-permute-done, f32[2240]{0:T(1024)S(1)} %get-tuple-element.12, ...), kind=kLoop, calls=%fused_computation.5 | loop fusion | flops 33259520 | bytes 19577600 | tf_op jit(solution)/shard_map/convert_element_type | solution.py:57
  91.3 4.7 %collective-permute-start.2 = (bf16[2,4,64,2240]{3,2,1,0:T(8,128)(2,1)}, bf16[2,4,64,2240]{3,2,1,0:T(8,128)(2,1)}, u32[]{:S(2)}, u32[]{:S(2)}) collective-permute-start(bf16[2,4,64,2240]{3,2,1,0:T(8,128)(2,1)} %add_convert_fusion.1), channel_id=1, source_target_pairs={{0,16},{16,32},{32,48},{48,64},{64,80},{80,96},{96,112},{112,128},... | collective-permute-start | bytes 6881288 | tf_op jit(solution)/shard_map/ppermute | solution.py:29
  96.0 28.4 %all-to-all-done = f32[256,1,980]{2,1,0:T(1,128)S(1)} async-done(((f32[256,1,980]{2,1,0:T(1,128)}), f32[256,1,980]{2,1,0:T(1,128)S(1)}, u32[]{:S(2)}, u32[]{:S(2)}) %all-to-all-start) | async-done | bytes 1003552 | tf_op jit(solution)/shard_map/all_to_all | solution.py:38
  127.8 7.0 %all-to-all-start.1 = ((bf16[256,2,490]{2,1,0:T(2,128)(2,1)}), bf16[256,2,490]{2,1,0:T(2,128)(2,1)}, u32[]{:S(2)}, u32[]{:S(2)}) async-start(bf16[256,2,490]{2,1,0:T(2,128)(2,1)} %reshape.85), calls=%async_computation.1 | async-start | bytes 1048576 | tf_op jit(solution)/shard_map/all_to_all | solution.py:42
  134.9 3.2 %broadcast_maximum_fusion = bf16[2,4,64,2240]{3,2,1,0:T(8,128)(2,1)} fusion(bf16[2,4,64,2240]{3,2,1,0:T(8,128)(2,1)} %param.7), kind=kLoop, calls=%fused_computation.24 | loop fusion | flops 1146880 | bytes 4587520 | tf_op jit(solution)/shard_map/max | solution.py:75
  138.1 5.2 %max.15 = bf16[512,20,112]{2,1,0:T(8,128)(2,1)S(1)} reshape(bf16[2,4,64,2240]{3,2,1,0:T(8,128)(2,1)} %broadcast_maximum_fusion) | data formatting | bytes 4587520 | tf_op jit(solution)/shard_map/max | solution.py:75
  143.4 19.7 %all-to-all-done.1 = bf16[256,2,490]{2,1,0:T(2,128)(2,1)} async-done(((bf16[256,2,490]{2,1,0:T(2,128)(2,1)}), bf16[256,2,490]{2,1,0:T(2,128)(2,1)}, u32[]{:S(2)}, u32[]{:S(2)}) %all-to-all-start.1) | async-done | bytes 501792 | tf_op jit(solution)/shard_map/all_to_all | solution.py:42
  163.2 4.8 %reshape.86 = bf16[256,1,980]{2,1,0:T(2,128)(2,1)} reshape(bf16[256,2,490]{2,1,0:T(2,128)(2,1)} %all-to-all-done.1) | data formatting | bytes 1003520
  167.9 5.0 %reduce = bf16[256,980]{1,0:T(8,128)(2,1)} reduce(bf16[256,1,980]{2,1,0:T(2,128)(2,1)} %reshape.86, bf16[]{:T(256)} %constant.20), dimensions={1}, to_apply=%all_to_all.15.reduce_sub_computation | reduce | bytes 1003522 | tf_op jit(solution)/shard_map/all_to_all | solution.py:42
  173.0 3.0 %reshape.61 = bf16[20,112,112]{2,1,0:T(8,128)(2,1)} reshape(bf16[256,980]{1,0:T(8,128)(2,1)} %reduce) | data formatting | bytes 1003520 | tf_op jit(solution)/shard_map/reshape | solution.py:43
  178.1 2.8 %bitcast_multiply_fusion = f32[512,20,112]{0,2,1:T(8,128)} fusion(f32[20,112,512]{2,1,0:T(8,128)S(1)} %get-tuple-element.20, f32[512,20]{0,1:T(8,128)S(1)} %add_rsqrt_fusion), kind=kLoop, calls=%fused_computation.9 | loop fusion | flops 1146880 | bytes 9216000 | tf_op jit(solution)/shard_map/mul | solution.py:78
  180.9 6.2 %copy.39 = f32[512,20,112]{2,1,0:T(8,128)} copy(f32[512,20,112]{0,2,1:T(8,128)} %bitcast_multiply_fusion) | data formatting | bytes 9175040 | tf_op jit(solution)/shard_map/mul | solution.py:78
  187.1 7.3 %reshape.62 = f32[2,4,64,2240]{3,2,1,0:T(8,128)} reshape(f32[512,20,112]{2,1,0:T(8,128)} %copy.39) | data formatting | bytes 9175040 | tf_op jit(solution)/shard_map/reshape | solution.py:78
  194.4 5.4 %add_convert_fusion = bf16[2,4,64,2240]{3,2,1,0:T(8,128)(2,1)S(1)} fusion(bf16[2,4,64,2240]{3,2,1,0:T(8,128)(2,1)} %collective-permute-done.2, bf16[2,4,64,2240]{3,2,1,0:T(8,128)(2,1)} %add_convert_fusion.1, f32[2,4,64,2240]{3,2,1,0:T(8,128)} %reshape.62, f32[2240]{0:T(1024)S(1)} %get-tuple-element.15, f32[2240]{0:T(1024)S(1)} %get-tuple-element.16, ...), kind=kLoop, calls=%fused_computation.4 | loop fusion | flops 13762560 | bytes 11504640 | tf_op jit(solution)/shard_map/convert_element_type | solution.py:90
  199.8 12.7 %reshape_reshape.3 = bf16[512,16,140]{2,1,0:T(8,128)(2,1)} reshape(bf16[2,4,64,2240]{3,2,1,0:T(8,128)(2,1)S(1)} %add_convert_fusion) | data formatting | bytes 4587520 | tf_op jit(solution)/shard_map/reshape;reshape | solution.py:94
  212.6 14.9 %fusion.5 = bf16[512,2240]{0,1:T(8,128)(2,1)S(1)} fusion(bf16[16,140,2240]{2,1,0:T(8,128)(2,1)} %all-gather.5.cloned.1.call-done, bf16[512,16,140]{2,1,0:T(8,128)(2,1)} %reshape_reshape.3), kind=kOutput, calls=%fused_computation.12 | convolution fusion | flops 5139169280 | bytes 14622720 | tf_op jit(solution)/shard_map/tsk,skc->tc/dot_general | solution.py:92
  (30 shorter events, 20.4 us)
Async XLA Ops:
  6.5 26.8 %copy-start = (bf16[2,4,64,2240]{3,2,1,0:T(8,128)(2,1)S(1)}, bf16[2,4,64,2240]{3,2,1,0:T(8,128)(2,1)}, u32[]{:S(2)}) copy-start(bf16[2,4,64,2240]{3,2,1,0:T(8,128)(2,1)} %param.9) | copy-start | bytes 6881284
  6.5 206.0 %all-gather.5.cloned.1.call-start = ((), (), s32[]{:S(2)}) async-start(), calls=%async_computation.2 | async-start | bytes 11280384 | tf_op jit(solution)/shard_map/all_gather | solution.py:65
  34.4 47.6 %collective-permute-start = (bf16[2,1,64,2240]{3,2,1,0:T(8,128)(2,1)}, bf16[2,1,64,2240]{3,2,1,0:T(8,128)(2,1)}, u32[]{:S(2)}, u32[]{:S(2)}) collective-permute-start(bf16[2,1,64,2240]{3,2,1,0:T(8,128)(2,1)} %get-tuple-element.17), channel_id=1, source_target_pairs={{0,1},{1,2},{2,3},{3,4},{4,5},{5,6},{6,7},{7,8},{8,9},{9,10},{10,1... | collective-permute-start | bytes 1720328 | tf_op jit(solution)/shard_map/ppermute | solution.py:18
  43.2 38.8 %collective-permute-start.1 = (bf16[2,1,64,2240]{3,2,1,0:T(8,128)(2,1)}, bf16[2,1,64,2240]{3,2,1,0:T(8,128)(2,1)}, u32[]{:S(2)}, u32[]{:S(2)}) collective-permute-start(bf16[2,1,64,2240]{3,2,1,0:T(8,128)(2,1)} %get-tuple-element.18), channel_id=1, source_target_pairs={{1,0},{2,1},{3,2},{4,3},{5,4},{6,5},{7,6},{8,7},{9,8},{10,9},{11,1... | collective-permute-start | bytes 1720328 | tf_op jit(solution)/shard_map/ppermute | solution.py:21
  67.0 57.4 %all-to-all-start = ((f32[256,1,980]{2,1,0:T(1,128)}), f32[256,1,980]{2,1,0:T(1,128)S(1)}, u32[]{:S(2)}, u32[]{:S(2)}) async-start(f32[256,1,980]{2,1,0:T(1,128)} %all_to_all.16), calls=%async_computation | async-start | bytes 2097152 | tf_op jit(solution)/shard_map/all_to_all | solution.py:38
  91.3 103.1 %collective-permute-start.2 = (bf16[2,4,64,2240]{3,2,1,0:T(8,128)(2,1)}, bf16[2,4,64,2240]{3,2,1,0:T(8,128)(2,1)}, u32[]{:S(2)}, u32[]{:S(2)}) collective-permute-start(bf16[2,4,64,2240]{3,2,1,0:T(8,128)(2,1)} %add_convert_fusion.1), channel_id=1, source_target_pairs={{0,16},{16,32},{32,48},{48,64},{64,80},{80,96},{96,112},{112,128},... | collective-permute-start | bytes 6881288 | tf_op jit(solution)/shard_map/ppermute | solution.py:29
  127.8 35.3 %all-to-all-start.1 = ((bf16[256,2,490]{2,1,0:T(2,128)(2,1)}), bf16[256,2,490]{2,1,0:T(2,128)(2,1)}, u32[]{:S(2)}, u32[]{:S(2)}) async-start(bf16[256,2,490]{2,1,0:T(2,128)(2,1)} %reshape.85), calls=%async_computation.1 | async-start | bytes 1048576 | tf_op jit(solution)/shard_map/all_to_all | solution.py:42
  134.8 8.5 %copy-start.1 = (f32[3,2240]{1,0:T(4,128)S(1)}, f32[3,2240]{1,0:T(4,128)}, u32[]{:S(2)}) copy-start(f32[3,2240]{1,0:T(4,128)} %param.12) | copy-start | bytes 80644
  187.1 7.3 %copy-start.2 = (f32[2240]{0:T(1024)S(1)}, f32[2240]{0:T(1024)}, u32[]{:S(2)}) copy-start(f32[2240]{0:T(1024)} %param.10) | copy-start | bytes 26884
Sparse Core Ops, SparseCore 0:
  33.5 95.4 all-gather.4

commit v2 on v1

--- a/solution.py
+++ b/solution.py
@@ -1,3 +1,5 @@
+import math
+
 import jax
 import jax.numpy as jnp
 from jax import lax
@@ -57,6 +59,43 @@
     return summed.astype(jnp.bfloat16)
 
 
+def banded_attention(queries, state_low):
+    heads, dim, _ = state_low.shape
+    group = math.lcm(dim, 128) // dim
+    pieces = []
+    for first in range(0, heads, group):
+        count = min(group, heads - first)
+        blocks = state_low[first : first + count]
+        eye = jnp.eye(count, dtype=bool)
+        diagonal = jnp.where(
+            eye[:, None, :, None], blocks[:, :, None, :], jnp.zeros((), blocks.dtype)
+        ).reshape(count * dim, count * dim)
+        pieces.append(
+            jnp.dot(
+                queries[:, first * dim : (first + count) * dim],
+                diagonal,
+                preferred_element_type=jnp.float32,
+            )
+        )
+    return jnp.concatenate(pieces, axis=1)
+
+
+def split_dot(values, matrix):
+    high = values.astype(jnp.bfloat16)
+    low = (values - high.astype(jnp.float32)).astype(jnp.bfloat16)
+    return jnp.dot(high, matrix, preferred_element_type=jnp.float32) + jnp.dot(
+        low, matrix, preferred_element_type=jnp.float32
+    )
+
+
+def head_norm(attended):
+    width = attended.shape[1]
+    member = (jnp.arange(width)[:, None] // HEAD_DIM == jnp.arange(HEADS)[None, :]).astype(jnp.bfloat16)
+    mean_square = split_dot(attended * attended, member) / HEAD_DIM
+    scale = split_dot(lax.rsqrt(mean_square + epsilon), member.T)
+    return attended * scale
+
+
 def per_device(
     query_heads, key_heads, value_heads, head_gain, spatial_kernel, temporal_kernel, out_weight
 ):
@@ -71,13 +110,9 @@
         "thd,the->hde", jnp.maximum(key_rows, 0), value_rows, preferred_element_type=jnp.float32
     )
     state_low = prefix_state(local_state)
-    attended = jnp.einsum(
-        "thd,hde->the", jnp.maximum(queries, 0), state_low, preferred_element_type=jnp.float32
-    )
-    mean_square = jnp.mean(attended * attended, axis=-1, keepdims=True)
-    normed = (attended * lax.rsqrt(mean_square + epsilon)).reshape(
-        frame_count, row_count, col_count, model_width
-    ) * head_gain
+    flat_queries = jnp.maximum(query_heads.reshape(token_count, model_width), 0)
+    attended = banded_attention(flat_queries, state_low)
+    normed = head_norm(attended).reshape(frame_count, row_count, col_count, model_width) * head_gain
     padded = extended(value_heads, (("space", 1),), 1)
     spatial = spatial_conv(padded, spatial_kernel)
     earlier_frames = from_behind(spatial, "tm", 1)
@@ -88,12 +123,8 @@
             2 - back_step : 2 - back_step + frame_count
         ].astype(jnp.float32)
     mixed = (normed + temporal).astype(jnp.bfloat16).reshape(token_count, model_width)
-    space_count = lax.axis_size("space")
-    projected = jnp.einsum(
-        "tsk,skc->tc",
-        mixed.reshape(token_count, space_count, model_width // space_count),
-        weight_stack,
-        preferred_element_type=jnp.float32,
+    projected = jnp.dot(
+        mixed, weight_stack.reshape(model_width, model_width), preferred_element_type=jnp.float32
     )
     return projected.astype(jnp.bfloat16).reshape(frame_count, row_count, col_count, model_width)
 

time: 238 us -> 263 us (1.11); the launches traced: 237 us -> 259 us
  waiting for transfers between devices: 48.2 us -> 65.4 us
  local copies, waits for them, and re-layouts: 66.5 us -> 55.2 us
  starting transfers between devices: 35.7 us -> 41.8 us
  matrix products: 21.1 us -> 27 us
  other arithmetic: 30.2 us -> 34.6 us
    ppermute x1, waiting for transfers between devices: 0.01 us -> 40.6 us  [extended(): lax.ppermute(lax.slice_in_dim(block, block.shape[dim] - width, None, axis...]
    all_to_all x1, waiting for transfers between devices: 28.4 us -> 0.01 us  [prefix_state(): mine = lax.all_to_all(flat, axes, 0, 0, tiled=True)]
    ppermute x1, waiting for transfers between devices: 0.01 us -> 17.3 us  [from_behind(): return lax.ppermute(block, axis, route)]
    all_to_all x1, waiting for transfers between devices: 19.7 us -> 4.72 us  [prefix_state(): gathered = lax.all_to_all(outgoing, axes, 0, 0, tiled=True)]
    another operation x1 -> x0, local copies, waits for them, and re-layouts: 12.7 us -> none  [per_device(): mixed.reshape(token_count, space_count, model_width // space_count)]
    unnamed x12 -> x37, local copies, waits for them, and re-layouts: 11.5 us -> 23 us
    reshape x1 -> x0, local copies, waits for them, and re-layouts: 7.3 us -> none  [per_device(): (attended * lax.rsqrt(mean_square + epsilon)).reshape(frame_count, row_co...]
    all_to_all x1, starting transfers between devices: 6.99 us -> 13.9 us  [prefix_state(): gathered = lax.all_to_all(outgoing, axes, 0, 0, tiled=True)]
  transfers between devices with their start and end apart: 6 -> 6, of which waited for: 2 -> 4; matrix products, arithmetic and copies ran while one was open for 39% -> 31% of each run, Pallas kernels for 0% -> 0%
where the time goes in v2:
time: 263 us; the launch traced here: 259 us
  waiting for transfers between devices  65.4 us (25%)
  local copies, waits for them, and re-layouts  55.2 us (21%)
  starting transfers between devices  41.8 us (16%)
  other arithmetic  34.6 us (13%)
  matrix products  27 us (10%)
  blocking collectives  21.3 us (8%)
  between operations  13.7 us (5%)
    ppermute x1, waiting for transfers between devices, extended(): lax.ppermute(lax.slice_in_dim(block, block.shape[dim] - width, None, axis...  40.6 us
    unnamed x37, local copies, waits for them, and re-layouts  23 us
    all_gather x1, blocking collectives, per_device(): weight_band = lax.all_gather(out_weight, 'tm', axis=1, tiled=True)  21.3 us
    all_to_all x1, starting transfers between devices, prefix_state(): mine = lax.all_to_all(flat, axes, 0, 0, tiled=True)  17.5 us
    ppermute x1, waiting for transfers between devices, from_behind(): return lax.ppermute(block, axis, route)  17.3 us
    all_to_all x1, starting transfers between devices, prefix_state(): gathered = lax.all_to_all(outgoing, axes, 0, 0, tiled=True)  13.9 us
    dot_general x1, matrix products, per_device(): jnp.dot(mixed, weight_stack.reshape(model_width, model_width), preferred_...  13.4 us
    convert_element_type x1, other arithmetic, spatial_conv(): return summed.astype(jnp.bfloat16)  11.1 us
  transfers between devices with their start and end apart: 6, of which 4 were waited for; matrix products, arithmetic and copies ran while one was open for 31% of the time, Pallas kernels for 0%

profile of v2, /device:TPU:1, one launch (start us, length us, event | category | flops | bytes accessed | tf_op | source)
XLA Modules:
  0.0 259.0 jit_solution(15104171424416362181)
XLA Ops:
  7.5 21.3 %all-gather.1 = bf16[16,140,140]{2,1,0:T(8,128)(2,1)S(1)} all-gather(bf16[1,140,140]{2,1,0:T(8,128)(2,1)S(1)} %bitcast.33), channel_id=1, replica_groups=mesh['tm'=16,'space'=16] {'tm'}, dimensions={0}, use_global_device_ids=true | all-gather | bytes 666400 | tf_op jit(solution)/shard_map/all_gather | solution.py:103
  30.8 3.2 %broadcast_maximum_fusion = bf16[2,4,64,2240]{3,2,1,0:T(8,128)(2,1)} fusion(bf16[2,4,64,2240]{3,2,1,0:T(8,128)(2,1)} %param.8), kind=kLoop, calls=%fused_computation.26 | loop fusion | flops 1146880 | bytes 4587520 | tf_op jit(solution)/shard_map/max | solution.py:110
  34.0 6.7 %max.20 = bf16[512,20,112]{2,1,0:T(8,128)(2,1)} reshape(bf16[2,4,64,2240]{3,2,1,0:T(8,128)(2,1)} %broadcast_maximum_fusion) | data formatting | bytes 4587520 | tf_op jit(solution)/shard_map/max | solution.py:110
  40.7 4.3 %reshape.112 = bf16[512,20,112]{2,1,0:T(8,128)(2,1)} reshape(bf16[2,4,64,2240]{3,2,1,0:T(8,128)(2,1)S(1)} %copy-done) | data formatting | bytes 4587520 | tf_op jit(solution)/shard_map/reshape | solution.py:108
  45.0 4.0 %fusion.8 = f32[20,112,112]{2,1,0:T(8,128)S(1)} fusion(bf16[512,20,112]{2,1,0:T(8,128)(2,1)} %reshape.112, bf16[512,20,112]{2,1,0:T(8,128)(2,1)} %max.20), kind=kOutput, calls=%fused_computation.17 | convolution fusion | flops 256901120 | bytes 5591040 | tf_op jit(solution)/shard_map/thd,the->hde/dot_general | solution.py:109
  49.0 3.6 %all_to_all.16 = f32[256,1,980]{2,1,0:T(1,128)} reshape(f32[20,112,112]{2,1,0:T(8,128)S(1)} %fusion.8) | data formatting | bytes 2007040 | tf_op jit(solution)/shard_map/all_to_all | solution.py:40
  52.6 17.5 %all-to-all-start = ((f32[256,1,980]{2,1,0:T(1,128)}), f32[256,1,980]{2,1,0:T(1,128)S(1)}, u32[]{:S(2)}, u32[]{:S(2)}) async-start(f32[256,1,980]{2,1,0:T(1,128)} %all_to_all.16), calls=%async_computation | async-start | bytes 2097152 | tf_op jit(solution)/shard_map/all_to_all | solution.py:40
  70.2 3.8 %collective-permute-start = (bf16[2,1,64,2240]{3,2,1,0:T(8,128)(2,1)S(1)}, bf16[2,1,64,2240]{3,2,1,0:T(8,128)(2,1)S(1)}, u32[]{:S(2)}, u32[]{:S(2)}) collective-permute-start(bf16[2,1,64,2240]{3,2,1,0:T(8,128)(2,1)S(1)} %get-tuple-element.17), channel_id=1, source_target_pairs={{0,1},{1,2},{2,3},{3,4},{4,5},{5,6},{6,7},{7,8},{8,9},{9,10},{10,1... | collective-permute-start | bytes 1720328 | tf_op jit(solution)/shard_map/ppermute | solution.py:20
  81.1 40.6 %collective-permute-done = bf16[2,1,64,2240]{3,2,1,0:T(8,128)(2,1)S(1)} collective-permute-done((bf16[2,1,64,2240]{3,2,1,0:T(8,128)(2,1)S(1)}, bf16[2,1,64,2240]{3,2,1,0:T(8,128)(2,1)S(1)}, u32[]{:S(2)}, u32[]{:S(2)}) %collective-permute-start) | collective-permute-done | bytes 573472 | tf_op jit(solution)/shard_map/ppermute | solution.py:20
  121.7 2.6 %collective-permute-done.1 = bf16[2,1,64,2240]{3,2,1,0:T(8,128)(2,1)S(1)} collective-permute-done((bf16[2,1,64,2240]{3,2,1,0:T(8,128)(2,1)S(1)}, bf16[2,1,64,2240]{3,2,1,0:T(8,128)(2,1)S(1)}, u32[]{:S(2)}, u32[]{:S(2)}) %collective-permute-start.1) | collective-permute-done | bytes 573472 | tf_op jit(solution)/shard_map/ppermute | solution.py:23
  134.8 2.7 %reduce.25 = bf16[256,980]{1,0:T(8,128)(2,1)} reduce(bf16[256,1,980]{2,0,1:T(8,128)(2,1)} %bitcast.32, bf16[]{:T(256)} %broadcast.76), dimensions={1}, to_apply=%copy.33.reduce_sub_computation | reduce | bytes 1003522 | tf_op jit(solution)/shard_map/all_to_all | solution.py:44
  139.9 13.9 %all-to-all-start.1 = ((bf16[256,2,490]{2,1,0:T(2,128)(2,1)}), bf16[256,2,490]{2,1,0:T(2,128)(2,1)}, u32[]{:S(2)}, u32[]{:S(2)}) async-start(bf16[256,2,490]{2,1,0:T(2,128)(2,1)} %reshape.139), calls=%async_computation.1 | async-start | bytes 1048576 | tf_op jit(solution)/shard_map/all_to_all | solution.py:44
  153.8 11.1 %add_convert_fusion.1 = bf16[2,4,64,2240]{3,2,1,0:T(8,128)(2,1)} fusion(bf16[2,4,64,2240]{3,2,1,0:T(8,128)(2,1)S(1)} %copy-done, bf16[2,6,66,2240]{3,2,1,0:T(8,128)(2,1)} %fusion.6, bf16[2,1,64,2240]{3,2,1,0:T(8,128)(2,1)S(1)} %copy-done.5, bf16[2,1,64,2240]{3,2,1,0:T(8,128)(2,1)S(1)} %copy-done.3, f32[2240]{0:T(1024)} %get-tuple-element.12, ...), kind=kLoop, calls=%fused_computation.7 | loop fusion | flops 33259520 | bytes 19577600 | tf_op jit(solution)/shard_map/convert_element_type | solution.py:59
  164.9 4.7 %collective-permute-start.2 = (bf16[2,4,64,2240]{3,2,1,0:T(8,128)(2,1)}, bf16[2,4,64,2240]{3,2,1,0:T(8,128)(2,1)}, u32[]{:S(2)}, u32[]{:S(2)}) collective-permute-start(bf16[2,4,64,2240]{3,2,1,0:T(8,128)(2,1)} %add_convert_fusion.1), channel_id=1, source_target_pairs={{0,16},{16,32},{32,48},{48,64},{64,80},{80,96},{96,112},{112,128},... | collective-permute-start | bytes 6881288 | tf_op jit(solution)/shard_map/ppermute | solution.py:31
  169.5 4.7 %all-to-all-done.1 = bf16[256,2,490]{2,1,0:T(2,128)(2,1)} async-done(((bf16[256,2,490]{2,1,0:T(2,128)(2,1)}), bf16[256,2,490]{2,1,0:T(2,128)(2,1)}, u32[]{:S(2)}, u32[]{:S(2)}) %all-to-all-start.1) | async-done | bytes 501792 | tf_op jit(solution)/shard_map/all_to_all | solution.py:44
  174.3 4.0 %reshape.140 = bf16[256,1,980]{2,1,0:T(2,128)(2,1)S(1)} reshape(bf16[256,2,490]{2,1,0:T(2,128)(2,1)} %all-to-all-done.1) | data formatting | bytes 1003520
  178.2 3.2 %reduce = bf16[256,980]{1,0:T(8,128)(2,1)S(1)} reduce(bf16[256,1,980]{2,1,0:T(2,128)(2,1)S(1)} %reshape.140, bf16[]{:T(256)} %constant.33), dimensions={1}, to_apply=%all_to_all.15.reduce_sub_computation | reduce | bytes 1003522 | tf_op jit(solution)/shard_map/all_to_all | solution.py:44
  184.5 4.1 %select_n.40 = bf16[896,896]{1,0:T(8,128)(2,1)} reshape(bf16[8,112,8,112]{3,2,1,0:T(8,128)(2,1)} %get-tuple-element.21) | data formatting | bytes 3211264 | tf_op jit(solution)/shard_map/jit(_where)/select_n | solution.py:70
  193.2 2.7 %fusion.19 = f32[512,896]{1,0:T(8,128)S(1)} fusion(bf16[896,896]{1,0:T(8,128)(2,1)} %select_n.40, bf16[512,2240]{1,0:T(8,128)(2,1)S(1)} %bitcast.28), kind=kOutput, calls=%fused_computation.36 | convolution fusion | flops 822083584 | bytes 4358144 | tf_op jit(solution)/shard_map/dot_general | solution.py:74
  201.3 17.3 %collective-permute-done.2 = bf16[2,4,64,2240]{3,2,1,0:T(8,128)(2,1)} collective-permute-done((bf16[2,4,64,2240]{3,2,1,0:T(8,128)(2,1)}, bf16[2,4,64,2240]{3,2,1,0:T(8,128)(2,1)}, u32[]{:S(2)}, u32[]{:S(2)}) %collective-permute-start.2) | collective-permute-done | bytes 2293792 | tf_op jit(solution)/shard_map/ppermute | solution.py:31
  218.6 4.0 %add_convert_fusion = bf16[2,4,64,2240]{3,2,1,0:T(8,128)(2,1)S(1)} fusion(bf16[2,4,64,2240]{3,2,1,0:T(8,128)(2,1)} %collective-permute-done.2, bf16[2,4,64,2240]{3,2,1,0:T(8,128)(2,1)} %add_convert_fusion.1, f32[2,4,64,2240]{3,2,1,0:T(8,128)S(1)} %bitcast.25, f32[2240]{0:T(1024)S(1)} %copy-done.10, f32[2240]{0:T(1024)S(1)} %copy-done.11, ...), kind=kLoop, calls=%fused_computation.6 | loop fusion | flops 13762560 | bytes 11504640 | tf_op jit(solution)/shard_map/convert_element_type | solution.py:125
  222.7 11.9 %reshape.124 = bf16[2240,2240]{1,0:T(8,128)(2,1)} reshape(bf16[16,140,2240]{2,1,0:T(8,128)(2,1)} %all-gather.5.cloned.1.call-done) | data formatting | bytes 20070400
  234.6 13.4 %convolution_convert_fusion = bf16[512,2240]{0,1:T(8,128)(2,1)} fusion(bf16[512,2240]{1,0:T(8,128)(2,1)S(1)} %bitcast.31, bf16[2240,2240]{1,0:T(8,128)(2,1)} %reshape.124), kind=kOutput, calls=%fused_computation.12 | convolution fusion | flops 5139169280 | bytes 14622720 | tf_op jit(solution)/shard_map/dot_general | solution.py:126
  248.0 4.2 %copy.39 = bf16[512,2240]{1,0:T(8,128)(2,1)} copy(bf16[512,2240]{0,1:T(8,128)(2,1)} %convolution_convert_fusion) | data formatting | bytes 4587520 | tf_op jit(solution)/shard_map/convert_element_type | solution.py:129
  (66 shorter events, 35.6 us)
Async XLA Ops:
  6.5 216.2 %all-gather.5.cloned.1.call-start = ((), (), s32[]{:S(2)}) async-start(), calls=%async_computation.2 | async-start | bytes 11280384 | tf_op jit(solution)/shard_map/all_gather | solution.py:104
  34.0 6.7 %copy-start = (bf16[2,4,64,2240]{3,2,1,0:T(8,128)(2,1)S(1)}, bf16[2,4,64,2240]{3,2,1,0:T(8,128)(2,1)}, u32[]{:S(2)}) copy-start(bf16[2,4,64,2240]{3,2,1,0:T(8,128)(2,1)} %param.9) | copy-start | bytes 6881284
  52.6 23.4 %copy-start.12 = (f32[3,2240]{1,0:T(4,128)S(1)}, f32[3,2240]{1,0:T(4,128)}, u32[]{:S(2)}) copy-start(f32[3,2240]{1,0:T(4,128)} %param.12) | copy-start | bytes 80644
  52.6 75.2 %all-to-all-start = ((f32[256,1,980]{2,1,0:T(1,128)}), f32[256,1,980]{2,1,0:T(1,128)S(1)}, u32[]{:S(2)}, u32[]{:S(2)}) async-start(f32[256,1,980]{2,1,0:T(1,128)} %all_to_all.16), calls=%async_computation | async-start | bytes 2097152 | tf_op jit(solution)/shard_map/all_to_all | solution.py:40
  70.1 9.5 %copy-start.6 = (bf16[2,4,64,2240]{3,2,1,0:T(8,128)(2,1)S(1)}, bf16[2,4,64,2240]{3,2,1,0:T(8,128)(2,1)}, u32[]{:S(2)}) copy-start(bf16[2,4,64,2240]{3,2,1,0:T(8,128)(2,1)} %param.7) | copy-start | bytes 6881284
  70.2 51.5 %collective-permute-start = (bf16[2,1,64,2240]{3,2,1,0:T(8,128)(2,1)S(1)}, bf16[2,1,64,2240]{3,2,1,0:T(8,128)(2,1)S(1)}, u32[]{:S(2)}, u32[]{:S(2)}) collective-permute-start(bf16[2,1,64,2240]{3,2,1,0:T(8,128)(2,1)S(1)} %get-tuple-element.17), channel_id=1, source_target_pairs={{0,1},{1,2},{2,3},{3,4},{4,5},{5,6},{6,7},{7,8},{8,9},{9,10},{10,1... | collective-permute-start | bytes 1720328 | tf_op jit(solution)/shard_map/ppermute | solution.py:20
  74.0 50.3 %collective-permute-start.1 = (bf16[2,1,64,2240]{3,2,1,0:T(8,128)(2,1)S(1)}, bf16[2,1,64,2240]{3,2,1,0:T(8,128)(2,1)S(1)}, u32[]{:S(2)}, u32[]{:S(2)}) collective-permute-start(bf16[2,1,64,2240]{3,2,1,0:T(8,128)(2,1)S(1)} %get-tuple-element.18), channel_id=1, source_target_pairs={{1,0},{2,1},{3,2},{4,3},{5,4},{6,5},{7,6},{8,7},{9,8},{10,9},{11,1... | collective-permute-start | bytes 1720328 | tf_op jit(solution)/shard_map/ppermute | solution.py:23
  121.7 2.6 %copy-start.2 = (bf16[2,1,64,2240]{3,2,1,0:T(8,128)(2,1)}, bf16[2,1,64,2240]{3,2,1,0:T(8,128)(2,1)S(1)}, u32[]{:S(2)}) copy-start(bf16[2,1,64,2240]{3,2,1,0:T(8,128)(2,1)S(1)} %collective-permute-done) | copy-start | bytes 1720324
  124.4 0.8 copy-start.4
  129.0 24.8 %copy-start.3 = (bf16[2,1,64,2240]{3,2,1,0:T(8,128)(2,1)S(1)}, bf16[2,1,64,2240]{3,2,1,0:T(8,128)(2,1)}, u32[]{:S(2)}) copy-start(bf16[2,1,64,2240]{3,2,1,0:T(8,128)(2,1)} %copy-done.2) | copy-start | bytes 1720324
  129.0 24.8 %copy-start.5 = (bf16[2,1,64,2240]{3,2,1,0:T(8,128)(2,1)S(1)}, bf16[2,1,64,2240]{3,2,1,0:T(8,128)(2,1)}, u32[]{:S(2)}) copy-start(bf16[2,1,64,2240]{3,2,1,0:T(8,128)(2,1)} %copy-done.4) | copy-start | bytes 1720324
  139.9 34.4 %all-to-all-start.1 = ((bf16[256,2,490]{2,1,0:T(2,128)(2,1)}), bf16[256,2,490]{2,1,0:T(2,128)(2,1)}, u32[]{:S(2)}, u32[]{:S(2)}) async-start(bf16[256,2,490]{2,1,0:T(2,128)(2,1)} %reshape.139), calls=%async_computation.1 | async-start | bytes 1048576 | tf_op jit(solution)/shard_map/all_to_all | solution.py:44
  164.9 53.8 %collective-permute-start.2 = (bf16[2,4,64,2240]{3,2,1,0:T(8,128)(2,1)}, bf16[2,4,64,2240]{3,2,1,0:T(8,128)(2,1)}, u32[]{:S(2)}, u32[]{:S(2)}) collective-permute-start(bf16[2,4,64,2240]{3,2,1,0:T(8,128)(2,1)} %add_convert_fusion.1), channel_id=1, source_target_pairs={{0,16},{16,32},{32,48},{48,64},{64,80},{80,96},{96,112},{112,128},... | collective-permute-start | bytes 6881288 | tf_op jit(solution)/shard_map/ppermute | solution.py:31
  182.7 5.9 %copy-start.7 = (bf16[20,112,112]{2,1,0:T(8,128)(2,1)}, bf16[20,112,112]{2,1,0:T(8,128)(2,1)S(1)}, u32[]{:S(2)}) copy-start(bf16[20,112,112]{2,1,0:T(8,128)(2,1)S(1)} %reshape.114) | copy-start | bytes 1505284
  184.5 6.5 %copy-start.14 = (pred[4,4]{1,0:T(4,128)(4,1)S(1)}, pred[4,4]{1,0:T(4,128)(4,1)}, u32[]{:S(2)}) copy-start(pred[4,4]{1,0:T(4,128)(4,1)} %iota_compare_fusion.16) | copy-start | bytes 52
  188.6 2.4 slice-start
  191.0 2.2 copy-start.1
  193.2 2.8 %copy-start.8 = (bf16[896,896]{1,0:T(8,128)(2,1)S(1)}, bf16[896,896]{1,0:T(8,128)(2,1)}, u32[]{:S(2)}) copy-start(bf16[896,896]{1,0:T(8,128)(2,1)} %select_n.42) | copy-start | bytes 4816900
  200.2 18.4 %copy-start.9 = (f32[2240]{0:T(1024)S(1)}, f32[2240]{0:T(1024)}, u32[]{:S(2)}) copy-start(f32[2240]{0:T(1024)} %get-tuple-element.14) | copy-start | bytes 26884
  200.2 18.4 %copy-start.10 = (f32[2240]{0:T(1024)S(1)}, f32[2240]{0:T(1024)}, u32[]{:S(2)}) copy-start(f32[2240]{0:T(1024)} %get-tuple-element.15) | copy-start | bytes 26884
  200.2 18.4 %copy-start.11 = (f32[2240]{0:T(1024)S(1)}, f32[2240]{0:T(1024)}, u32[]{:S(2)}) copy-start(f32[2240]{0:T(1024)} %get-tuple-element.16) | copy-start | bytes 26884
  200.2 18.4 %copy-start.13 = (f32[2240]{0:T(1024)S(1)}, f32[2240]{0:T(1024)}, u32[]{:S(2)}) copy-start(f32[2240]{0:T(1024)} %param.10) | copy-start | bytes 26884
Sparse Core Ops, SparseCore 0:
  30.9 99.2 all-gather.4

commit v3 on v2

--- a/solution.py
+++ b/solution.py
@@ -31,18 +31,20 @@
     return lax.ppermute(block, axis, route)
 
 
-def prefix_state(local_state):
+def prefix_state(local_state, beside_out, beside_back):
     axes = ("tm", "space")
     blocks, bands = lax.axis_size("tm"), lax.axis_size("space")
     devices = blocks * bands
     flat = local_state.reshape(devices, -1)
     chunk = flat.shape[1]
     mine = lax.all_to_all(flat, axes, 0, 0, tiled=True)
+    mine, beside_out = lax.optimization_barrier((mine, beside_out))
     block_sums = mine.reshape(blocks, bands, chunk).sum(axis=1)
     prefixes = jnp.cumsum(block_sums, axis=0).astype(jnp.bfloat16)
     outgoing = jnp.broadcast_to(prefixes[:, None, :], (blocks, bands, chunk)).reshape(devices, chunk)
     gathered = lax.all_to_all(outgoing, axes, 0, 0, tiled=True)
-    return gathered.reshape(local_state.shape)
+    gathered, beside_back = lax.optimization_barrier((gathered, beside_back))
+    return gathered.reshape(local_state.shape), beside_out, beside_back
 
 
 def spatial_conv(padded, spatial_kernel):
@@ -81,11 +83,11 @@
 
 
 def split_dot(values, matrix):
-    high = values.astype(jnp.bfloat16)
-    low = (values - high.astype(jnp.float32)).astype(jnp.bfloat16)
-    return jnp.dot(high, matrix, preferred_element_type=jnp.float32) + jnp.dot(
-        low, matrix, preferred_element_type=jnp.float32
-    )
+    high = lax.reduce_precision(values, exponent_bits=8, mantissa_bits=7)
+    low = values - high
+    return jnp.dot(
+        high.astype(jnp.bfloat16), matrix, preferred_element_type=jnp.float32
+    ) + jnp.dot(low.astype(jnp.bfloat16), matrix, preferred_element_type=jnp.float32)
 
 
 def head_norm(attended):
@@ -109,13 +111,14 @@
     local_state = jnp.einsum(
         "thd,the->hde", jnp.maximum(key_rows, 0), value_rows, preferred_element_type=jnp.float32
     )
-    state_low = prefix_state(local_state)
+    padded = extended(value_heads, (("space", 1),), 1)
+    spatial = spatial_conv(padded, spatial_kernel)
+    earlier_frames = from_behind(spatial, "tm", 1)
+    weight_flat = weight_stack.reshape(model_width, model_width)
+    state_low, spatial, weight_flat = prefix_state(local_state, spatial, weight_flat)
     flat_queries = jnp.maximum(query_heads.reshape(token_count, model_width), 0)
     attended = banded_attention(flat_queries, state_low)
     normed = head_norm(attended).reshape(frame_count, row_count, col_count, model_width) * head_gain
-    padded = extended(value_heads, (("space", 1),), 1)
-    spatial = spatial_conv(padded, spatial_kernel)
-    earlier_frames = from_behind(spatial, "tm", 1)
     window = jnp.concatenate([earlier_frames, spatial], axis=0)
     temporal = jnp.zeros(normed.shape, jnp.float32)
     for back_step in range(3):
@@ -124,7 +127,7 @@
         ].astype(jnp.float32)
     mixed = (normed + temporal).astype(jnp.bfloat16).reshape(token_count, model_width)
     projected = jnp.dot(
-        mixed, weight_stack.reshape(model_width, model_width), preferred_element_type=jnp.float32
+        mixed, weight_flat, preferred_element_type=jnp.float32
     )
     return projected.astype(jnp.bfloat16).reshape(frame_count, row_count, col_count, model_width)
 

time: 263 us -> 220 us (0.84); the launches traced: 259 us -> 219 us
  waiting for transfers between devices: 65.4 us -> 45.4 us
  other arithmetic: 34.6 us -> 24.1 us
  starting transfers between devices: 41.8 us -> 34.1 us
  matrix products: 27 us -> 23.1 us
    ppermute x1, waiting for transfers between devices: 40.6 us -> 0.01 us  [extended(): lax.ppermute(lax.slice_in_dim(block, block.shape[dim] - width, None, axis...]
    all_to_all x1, waiting for transfers between devices: 0.01 us -> 33 us  [prefix_state(): mine = lax.all_to_all(flat, axes, 0, 0, tiled=True)]
    ppermute x1, waiting for transfers between devices: 17.3 us -> 0.01 us  [from_behind(): return lax.ppermute(block, axis, route)]
    optimization_barrier x0 -> x3, local copies, waits for them, and re-layouts: none -> 12.5 us  [the longest x2 12.1 us: prefix_state(): gathered, beside_back = lax.optimization_barrier((gathered, beside_back))]
    unnamed x37 -> x27, local copies, waits for them, and re-layouts: 23 us -> 10.6 us
    all_to_all x1, waiting for transfers between devices: 4.72 us -> 12.4 us  [prefix_state(): gathered = lax.all_to_all(outgoing, axes, 0, 0, tiled=True)]
    all_to_all x1, starting transfers between devices: 13.9 us -> 6.94 us  [prefix_state(): gathered = lax.all_to_all(outgoing, axes, 0, 0, tiled=True)]
    ppermute x1, starting transfers between devices: 3.79 us -> 8.79 us  [extended(): lax.ppermute(lax.slice_in_dim(block, block.shape[dim] - width, None, axis...]
  transfers between devices with their start and end apart: 6 -> 6, of which waited for: 4 -> 2; matrix products, arithmetic and copies ran while one was open for 31% -> 36% of each run, Pallas kernels for 0% -> 0%
where the time goes in v3:
time: 220 us; the launch traced here: 219 us
  local copies, waits for them, and re-layouts  57.2 us (26%)
  waiting for transfers between devices  45.4 us (21%)
  starting transfers between devices  34.1 us (16%)
  other arithmetic  24.1 us (11%)
  matrix products  23.1 us (10%)
  blocking collectives  21.5 us (10%)
  between operations  13.7 us (6%)
    all_to_all x1, waiting for transfers between devices, prefix_state(): mine = lax.all_to_all(flat, axes, 0, 0, tiled=True)  33 us
    all_gather x1, blocking collectives, per_device(): weight_band = lax.all_gather(out_weight, 'tm', axis=1, tiled=True)  21.5 us
    all_to_all x1, starting transfers between devices, prefix_state(): mine = lax.all_to_all(flat, axes, 0, 0, tiled=True)  13.1 us
    all_to_all x1, waiting for transfers between devices, prefix_state(): gathered = lax.all_to_all(outgoing, axes, 0, 0, tiled=True)  12.4 us
    optimization_barrier x2, local copies, waits for them, and re-layouts, prefix_state(): gathered, beside_back = lax.optimization_barrier((gathered, beside_back))  12.1 us
    unnamed x27, local copies, waits for them, and re-layouts  10.6 us
    select_n x3, local copies, waits for them, and re-layouts, banded_attention(): jnp.where(eye[:, None, :, None], blocks[:, :, None, :], jnp.zeros((), blo...  9.26 us
    dot_general x1, matrix products, per_device(): projected = jnp.dot(mixed, weight_flat, preferred_element_type=jnp.float32)  9.08 us
  transfers between devices with their start and end apart: 6, of which 2 were waited for; matrix products, arithmetic and copies ran while one was open for 36% of the time, Pallas kernels for 0%

profile of v3, /device:TPU:1, one launch (start us, length us, event | category | flops | bytes accessed | tf_op | source)
XLA Modules:
  0.0 219.2 jit_solution(9935309532955399902)
XLA Ops:
  8.3 21.5 %all-gather.1 = bf16[16,140,140]{2,1,0:T(8,128)(2,1)S(1)} all-gather(bf16[1,140,140]{2,1,0:T(8,128)(2,1)} %bitcast.39), channel_id=1, replica_groups=mesh['tm'=16,'space'=16] {'tm'}, dimensions={0}, use_global_device_ids=true | all-gather | bytes 666400 | tf_op jit(solution)/shard_map/all_gather | solution.py:105
  34.5 8.8 %collective-permute-start = (bf16[2,1,64,2240]{3,2,1,0:T(8,128)(2,1)}, bf16[2,1,64,2240]{3,2,1,0:T(8,128)(2,1)}, u32[]{:S(2)}, u32[]{:S(2)}) collective-permute-start(bf16[2,1,64,2240]{3,2,1,0:T(8,128)(2,1)} %get-tuple-element.25), channel_id=1, source_target_pairs={{0,1},{1,2},{2,3},{3,4},{4,5},{5,6},{6,7},{7,8},{8,9},{9,10},{10,1... | collective-permute-start | bytes 1720328 | tf_op jit(solution)/shard_map/ppermute | solution.py:20
  45.2 4.3 %reshape.110 = bf16[512,20,112]{2,1,0:T(8,128)(2,1)} reshape(bf16[2,4,64,2240]{3,2,1,0:T(8,128)(2,1)S(1)} %copy-done) | data formatting | bytes 4587520 | tf_op jit(solution)/shard_map/reshape | solution.py:110
  49.5 3.7 %broadcast_maximum_fusion = bf16[2,4,64,2240]{3,2,1,0:T(8,128)(2,1)} fusion(bf16[2,4,64,2240]{3,2,1,0:T(8,128)(2,1)} %param.8), kind=kLoop, calls=%fused_computation.27 | loop fusion | flops 1146880 | bytes 4587520 | tf_op jit(solution)/shard_map/max | solution.py:112
  53.2 6.5 %max.20 = bf16[512,20,112]{2,1,0:T(8,128)(2,1)} reshape(bf16[2,4,64,2240]{3,2,1,0:T(8,128)(2,1)} %broadcast_maximum_fusion) | data formatting | bytes 4587520 | tf_op jit(solution)/shard_map/max | solution.py:112
  59.7 4.1 %fusion.8 = f32[20,112,112]{2,1,0:T(8,128)S(1)} fusion(bf16[512,20,112]{2,1,0:T(8,128)(2,1)} %reshape.110, bf16[512,20,112]{2,1,0:T(8,128)(2,1)} %max.20), kind=kOutput, calls=%fused_computation.17 | convolution fusion | flops 256901120 | bytes 5591040 | tf_op jit(solution)/shard_map/thd,the->hde/dot_general | solution.py:111
  63.8 3.6 %all_to_all.22 = f32[256,1,980]{2,1,0:T(1,128)} reshape(f32[20,112,112]{2,1,0:T(8,128)S(1)} %fusion.8) | data formatting | bytes 2007040 | tf_op jit(solution)/shard_map/all_to_all | solution.py:40
  67.4 13.1 %all-to-all-start = ((f32[256,1,980]{2,1,0:T(1,128)}), f32[256,1,980]{2,1,0:T(1,128)S(1)}, u32[]{:S(2)}, u32[]{:S(2)}) async-start(f32[256,1,980]{2,1,0:T(1,128)} %all_to_all.22), calls=%async_computation | async-start | bytes 2097152 | tf_op jit(solution)/shard_map/all_to_all | solution.py:40
  82.4 2.4 %fusion.7 = bf16[2,6,66,2240]{3,2,1,0:T(8,128)(2,1)S(1)} fusion(bf16[2,1,64,2240]{3,2,1,0:T(8,128)(2,1)} %collective-permute-done.1, bf16[2,4,64,2240]{3,2,1,0:T(8,128)(2,1)S(1)} %copy-done, bf16[2,1,64,2240]{3,2,1,0:T(8,128)(2,1)} %collective-permute-done), kind=kLoop, calls=%fused_computation.16 | loop fusion | flops 21288960 | bytes 6988800 | tf_op jit(solution)/shard_map/concatenate | solution.py:24
  84.8 6.8 %add_convert_fusion.1 = bf16[2,4,64,2240]{3,2,1,0:T(8,128)(2,1)} fusion(bf16[2,4,64,2240]{3,2,1,0:T(8,128)(2,1)S(1)} %copy-done, bf16[2,6,66,2240]{3,2,1,0:T(8,128)(2,1)S(1)} %fusion.7, bf16[2,1,64,2240]{3,2,1,0:T(8,128)(2,1)} %collective-permute-done.1, bf16[2,1,64,2240]{3,2,1,0:T(8,128)(2,1)} %collective-permute-done, f32[2240]{0:T(1024)S(1)} %get-tuple-element.20, ...), kind=kLoop, calls=%fused_computation.10 | loop fusion | flops 33259520 | bytes 19577600 | tf_op jit(solution)/shard_map/convert_element_type | solution.py:61
  91.6 33.0 %all-to-all-done = f32[256,1,980]{2,1,0:T(1,128)S(1)} async-done(((f32[256,1,980]{2,1,0:T(1,128)}), f32[256,1,980]{2,1,0:T(1,128)S(1)}, u32[]{:S(2)}, u32[]{:S(2)}) %all-to-all-start) | async-done | bytes 1003552 | tf_op jit(solution)/shard_map/all_to_all | solution.py:40
  129.4 6.9 %all-to-all-start.1 = ((bf16[256,2,490]{2,1,0:T(2,128)(2,1)}), bf16[256,2,490]{2,1,0:T(2,128)(2,1)}, u32[]{:S(2)}, u32[]{:S(2)}) async-start(bf16[256,2,490]{2,1,0:T(2,128)(2,1)} %reshape.136), calls=%async_computation.1 | async-start | bytes 1048576 | tf_op jit(solution)/shard_map/all_to_all | solution.py:45
  136.5 3.3 %broadcast_maximum_fusion.1 = bf16[2,4,64,2240]{3,2,1,0:T(8,128)(2,1)} fusion(bf16[2,4,64,2240]{3,2,1,0:T(8,128)(2,1)} %param.7), kind=kLoop, calls=%fused_computation.28 | loop fusion | flops 1146880 | bytes 4587520 | tf_op jit(solution)/shard_map/max | solution.py:119
  139.8 3.3 %collective-permute-start.2 = (bf16[2,4,64,2240]{3,2,1,0:T(8,128)(2,1)S(1)}, bf16[2,4,64,2240]{3,2,1,0:T(8,128)(2,1)}, u32[]{:S(2)}, u32[]{:S(2)}) collective-permute-start(bf16[2,4,64,2240]{3,2,1,0:T(8,128)(2,1)S(1)} %copy-done.1), channel_id=1, source_target_pairs={{0,16},{16,32},{32,48},{48,64},{64,80},{80,96},{96,112},{112,128},... | collective-permute-start | bytes 6881288 | tf_op jit(solution)/shard_map/ppermute | solution.py:31
  143.0 12.4 %all-to-all-done.1 = bf16[256,2,490]{2,1,0:T(2,128)(2,1)} async-done(((bf16[256,2,490]{2,1,0:T(2,128)(2,1)}), bf16[256,2,490]{2,1,0:T(2,128)(2,1)}, u32[]{:S(2)}, u32[]{:S(2)}) %all-to-all-start.1) | async-done | bytes 501792 | tf_op jit(solution)/shard_map/all_to_all | solution.py:45
  155.5 4.0 %reshape.137 = bf16[256,1,980]{2,1,0:T(2,128)(2,1)S(1)} reshape(bf16[256,2,490]{2,1,0:T(2,128)(2,1)} %all-to-all-done.1) | data formatting | bytes 1003520
  161.4 11.9 %reshape.122 = bf16[2240,2240]{1,0:T(8,128)(2,1)} reshape(bf16[16,140,2240]{2,1,0:T(8,128)(2,1)} %all-gather.5.cloned.1.call-done) | data formatting | bytes 20070400 | tf_op jit(solution)/shard_map/optimization_barrier | solution.py:46
  176.1 2.4 %broadcast_select_fusion.1 = (bf16[8,112,8,112]{3,2,1,0:T(8,128)(2,1)}, bf16[8,112,8,112]{3,2,1,0:T(8,128)(2,1)}) fusion(pred[8,8]{1,0:T(8,128)(4,1)S(1)} %iota_compare_fusion.15, bf16[8,112,112]{2,1,0:T(8,128)(2,1)S(1)} %get-tuple-element.27, bf16[8,112,112]{2,1,0:T(8,128)(2,1)S(1)} %get-tuple-element.28), kind=kLoop, calls=%fused_computation.26 | loop fusion | flops 1605632 | bytes 3612736 | tf_op jit(solution)/shard_map/jit(_where)/select_n | solution.py:72
  180.0 4.1 %select_n.40 = bf16[896,896]{1,0:T(8,128)(2,1)} reshape(bf16[8,112,8,112]{3,2,1,0:T(8,128)(2,1)} %get-tuple-element.29) | data formatting | bytes 3211264 | tf_op jit(solution)/shard_map/jit(_where)/select_n | solution.py:72
  184.1 4.1 %select_n.42 = bf16[896,896]{1,0:T(8,128)(2,1)} reshape(bf16[8,112,8,112]{3,2,1,0:T(8,128)(2,1)} %get-tuple-element.30) | data formatting | bytes 3211264 | tf_op jit(solution)/shard_map/jit(_where)/select_n | solution.py:72
  188.2 3.0 %fusion.29 = f32[512,896]{1,0:T(8,128)S(1)} fusion(bf16[896,896]{1,0:T(8,128)(2,1)} %select_n.40, bf16[512,2240]{1,0:T(8,128)(2,1)} %bitcast.33), kind=kOutput, calls=%fused_computation.38 | convolution fusion | flops 822083584 | bytes 4358144 | tf_op jit(solution)/shard_map/dot_general | solution.py:76
  196.7 4.0 %add_convert_fusion = bf16[2,4,64,2240]{3,2,1,0:T(8,128)(2,1)S(1)} fusion(bf16[2,4,64,2240]{3,2,1,0:T(8,128)(2,1)} %collective-permute-done.2, bf16[2,4,64,2240]{3,2,1,0:T(8,128)(2,1)S(1)} %copy-done.1, f32[2,4,64,2240]{3,2,1,0:T(8,128)S(1)} %bitcast.28, f32[2240]{0:T(1024)S(1)} %get-tuple-element.23, f32[2240]{0:T(1024)S(1)} %get-tuple-element.24, ...), kind=kLoop, calls=%fused_computation.9 | loop fusion | flops 13762560 | bytes 11504640 | tf_op jit(solution)/shard_map/convert_element_type | solution.py:128
  200.8 9.1 %convolution_convert_fusion = bf16[512,2240]{0,1:T(8,128)(2,1)S(1)} fusion(bf16[512,2240]{1,0:T(8,128)(2,1)S(1)} %bitcast.36, bf16[2240,2240]{1,0:T(8,128)(2,1)S(1)} %bitcast.30), kind=kOutput, calls=%fused_computation.14 | convolution fusion | flops 5139169280 | bytes 14622720 | tf_op jit(solution)/shard_map/dot_general | solution.py:129
  209.9 2.5 %copy.56 = bf16[512,2240]{1,0:T(8,128)(2,1)} copy(bf16[512,2240]{0,1:T(8,128)(2,1)S(1)} %convolution_convert_fusion) | data formatting | bytes 4587520 | tf_op jit(solution)/shard_map/convert_element_type | solution.py:132
  (60 shorter events, 26.6 us)
Async XLA Ops:
  6.5 26.8 %copy-start = (bf16[2,4,64,2240]{3,2,1,0:T(8,128)(2,1)S(1)}, bf16[2,4,64,2240]{3,2,1,0:T(8,128)(2,1)}, u32[]{:S(2)}) copy-start(bf16[2,4,64,2240]{3,2,1,0:T(8,128)(2,1)} %param.9) | copy-start | bytes 6881284
  6.5 154.9 %all-gather.5.cloned.1.call-start = ((), (), s32[]{:S(2)}) async-start(), calls=%async_computation.2 | async-start | bytes 11280384 | tf_op jit(solution)/shard_map/all_gather | solution.py:106
  34.5 47.9 %collective-permute-start = (bf16[2,1,64,2240]{3,2,1,0:T(8,128)(2,1)}, bf16[2,1,64,2240]{3,2,1,0:T(8,128)(2,1)}, u32[]{:S(2)}, u32[]{:S(2)}) collective-permute-start(bf16[2,1,64,2240]{3,2,1,0:T(8,128)(2,1)} %get-tuple-element.25), channel_id=1, source_target_pairs={{0,1},{1,2},{2,3},{3,4},{4,5},{5,6},{6,7},{7,8},{8,9},{9,10},{10,1... | collective-permute-start | bytes 1720328 | tf_op jit(solution)/shard_map/ppermute | solution.py:20
  43.3 39.1 %collective-permute-start.1 = (bf16[2,1,64,2240]{3,2,1,0:T(8,128)(2,1)}, bf16[2,1,64,2240]{3,2,1,0:T(8,128)(2,1)}, u32[]{:S(2)}, u32[]{:S(2)}) collective-permute-start(bf16[2,1,64,2240]{3,2,1,0:T(8,128)(2,1)} %get-tuple-element.26), channel_id=1, source_target_pairs={{1,0},{2,1},{3,2},{4,3},{5,4},{6,5},{7,6},{8,7},{9,8},{10,9},{11,1... | collective-permute-start | bytes 1720328 | tf_op jit(solution)/shard_map/ppermute | solution.py:23
  67.4 57.1 %all-to-all-start = ((f32[256,1,980]{2,1,0:T(1,128)}), f32[256,1,980]{2,1,0:T(1,128)S(1)}, u32[]{:S(2)}, u32[]{:S(2)}) async-start(f32[256,1,980]{2,1,0:T(1,128)} %all_to_all.22), calls=%async_computation | async-start | bytes 2097152 | tf_op jit(solution)/shard_map/all_to_all | solution.py:40
  125.8 10.6 %copy-start.6 = (f32[3,2240]{1,0:T(4,128)S(1)}, f32[3,2240]{1,0:T(4,128)}, u32[]{:S(2)}) copy-start(f32[3,2240]{1,0:T(4,128)} %param.12) | copy-start | bytes 80644
  129.4 10.4 %copy-start.1 = (bf16[2,4,64,2240]{3,2,1,0:T(8,128)(2,1)S(1)}, bf16[2,4,64,2240]{3,2,1,0:T(8,128)(2,1)}, u32[]{:S(2)}) copy-start(bf16[2,4,64,2240]{3,2,1,0:T(8,128)(2,1)} %add_convert_fusion.1) | copy-start | bytes 6881284
  129.4 26.0 %all-to-all-start.1 = ((bf16[256,2,490]{2,1,0:T(2,128)(2,1)}), bf16[256,2,490]{2,1,0:T(2,128)(2,1)}, u32[]{:S(2)}, u32[]{:S(2)}) async-start(bf16[256,2,490]{2,1,0:T(2,128)(2,1)} %reshape.136), calls=%async_computation.1 | async-start | bytes 1048576 | tf_op jit(solution)/shard_map/all_to_all | solution.py:45
  139.8 56.9 %collective-permute-start.2 = (bf16[2,4,64,2240]{3,2,1,0:T(8,128)(2,1)S(1)}, bf16[2,4,64,2240]{3,2,1,0:T(8,128)(2,1)}, u32[]{:S(2)}, u32[]{:S(2)}) collective-permute-start(bf16[2,4,64,2240]{3,2,1,0:T(8,128)(2,1)S(1)} %copy-done.1), channel_id=1, source_target_pairs={{0,16},{16,32},{32,48},{48,64},{64,80},{80,96},{96,112},{112,128},... | collective-permute-start | bytes 6881288 | tf_op jit(solution)/shard_map/ppermute | solution.py:31
  161.4 11.9 %copy-start.3 = (bf16[256,1,980]{0,2,1:T(8,128)(2,1)S(1)}, bf16[256,1,980]{0,2,1:T(8,128)(2,1)}, u32[]{:S(2)}) copy-start(bf16[256,1,980]{0,2,1:T(8,128)(2,1)} %copy.49) | copy-start | bytes 1505284
  176.1 2.4 %copy-start.4 = (bf16[448,448]{1,0:T(8,128)(2,1)S(1)}, bf16[448,448]{1,0:T(8,128)(2,1)}, u32[]{:S(2)}) copy-start(bf16[448,448]{1,0:T(8,128)(2,1)} %select_n.44) | copy-start | bytes 1204228
  188.2 3.1 %copy-start.2 = (bf16[2,4,64,2240]{3,2,1,0:T(8,128)(2,1)S(1)}, bf16[2,4,64,2240]{3,2,1,0:T(8,128)(2,1)}, u32[]{:S(2)}) copy-start(bf16[2,4,64,2240]{3,2,1,0:T(8,128)(2,1)} %broadcast_maximum_fusion.1) | copy-start | bytes 6881284
  188.2 3.1 %copy-start.5 = (bf16[896,896]{1,0:T(8,128)(2,1)S(1)}, bf16[896,896]{1,0:T(8,128)(2,1)}, u32[]{:S(2)}) copy-start(bf16[896,896]{1,0:T(8,128)(2,1)} %select_n.42) | copy-start | bytes 4816900
  195.5 1.2 copy-start.7
  195.5 5.2 %slice-start = ((s8[10321920]{0:T(1024)(128)(4,1)}), s8[4194304]{0:T(1024)(128)(4,1)S(1)}, s32[]{:S(2)}) async-start(s8[10321920]{0:T(1024)(128)(4,1)} %bitcast.29), calls=%async_computation.3 | async-start | bytes 8388608
  195.5 5.2 %slice-start.1 = ((s8[10321920]{0:T(1024)(128)(4,1)}), s8[4194304]{0:T(1024)(128)(4,1)S(1)}, s32[]{:S(2)}) async-start(s8[10321920]{0:T(1024)(128)(4,1)} %bitcast.29), calls=%async_computation.4 | async-start | bytes 8388608
  196.7 4.1 %slice-start.2 = ((s8[10321920]{0:T(1024)(128)(4,1)}), s8[1933312]{0:T(1024)(128)(4,1)S(1)}, s32[]{:S(2)}) async-start(s8[10321920]{0:T(1024)(128)(4,1)} %bitcast.29), calls=%async_computation.5 | async-start | bytes 3866624
Sparse Core Ops, SparseCore 0:
  33.5 95.4 all-gather.4

commit v4 on v3

--- a/solution.py
+++ b/solution.py
@@ -102,8 +102,8 @@
     query_heads, key_heads, value_heads, head_gain, spatial_kernel, temporal_kernel, out_weight
 ):
     frame_count, row_count, col_count, model_width = query_heads.shape
-    weight_band = lax.all_gather(out_weight, "tm", axis=1, tiled=True)
-    weight_stack = lax.all_gather(weight_band, "space", axis=0)
+    weight_cols = lax.all_gather(out_weight, "space", axis=0, tiled=True)
+    weight_stack = lax.all_gather(weight_cols, "tm", axis=0)
     token_count = frame_count * row_count * col_count
     queries = query_heads.reshape(token_count, HEADS, HEAD_DIM)
     key_rows = key_heads.reshape(token_count, HEADS, HEAD_DIM)
@@ -114,7 +114,7 @@
     padded = extended(value_heads, (("space", 1),), 1)
     spatial = spatial_conv(padded, spatial_kernel)
     earlier_frames = from_behind(spatial, "tm", 1)
-    weight_flat = weight_stack.reshape(model_width, model_width)
+    weight_flat = weight_stack.transpose(1, 0, 2).reshape(model_width, model_width)
     state_low, spatial, weight_flat = prefix_state(local_state, spatial, weight_flat)
     flat_queries = jnp.maximum(query_heads.reshape(token_count, model_width), 0)
     attended = banded_attention(flat_queries, state_low)

time: 220 us -> 205 us (0.932); the launches traced: 219 us -> 201 us
  waiting for transfers between devices: 45.4 us -> 37.3 us
  starting transfers between devices: 34.1 us -> 26.5 us
  blocking collectives: 21.5 us -> 25 us
  matrix products: 23.1 us -> 19.8 us
    reshape x0 -> x1, local copies, waits for them, and re-layouts: none -> 11.9 us  [per_device(): weight_stack.transpose(1, 0, 2).reshape(model_width, model_width)]
    optimization_barrier x2 -> x1, local copies, waits for them, and re-layouts: 12.1 us -> 0.21 us  [prefix_state(): gathered, beside_back = lax.optimization_barrier((gathered, beside_back))]
    all_to_all x1, waiting for transfers between devices: 33 us -> 21.5 us  [prefix_state(): mine = lax.all_to_all(flat, axes, 0, 0, tiled=True)]
    ppermute x1, starting transfers between devices: 8.79 us -> 1.91 us  [extended(): lax.ppermute(lax.slice_in_dim(block, block.shape[dim] - width, None, axis...]
    all_gather x1, blocking collectives: 21.5 us -> 25 us  [per_device(): weight_cols = lax.all_gather(out_weight, 'space', axis=0, tiled=True)]
    dot_general x1, matrix products: 9.08 us -> 5.82 us  [per_device(): projected = jnp.dot(mixed, weight_flat, preferred_element_type=jnp.float32)]
    ppermute x1, waiting for transfers between devices: 0.01 us -> 3.2 us  [from_behind(): return lax.ppermute(block, axis, route)]
    unnamed x27 -> x26, local copies, waits for them, and re-layouts: 10.6 us -> 8.79 us
  transfers between devices with their start and end apart: 6 -> 6, of which waited for: 2 -> 3; matrix products, arithmetic and copies ran while one was open for 36% -> 40% of each run, Pallas kernels for 0% -> 0%
where the time goes in v4:
time: 205 us; the launch traced here: 201 us
  local copies, waits for them, and re-layouts  55.4 us (27%)
  waiting for transfers between devices  37.3 us (18%)
  starting transfers between devices  26.5 us (13%)
  blocking collectives  25 us (12%)
  other arithmetic  23.4 us (11%)
  matrix products  19.8 us (10%)
  between operations  13.7 us (7%)
    all_gather x1, blocking collectives, per_device(): weight_cols = lax.all_gather(out_weight, 'space', axis=0, tiled=True)  25 us
    all_to_all x1, waiting for transfers between devices, prefix_state(): mine = lax.all_to_all(flat, axes, 0, 0, tiled=True)  21.5 us
    all_to_all x1, waiting for transfers between devices, prefix_state(): gathered = lax.all_to_all(outgoing, axes, 0, 0, tiled=True)  12.6 us
    reshape x1, local copies, waits for them, and re-layouts, per_device(): weight_stack.transpose(1, 0, 2).reshape(model_width, model_width)  11.9 us
    all_to_all x1, starting transfers between devices, prefix_state(): mine = lax.all_to_all(flat, axes, 0, 0, tiled=True)  11 us
    select_n x3, local copies, waits for them, and re-layouts, banded_attention(): jnp.where(eye[:, None, :, None], blocks[:, :, None, :], jnp.zeros((), blo...  9.26 us
    unnamed x26, local copies, waits for them, and re-layouts  8.79 us
    all_to_all x1, starting transfers between devices, prefix_state(): gathered = lax.all_to_all(outgoing, axes, 0, 0, tiled=True)  7.12 us
  transfers between devices with their start and end apart: 6, of which 3 were waited for; matrix products, arithmetic and copies ran while one was open for 40% of the time, Pallas kernels for 0%

profile of v4, /device:TPU:1, one launch (start us, length us, event | category | flops | bytes accessed | tf_op | source)
XLA Modules:
  0.0 201.1 jit_solution(1198886503408788469)
XLA Ops:
  6.5 25.0 %all-gather.1 = bf16[16,140,140]{2,1,0:T(8,128)(2,1)S(1)} all-gather(bf16[1,140,140]{2,1,0:T(8,128)(2,1)} %bitcast.37), channel_id=1, replica_groups=mesh['tm'=16,'space'=16] {'space'}, dimensions={0}, use_global_device_ids=true | all-gather | bytes 666400 | tf_op jit(solution)/shard_map/all_gather | solution.py:105
  38.1 3.2 %collective-permute-start.1 = (bf16[2,1,64,2240]{3,2,1,0:T(8,128)(2,1)}, bf16[2,1,64,2240]{3,2,1,0:T(8,128)(2,1)}, u32[]{:S(2)}, u32[]{:S(2)}) collective-permute-start(bf16[2,1,64,2240]{3,2,1,0:T(8,128)(2,1)} %get-tuple-element.26), channel_id=1, source_target_pairs={{1,0},{2,1},{3,2},{4,3},{5,4},{6,5},{7,6},{8,7},{9,8},{10,9},{11,1... | collective-permute-start | bytes 1720328 | tf_op jit(solution)/shard_map/ppermute | solution.py:23
  41.3 4.3 %reshape.110 = bf16[512,20,112]{2,1,0:T(8,128)(2,1)} reshape(bf16[2,4,64,2240]{3,2,1,0:T(8,128)(2,1)S(1)} %copy-done) | data formatting | bytes 4587520 | tf_op jit(solution)/shard_map/reshape | solution.py:110
  45.6 3.4 %broadcast_maximum_fusion = bf16[2,4,64,2240]{3,2,1,0:T(8,128)(2,1)} fusion(bf16[2,4,64,2240]{3,2,1,0:T(8,128)(2,1)} %param.8), kind=kLoop, calls=%fused_computation.27 | loop fusion | flops 1146880 | bytes 4587520 | tf_op jit(solution)/shard_map/max | solution.py:112
  49.0 6.6 %max.20 = bf16[512,20,112]{2,1,0:T(8,128)(2,1)} reshape(bf16[2,4,64,2240]{3,2,1,0:T(8,128)(2,1)} %broadcast_maximum_fusion) | data formatting | bytes 4587520 | tf_op jit(solution)/shard_map/max | solution.py:112
  55.6 4.1 %fusion.8 = f32[20,112,112]{2,1,0:T(8,128)S(1)} fusion(bf16[512,20,112]{2,1,0:T(8,128)(2,1)} %reshape.110, bf16[512,20,112]{2,1,0:T(8,128)(2,1)} %max.20), kind=kOutput, calls=%fused_computation.17 | convolution fusion | flops 256901120 | bytes 5591040 | tf_op jit(solution)/shard_map/thd,the->hde/dot_general | solution.py:111
  59.7 3.6 %all_to_all.22 = f32[256,1,980]{2,1,0:T(1,128)} reshape(f32[20,112,112]{2,1,0:T(8,128)S(1)} %fusion.8) | data formatting | bytes 2007040 | tf_op jit(solution)/shard_map/all_to_all | solution.py:40
  63.3 11.0 %all-to-all-start = ((f32[256,1,980]{2,1,0:T(1,128)}), f32[256,1,980]{2,1,0:T(1,128)S(1)}, u32[]{:S(2)}, u32[]{:S(2)}) async-start(f32[256,1,980]{2,1,0:T(1,128)} %all_to_all.22), calls=%async_computation | async-start | bytes 2097152 | tf_op jit(solution)/shard_map/all_to_all | solution.py:40
  76.1 2.4 %fusion.7 = bf16[2,6,66,2240]{3,2,1,0:T(8,128)(2,1)S(1)} fusion(bf16[2,1,64,2240]{3,2,1,0:T(8,128)(2,1)} %collective-permute-done.1, bf16[2,4,64,2240]{3,2,1,0:T(8,128)(2,1)S(1)} %copy-done, bf16[2,1,64,2240]{3,2,1,0:T(8,128)(2,1)} %collective-permute-done), kind=kLoop, calls=%fused_computation.16 | loop fusion | flops 21288960 | bytes 6988800 | tf_op jit(solution)/shard_map/concatenate | solution.py:24
  78.5 6.8 %add_convert_fusion.1 = bf16[2,4,64,2240]{3,2,1,0:T(8,128)(2,1)} fusion(bf16[2,4,64,2240]{3,2,1,0:T(8,128)(2,1)S(1)} %copy-done, bf16[2,6,66,2240]{3,2,1,0:T(8,128)(2,1)S(1)} %fusion.7, bf16[2,1,64,2240]{3,2,1,0:T(8,128)(2,1)} %collective-permute-done.1, bf16[2,1,64,2240]{3,2,1,0:T(8,128)(2,1)} %collective-permute-done, f32[2240]{0:T(1024)S(1)} %get-tuple-element.20, ...), kind=kLoop, calls=%fused_computation.10 | loop fusion | flops 33259520 | bytes 19577600 | tf_op jit(solution)/shard_map/convert_element_type | solution.py:61
  85.3 21.5 %all-to-all-done = f32[256,1,980]{2,1,0:T(1,128)S(1)} async-done(((f32[256,1,980]{2,1,0:T(1,128)}), f32[256,1,980]{2,1,0:T(1,128)S(1)}, u32[]{:S(2)}, u32[]{:S(2)}) %all-to-all-start) | async-done | bytes 1003552 | tf_op jit(solution)/shard_map/all_to_all | solution.py:40
  111.7 7.1 %all-to-all-start.1 = ((bf16[256,2,490]{2,1,0:T(2,128)(2,1)}), bf16[256,2,490]{2,1,0:T(2,128)(2,1)}, u32[]{:S(2)}, u32[]{:S(2)}) async-start(bf16[256,2,490]{2,1,0:T(2,128)(2,1)} %reshape.137), calls=%async_computation.1 | async-start | bytes 1048576 | tf_op jit(solution)/shard_map/all_to_all | solution.py:45
  118.9 3.3 %broadcast_maximum_fusion.1 = bf16[2,4,64,2240]{3,2,1,0:T(8,128)(2,1)} fusion(bf16[2,4,64,2240]{3,2,1,0:T(8,128)(2,1)} %param.7), kind=kLoop, calls=%fused_computation.28 | loop fusion | flops 1146880 | bytes 4587520 | tf_op jit(solution)/shard_map/max | solution.py:119
  122.2 3.2 %collective-permute-start.2 = (bf16[2,4,64,2240]{3,2,1,0:T(8,128)(2,1)S(1)}, bf16[2,4,64,2240]{3,2,1,0:T(8,128)(2,1)}, u32[]{:S(2)}, u32[]{:S(2)}) collective-permute-start(bf16[2,4,64,2240]{3,2,1,0:T(8,128)(2,1)S(1)} %copy-done.1), channel_id=1, source_target_pairs={{0,16},{16,32},{32,48},{48,64},{64,80},{80,96},{96,112},{112,128},... | collective-permute-start | bytes 6881288 | tf_op jit(solution)/shard_map/ppermute | solution.py:31
  125.5 12.6 %all-to-all-done.1 = bf16[256,2,490]{2,1,0:T(2,128)(2,1)} async-done(((bf16[256,2,490]{2,1,0:T(2,128)(2,1)}), bf16[256,2,490]{2,1,0:T(2,128)(2,1)}, u32[]{:S(2)}, u32[]{:S(2)}) %all-to-all-start.1) | async-done | bytes 501792 | tf_op jit(solution)/shard_map/all_to_all | solution.py:45
  138.0 4.0 %reshape.138 = bf16[256,1,980]{2,1,0:T(2,128)(2,1)S(1)} reshape(bf16[256,2,490]{2,1,0:T(2,128)(2,1)} %all-to-all-done.1) | data formatting | bytes 1003520
  144.0 11.9 %reshape.112 = bf16[2240,2240]{0,1:T(8,128)(2,1)} reshape(bf16[2240,16,140]{0,2,1:T(8,128)(2,1)} %bitcast.27) | data formatting | bytes 20070400 | tf_op jit(solution)/shard_map/reshape | solution.py:117
  162.5 4.1 %select_n.40 = bf16[896,896]{1,0:T(8,128)(2,1)} reshape(bf16[8,112,8,112]{3,2,1,0:T(8,128)(2,1)} %get-tuple-element.29) | data formatting | bytes 3211264 | tf_op jit(solution)/shard_map/jit(_where)/select_n | solution.py:72
  166.6 4.1 %select_n.42 = bf16[896,896]{1,0:T(8,128)(2,1)} reshape(bf16[8,112,8,112]{3,2,1,0:T(8,128)(2,1)} %get-tuple-element.30) | data formatting | bytes 3211264 | tf_op jit(solution)/shard_map/jit(_where)/select_n | solution.py:72
  170.7 3.0 %fusion.29 = f32[512,896]{1,0:T(8,128)S(1)} fusion(bf16[896,896]{1,0:T(8,128)(2,1)} %select_n.40, bf16[512,2240]{1,0:T(8,128)(2,1)} %bitcast.32), kind=kOutput, calls=%fused_computation.38 | convolution fusion | flops 822083584 | bytes 4358144 | tf_op jit(solution)/shard_map/dot_general | solution.py:76
  179.2 3.2 %collective-permute-done.2 = bf16[2,4,64,2240]{3,2,1,0:T(8,128)(2,1)} collective-permute-done((bf16[2,4,64,2240]{3,2,1,0:T(8,128)(2,1)S(1)}, bf16[2,4,64,2240]{3,2,1,0:T(8,128)(2,1)}, u32[]{:S(2)}, u32[]{:S(2)}) %collective-permute-start.2) | collective-permute-done | bytes 2293792 | tf_op jit(solution)/shard_map/ppermute | solution.py:31
  182.4 3.5 %add_convert_fusion = bf16[2,4,64,2240]{3,2,1,0:T(8,128)(2,1)S(1)} fusion(bf16[2,4,64,2240]{3,2,1,0:T(8,128)(2,1)} %collective-permute-done.2, bf16[2,4,64,2240]{3,2,1,0:T(8,128)(2,1)S(1)} %copy-done.1, f32[2,4,64,2240]{3,2,1,0:T(8,128)S(1)} %bitcast.26, f32[2240]{0:T(1024)S(1)} %get-tuple-element.23, f32[2240]{0:T(1024)S(1)} %get-tuple-element.24, ...), kind=kLoop, calls=%fused_computation.9 | loop fusion | flops 13762560 | bytes 11504640 | tf_op jit(solution)/shard_map/convert_element_type | solution.py:128
  186.0 5.8 %convolution_convert_fusion = bf16[512,2240]{0,1:T(8,128)(2,1)S(1)} fusion(bf16[512,2240]{1,0:T(8,128)(2,1)S(1)} %bitcast.34, bf16[2240,2240]{0,1:T(8,128)(2,1)S(1)} %bitcast.29), kind=kOutput, calls=%fused_computation.14 | convolution fusion | flops 5139169280 | bytes 14622720 | tf_op jit(solution)/shard_map/dot_general | solution.py:129
  191.8 2.5 %copy.53 = bf16[512,2240]{1,0:T(8,128)(2,1)} copy(bf16[512,2240]{0,1:T(8,128)(2,1)S(1)} %convolution_convert_fusion) | data formatting | bytes 4587520 | tf_op jit(solution)/shard_map/convert_element_type | solution.py:132
  (59 shorter events, 27.1 us)
Async XLA Ops:
  6.5 28.5 %copy-start = (bf16[2,4,64,2240]{3,2,1,0:T(8,128)(2,1)S(1)}, bf16[2,4,64,2240]{3,2,1,0:T(8,128)(2,1)}, u32[]{:S(2)}) copy-start(bf16[2,4,64,2240]{3,2,1,0:T(8,128)(2,1)} %param.9) | copy-start | bytes 6881284
  6.5 137.4 %all-gather.5.cloned.1.call-start = ((), (), s32[]{:S(2)}) async-start(), calls=%async_computation.2 | async-start | bytes 11280384 | tf_op jit(solution)/shard_map/all_gather | solution.py:106
  36.2 39.9 %collective-permute-start = (bf16[2,1,64,2240]{3,2,1,0:T(8,128)(2,1)}, bf16[2,1,64,2240]{3,2,1,0:T(8,128)(2,1)}, u32[]{:S(2)}, u32[]{:S(2)}) collective-permute-start(bf16[2,1,64,2240]{3,2,1,0:T(8,128)(2,1)} %get-tuple-element.25), channel_id=1, source_target_pairs={{0,1},{1,2},{2,3},{3,4},{4,5},{5,6},{6,7},{7,8},{8,9},{9,10},{10,1... | collective-permute-start | bytes 1720328 | tf_op jit(solution)/shard_map/ppermute | solution.py:20
  38.1 38.0 %collective-permute-start.1 = (bf16[2,1,64,2240]{3,2,1,0:T(8,128)(2,1)}, bf16[2,1,64,2240]{3,2,1,0:T(8,128)(2,1)}, u32[]{:S(2)}, u32[]{:S(2)}) collective-permute-start(bf16[2,1,64,2240]{3,2,1,0:T(8,128)(2,1)} %get-tuple-element.26), channel_id=1, source_target_pairs={{1,0},{2,1},{3,2},{4,3},{5,4},{6,5},{7,6},{8,7},{9,8},{10,9},{11,1... | collective-permute-start | bytes 1720328 | tf_op jit(solution)/shard_map/ppermute | solution.py:23
  63.3 43.6 %all-to-all-start = ((f32[256,1,980]{2,1,0:T(1,128)}), f32[256,1,980]{2,1,0:T(1,128)S(1)}, u32[]{:S(2)}, u32[]{:S(2)}) async-start(f32[256,1,980]{2,1,0:T(1,128)} %all_to_all.22), calls=%async_computation | async-start | bytes 2097152 | tf_op jit(solution)/shard_map/all_to_all | solution.py:40
  108.0 10.8 %copy-start.6 = (f32[3,2240]{1,0:T(4,128)S(1)}, f32[3,2240]{1,0:T(4,128)}, u32[]{:S(2)}) copy-start(f32[3,2240]{1,0:T(4,128)} %param.12) | copy-start | bytes 80644
  111.7 10.5 %copy-start.1 = (bf16[2,4,64,2240]{3,2,1,0:T(8,128)(2,1)S(1)}, bf16[2,4,64,2240]{3,2,1,0:T(8,128)(2,1)}, u32[]{:S(2)}) copy-start(bf16[2,4,64,2240]{3,2,1,0:T(8,128)(2,1)} %add_convert_fusion.1) | copy-start | bytes 6881284
  111.7 26.3 %all-to-all-start.1 = ((bf16[256,2,490]{2,1,0:T(2,128)(2,1)}), bf16[256,2,490]{2,1,0:T(2,128)(2,1)}, u32[]{:S(2)}, u32[]{:S(2)}) async-start(bf16[256,2,490]{2,1,0:T(2,128)(2,1)} %reshape.137), calls=%async_computation.1 | async-start | bytes 1048576 | tf_op jit(solution)/shard_map/all_to_all | solution.py:45
  122.2 60.2 %collective-permute-start.2 = (bf16[2,4,64,2240]{3,2,1,0:T(8,128)(2,1)S(1)}, bf16[2,4,64,2240]{3,2,1,0:T(8,128)(2,1)}, u32[]{:S(2)}, u32[]{:S(2)}) collective-permute-start(bf16[2,4,64,2240]{3,2,1,0:T(8,128)(2,1)S(1)} %copy-done.1), channel_id=1, source_target_pairs={{0,16},{16,32},{32,48},{48,64},{64,80},{80,96},{96,112},{112,128},... | collective-permute-start | bytes 6881288 | tf_op jit(solution)/shard_map/ppermute | solution.py:31
  144.0 11.9 %copy-start.3 = (bf16[256,1,980]{0,2,1:T(8,128)(2,1)S(1)}, bf16[256,1,980]{0,2,1:T(8,128)(2,1)}, u32[]{:S(2)}) copy-start(bf16[256,1,980]{0,2,1:T(8,128)(2,1)} %copy.47) | copy-start | bytes 1505284
  158.7 2.4 %copy-start.4 = (bf16[448,448]{1,0:T(8,128)(2,1)S(1)}, bf16[448,448]{1,0:T(8,128)(2,1)}, u32[]{:S(2)}) copy-start(bf16[448,448]{1,0:T(8,128)(2,1)} %select_n.44) | copy-start | bytes 1204228
  170.7 3.1 %copy-start.2 = (bf16[2,4,64,2240]{3,2,1,0:T(8,128)(2,1)S(1)}, bf16[2,4,64,2240]{3,2,1,0:T(8,128)(2,1)}, u32[]{:S(2)}) copy-start(bf16[2,4,64,2240]{3,2,1,0:T(8,128)(2,1)} %broadcast_maximum_fusion.1) | copy-start | bytes 6881284
  170.7 3.1 %copy-start.5 = (bf16[896,896]{1,0:T(8,128)(2,1)S(1)}, bf16[896,896]{1,0:T(8,128)(2,1)}, u32[]{:S(2)}) copy-start(bf16[896,896]{1,0:T(8,128)(2,1)} %select_n.42) | copy-start | bytes 4816900
  178.1 4.3 %copy-start.7 = (f32[2240]{0:T(1024)S(1)}, f32[2240]{0:T(1024)}, u32[]{:S(2)}) copy-start(f32[2240]{0:T(1024)} %param.10) | copy-start | bytes 26884
  178.1 7.9 %slice-start = ((s8[10321920]{0:T(1024)(128)(4,1)}), s8[4194304]{0:T(1024)(128)(4,1)S(1)}, s32[]{:S(2)}) async-start(s8[10321920]{0:T(1024)(128)(4,1)} %bitcast.28), calls=%async_computation.3 | async-start | bytes 8388608
  178.1 7.9 %slice-start.1 = ((s8[10321920]{0:T(1024)(128)(4,1)}), s8[1933312]{0:T(1024)(128)(4,1)S(1)}, s32[]{:S(2)}) async-start(s8[10321920]{0:T(1024)(128)(4,1)} %bitcast.28), calls=%async_computation.4 | async-start | bytes 3866624
  182.4 3.6 %slice-start.2 = ((s8[10321920]{0:T(1024)(128)(4,1)}), s8[4194304]{0:T(1024)(128)(4,1)S(1)}, s32[]{:S(2)}) async-start(s8[10321920]{0:T(1024)(128)(4,1)} %bitcast.28), calls=%async_computation.5 | async-start | bytes 8388608
Sparse Core Ops, SparseCore 0:
  35.2 104.6 all-gather.4

commit v5 on v4

--- a/solution.py
+++ b/solution.py
@@ -103,7 +103,8 @@
 ):
     frame_count, row_count, col_count, model_width = query_heads.shape
     weight_cols = lax.all_gather(out_weight, "space", axis=0, tiled=True)
-    weight_stack = lax.all_gather(weight_cols, "tm", axis=0)
+    column_pad = -weight_cols.shape[1] % 16
+    weight_stack = lax.all_gather(jnp.pad(weight_cols, ((0, 0), (0, column_pad))), "tm", axis=0)
     token_count = frame_count * row_count * col_count
     queries = query_heads.reshape(token_count, HEADS, HEAD_DIM)
     key_rows = key_heads.reshape(token_count, HEADS, HEAD_DIM)
@@ -114,7 +115,8 @@
     padded = extended(value_heads, (("space", 1),), 1)
     spatial = spatial_conv(padded, spatial_kernel)
     earlier_frames = from_behind(spatial, "tm", 1)
-    weight_flat = weight_stack.transpose(1, 0, 2).reshape(model_width, model_width)
+    blocks, _, padded_width = weight_stack.shape
+    weight_flat = weight_stack.transpose(1, 0, 2).reshape(model_width, blocks * padded_width)
     state_low, spatial, weight_flat = prefix_state(local_state, spatial, weight_flat)
     flat_queries = jnp.maximum(query_heads.reshape(token_count, model_width), 0)
     attended = banded_attention(flat_queries, state_low)
@@ -126,9 +128,8 @@
             2 - back_step : 2 - back_step + frame_count
         ].astype(jnp.float32)
     mixed = (normed + temporal).astype(jnp.bfloat16).reshape(token_count, model_width)
-    projected = jnp.dot(
-        mixed, weight_flat, preferred_element_type=jnp.float32
-    )
+    projected = jnp.dot(mixed, weight_flat, preferred_element_type=jnp.float32)
+    projected = projected.reshape(token_count, blocks, padded_width)[:, :, : padded_width - column_pad]
     return projected.astype(jnp.bfloat16).reshape(frame_count, row_count, col_count, model_width)
 
 

time: 205 us -> 215 us (1.049)
  waiting for transfers between devices: 37.3 us -> 48.5 us
    ppermute x1, waiting for transfers between devices: 3.2 us -> 14.6 us  [from_behind(): return lax.ppermute(block, axis, route)]
    convert_element_type x1 -> x0, local copies, waits for them, and re-layouts: 2.47 us -> none  [per_device(): projected.astype(jnp.bfloat16)]
    reshape x1 -> x2, local copies, waits for them, and re-layouts: 11.9 us -> 11.6 us  [per_device(): projected.astype(jnp.bfloat16)]
    unnamed x26 -> x25, local copies, waits for them, and re-layouts: 8.79 us -> 9.05 us
  transfers between devices with their start and end apart: 6 -> 6, of which waited for: 3 -> 3; matrix products, arithmetic and copies ran while one was open for 40% -> 33% of each run, Pallas kernels for 0% -> 0%
where the time goes in v5:
time: 215 us; the launch traced here: 211 us
  local copies, waits for them, and re-layouts  54 us (25%)
  waiting for transfers between devices  48.5 us (23%)
  starting transfers between devices  26.3 us (12%)
  blocking collectives  24.9 us (12%)
  other arithmetic  23.3 us (11%)
  matrix products  20.2 us (9%)
  between operations  13.7 us (6%)
    all_gather x1, blocking collectives, per_device(): weight_cols = lax.all_gather(out_weight, 'space', axis=0, tiled=True)  24.9 us
    all_to_all x1, waiting for transfers between devices, prefix_state(): mine = lax.all_to_all(flat, axes, 0, 0, tiled=True)  21.5 us
    ppermute x1, waiting for transfers between devices, from_behind(): return lax.ppermute(block, axis, route)  14.6 us
    all_to_all x1, waiting for transfers between devices, prefix_state(): gathered = lax.all_to_all(outgoing, axes, 0, 0, tiled=True)  12.4 us
    reshape x2, local copies, waits for them, and re-layouts, per_device(): projected.astype(jnp.bfloat16)  11.6 us
    all_to_all x1, starting transfers between devices, prefix_state(): mine = lax.all_to_all(flat, axes, 0, 0, tiled=True)  11 us
    select_n x3, local copies, waits for them, and re-layouts, banded_attention(): jnp.where(eye[:, None, :, None], blocks[:, :, None, :], jnp.zeros((), blo...  9.27 us
    unnamed x25, local copies, waits for them, and re-layouts  9.05 us
  transfers between devices with their start and end apart: 6, of which 3 were waited for; matrix products, arithmetic and copies ran while one was open for 33% of the time, Pallas kernels for 0%

profile of v5, /device:TPU:1, one launch (start us, length us, event | category | flops | bytes accessed | tf_op | source)
XLA Modules:
  0.0 210.9 jit_solution(5996066947958125334)
XLA Ops:
  6.5 24.9 %all-gather.1 = bf16[16,140,140]{2,1,0:T(8,128)(2,1)S(1)} all-gather(bf16[1,140,140]{2,1,0:T(8,128)(2,1)} %bitcast.44), channel_id=1, replica_groups=mesh['tm'=16,'space'=16] {'space'}, dimensions={0}, use_global_device_ids=true | all-gather | bytes 666400 | tf_op jit(solution)/shard_map/all_gather | solution.py:105
  38.3 3.2 %collective-permute-start.1 = (bf16[2,1,64,2240]{3,2,1,0:T(8,128)(2,1)}, bf16[2,1,64,2240]{3,2,1,0:T(8,128)(2,1)}, u32[]{:S(2)}, u32[]{:S(2)}) collective-permute-start(bf16[2,1,64,2240]{3,2,1,0:T(8,128)(2,1)} %get-tuple-element.26), channel_id=1, source_target_pairs={{1,0},{2,1},{3,2},{4,3},{5,4},{6,5},{7,6},{8,7},{9,8},{10,9},{11,1... | collective-permute-start | bytes 1720328 | tf_op jit(solution)/shard_map/ppermute | solution.py:23
  41.5 4.3 %reshape.112 = bf16[512,20,112]{2,1,0:T(8,128)(2,1)} reshape(bf16[2,4,64,2240]{3,2,1,0:T(8,128)(2,1)S(1)} %copy-done) | data formatting | bytes 4587520 | tf_op jit(solution)/shard_map/reshape | solution.py:111
  45.8 3.4 %broadcast_maximum_fusion = bf16[2,4,64,2240]{3,2,1,0:T(8,128)(2,1)} fusion(bf16[2,4,64,2240]{3,2,1,0:T(8,128)(2,1)} %param.8), kind=kLoop, calls=%fused_computation.27 | loop fusion | flops 1146880 | bytes 4587520 | tf_op jit(solution)/shard_map/max | solution.py:113
  49.2 6.6 %max.20 = bf16[512,20,112]{2,1,0:T(8,128)(2,1)} reshape(bf16[2,4,64,2240]{3,2,1,0:T(8,128)(2,1)} %broadcast_maximum_fusion) | data formatting | bytes 4587520 | tf_op jit(solution)/shard_map/max | solution.py:113
  55.8 4.1 %fusion.8 = f32[20,112,112]{2,1,0:T(8,128)S(1)} fusion(bf16[512,20,112]{2,1,0:T(8,128)(2,1)} %reshape.112, bf16[512,20,112]{2,1,0:T(8,128)(2,1)} %max.20), kind=kOutput, calls=%fused_computation.17 | convolution fusion | flops 256901120 | bytes 5591040 | tf_op jit(solution)/shard_map/thd,the->hde/dot_general | solution.py:112
  59.9 3.6 %all_to_all.22 = f32[256,1,980]{2,1,0:T(1,128)} reshape(f32[20,112,112]{2,1,0:T(8,128)S(1)} %fusion.8) | data formatting | bytes 2007040 | tf_op jit(solution)/shard_map/all_to_all | solution.py:40
  63.5 11.0 %all-to-all-start = ((f32[256,1,980]{2,1,0:T(1,128)}), f32[256,1,980]{2,1,0:T(1,128)S(1)}, u32[]{:S(2)}, u32[]{:S(2)}) async-start(f32[256,1,980]{2,1,0:T(1,128)} %all_to_all.22), calls=%async_computation | async-start | bytes 2097152 | tf_op jit(solution)/shard_map/all_to_all | solution.py:40
  76.3 2.4 %fusion.7 = bf16[2,6,66,2240]{3,2,1,0:T(8,128)(2,1)S(1)} fusion(bf16[2,1,64,2240]{3,2,1,0:T(8,128)(2,1)} %collective-permute-done.1, bf16[2,4,64,2240]{3,2,1,0:T(8,128)(2,1)S(1)} %copy-done, bf16[2,1,64,2240]{3,2,1,0:T(8,128)(2,1)} %collective-permute-done), kind=kLoop, calls=%fused_computation.16 | loop fusion | flops 21288960 | bytes 6988800 | tf_op jit(solution)/shard_map/concatenate | solution.py:24
  78.7 6.8 %add_convert_fusion.1 = bf16[2,4,64,2240]{3,2,1,0:T(8,128)(2,1)} fusion(bf16[2,4,64,2240]{3,2,1,0:T(8,128)(2,1)S(1)} %copy-done, bf16[2,6,66,2240]{3,2,1,0:T(8,128)(2,1)S(1)} %fusion.7, bf16[2,1,64,2240]{3,2,1,0:T(8,128)(2,1)} %collective-permute-done.1, bf16[2,1,64,2240]{3,2,1,0:T(8,128)(2,1)} %collective-permute-done, f32[2240]{0:T(1024)S(1)} %get-tuple-element.20, ...), kind=kLoop, calls=%fused_computation.11 | loop fusion | flops 33259520 | bytes 19577600 | tf_op jit(solution)/shard_map/convert_element_type | solution.py:61
  85.5 21.5 %all-to-all-done = f32[256,1,980]{2,1,0:T(1,128)S(1)} async-done(((f32[256,1,980]{2,1,0:T(1,128)}), f32[256,1,980]{2,1,0:T(1,128)S(1)}, u32[]{:S(2)}, u32[]{:S(2)}) %all-to-all-start) | async-done | bytes 1003552 | tf_op jit(solution)/shard_map/all_to_all | solution.py:40
  111.8 7.0 %all-to-all-start.1 = ((bf16[256,2,490]{2,1,0:T(2,128)(2,1)}), bf16[256,2,490]{2,1,0:T(2,128)(2,1)}, u32[]{:S(2)}, u32[]{:S(2)}) async-start(bf16[256,2,490]{2,1,0:T(2,128)(2,1)} %reshape.140), calls=%async_computation.1 | async-start | bytes 1048576 | tf_op jit(solution)/shard_map/all_to_all | solution.py:45
  118.9 3.2 %broadcast_maximum_fusion.1 = bf16[2,4,64,2240]{3,2,1,0:T(8,128)(2,1)} fusion(bf16[2,4,64,2240]{3,2,1,0:T(8,128)(2,1)} %param.7), kind=kLoop, calls=%fused_computation.28 | loop fusion | flops 1146880 | bytes 4587520 | tf_op jit(solution)/shard_map/max | solution.py:121
  122.2 3.2 %collective-permute-start.2 = (bf16[2,4,64,2240]{3,2,1,0:T(8,128)(2,1)S(1)}, bf16[2,4,64,2240]{3,2,1,0:T(8,128)(2,1)}, u32[]{:S(2)}, u32[]{:S(2)}) collective-permute-start(bf16[2,4,64,2240]{3,2,1,0:T(8,128)(2,1)S(1)} %copy-done.1), channel_id=1, source_target_pairs={{0,16},{16,32},{32,48},{48,64},{64,80},{80,96},{96,112},{112,128},... | collective-permute-start | bytes 6881288 | tf_op jit(solution)/shard_map/ppermute | solution.py:31
  125.3 12.4 %all-to-all-done.1 = bf16[256,2,490]{2,1,0:T(2,128)(2,1)} async-done(((bf16[256,2,490]{2,1,0:T(2,128)(2,1)}), bf16[256,2,490]{2,1,0:T(2,128)(2,1)}, u32[]{:S(2)}, u32[]{:S(2)}) %all-to-all-start.1) | async-done | bytes 501792 | tf_op jit(solution)/shard_map/all_to_all | solution.py:45
  137.8 4.0 %reshape.141 = bf16[256,1,980]{2,1,0:T(2,128)(2,1)S(1)} reshape(bf16[256,2,490]{2,1,0:T(2,128)(2,1)} %all-to-all-done.1) | data formatting | bytes 1003520
  151.4 4.1 %select_n.40 = bf16[896,896]{1,0:T(8,128)(2,1)} reshape(bf16[8,112,8,112]{3,2,1,0:T(8,128)(2,1)} %get-tuple-element.29) | data formatting | bytes 3211264 | tf_op jit(solution)/shard_map/jit(_where)/select_n | solution.py:72
  155.5 4.1 %select_n.42 = bf16[896,896]{1,0:T(8,128)(2,1)} reshape(bf16[8,112,8,112]{3,2,1,0:T(8,128)(2,1)} %get-tuple-element.30) | data formatting | bytes 3211264 | tf_op jit(solution)/shard_map/jit(_where)/select_n | solution.py:72
  159.6 3.0 %fusion.29 = f32[512,896]{1,0:T(8,128)S(1)} fusion(bf16[896,896]{1,0:T(8,128)(2,1)} %select_n.40, bf16[512,2240]{1,0:T(8,128)(2,1)} %bitcast.38), kind=kOutput, calls=%fused_computation.38 | convolution fusion | flops 822083584 | bytes 4358144 | tf_op jit(solution)/shard_map/dot_general | solution.py:76
  168.0 14.6 %collective-permute-done.2 = bf16[2,4,64,2240]{3,2,1,0:T(8,128)(2,1)} collective-permute-done((bf16[2,4,64,2240]{3,2,1,0:T(8,128)(2,1)S(1)}, bf16[2,4,64,2240]{3,2,1,0:T(8,128)(2,1)}, u32[]{:S(2)}, u32[]{:S(2)}) %collective-permute-start.2) | collective-permute-done | bytes 2293792 | tf_op jit(solution)/shard_map/ppermute | solution.py:31
  182.6 3.5 %add_convert_fusion = bf16[2,4,64,2240]{3,2,1,0:T(8,128)(2,1)S(1)} fusion(bf16[2,4,64,2240]{3,2,1,0:T(8,128)(2,1)} %collective-permute-done.2, bf16[2,4,64,2240]{3,2,1,0:T(8,128)(2,1)S(1)} %copy-done.1, f32[2,4,64,2240]{3,2,1,0:T(8,128)S(1)} %bitcast.35, f32[2240]{0:T(1024)S(1)} %get-tuple-element.23, f32[2240]{0:T(1024)S(1)} %get-tuple-element.24, ...), kind=kLoop, calls=%fused_computation.10 | loop fusion | flops 13762560 | bytes 11504640 | tf_op jit(solution)/shard_map/convert_element_type | solution.py:130
  186.2 6.3 %fusion.46 = bf16[512,16,144]{0,2,1:T(8,128)(2,1)S(1)} fusion(bf16[512,2240,1]{1,0,2:T(8,128)(2,1)S(1)} %bitcast.41, bf16[16,144,2240]{2,1,0:T(8,128)(2,1)S(1)} %bitcast.47), kind=kOutput, calls=%fused_computation.76 | convolution fusion | flops 5284823040 | bytes 14974976 | tf_op jit(solution)/shard_map/dot_general | solution.py:131
  192.4 3.8 %reshape.127 = bf16[2,4,64,2240]{2,1,0,3:T(4,128)(2,1)} reshape(bf16[512,16,140]{0,2,1:T(8,128)(2,1)S(1)} %bitcast.40) | data formatting | bytes 4587520 | tf_op jit(solution)/shard_map/reshape | solution.py:133
  196.3 7.8 %copy.65 = bf16[2,4,64,2240]{3,2,1,0:T(8,128)(2,1)} copy(bf16[2,4,64,2240]{2,1,0,3:T(4,128)(2,1)} %reshape.127) | data formatting | bytes 4587520 | tf_op jit(solution)/shard_map/reshape | solution.py:133
  (58 shorter events, 28.4 us)
Async XLA Ops:
  6.5 137.2 %all-gather.5.cloned.1.call-start = ((), (), s32[]{:S(2)}) async-start(), calls=%async_computation.2 | async-start | bytes 11280384 | tf_op jit(solution)/shard_map/all_gather | solution.py:107
  31.4 3.8 %copy-start = (bf16[2,4,64,2240]{3,2,1,0:T(8,128)(2,1)S(1)}, bf16[2,4,64,2240]{3,2,1,0:T(8,128)(2,1)}, u32[]{:S(2)}) copy-start(bf16[2,4,64,2240]{3,2,1,0:T(8,128)(2,1)} %param.9) | copy-start | bytes 6881284
  36.3 40.0 %collective-permute-start = (bf16[2,1,64,2240]{3,2,1,0:T(8,128)(2,1)}, bf16[2,1,64,2240]{3,2,1,0:T(8,128)(2,1)}, u32[]{:S(2)}, u32[]{:S(2)}) collective-permute-start(bf16[2,1,64,2240]{3,2,1,0:T(8,128)(2,1)} %get-tuple-element.25), channel_id=1, source_target_pairs={{0,1},{1,2},{2,3},{3,4},{4,5},{5,6},{6,7},{7,8},{8,9},{9,10},{10,1... | collective-permute-start | bytes 1720328 | tf_op jit(solution)/shard_map/ppermute | solution.py:20
  38.3 38.0 %collective-permute-start.1 = (bf16[2,1,64,2240]{3,2,1,0:T(8,128)(2,1)}, bf16[2,1,64,2240]{3,2,1,0:T(8,128)(2,1)}, u32[]{:S(2)}, u32[]{:S(2)}) collective-permute-start(bf16[2,1,64,2240]{3,2,1,0:T(8,128)(2,1)} %get-tuple-element.26), channel_id=1, source_target_pairs={{1,0},{2,1},{3,2},{4,3},{5,4},{6,5},{7,6},{8,7},{9,8},{10,9},{11,1... | collective-permute-start | bytes 1720328 | tf_op jit(solution)/shard_map/ppermute | solution.py:23
  63.5 43.6 %all-to-all-start = ((f32[256,1,980]{2,1,0:T(1,128)}), f32[256,1,980]{2,1,0:T(1,128)S(1)}, u32[]{:S(2)}, u32[]{:S(2)}) async-start(f32[256,1,980]{2,1,0:T(1,128)} %all_to_all.22), calls=%async_computation | async-start | bytes 2097152 | tf_op jit(solution)/shard_map/all_to_all | solution.py:40
  108.2 10.6 %copy-start.5 = (f32[3,2240]{1,0:T(4,128)S(1)}, f32[3,2240]{1,0:T(4,128)}, u32[]{:S(2)}) copy-start(f32[3,2240]{1,0:T(4,128)} %param.12) | copy-start | bytes 80644
  111.8 10.3 %copy-start.1 = (bf16[2,4,64,2240]{3,2,1,0:T(8,128)(2,1)S(1)}, bf16[2,4,64,2240]{3,2,1,0:T(8,128)(2,1)}, u32[]{:S(2)}) copy-start(bf16[2,4,64,2240]{3,2,1,0:T(8,128)(2,1)} %add_convert_fusion.1) | copy-start | bytes 6881284
  111.8 25.9 %all-to-all-start.1 = ((bf16[256,2,490]{2,1,0:T(2,128)(2,1)}), bf16[256,2,490]{2,1,0:T(2,128)(2,1)}, u32[]{:S(2)}, u32[]{:S(2)}) async-start(bf16[256,2,490]{2,1,0:T(2,128)(2,1)} %reshape.140), calls=%async_computation.1 | async-start | bytes 1048576 | tf_op jit(solution)/shard_map/all_to_all | solution.py:45
  122.2 60.4 %collective-permute-start.2 = (bf16[2,4,64,2240]{3,2,1,0:T(8,128)(2,1)S(1)}, bf16[2,4,64,2240]{3,2,1,0:T(8,128)(2,1)}, u32[]{:S(2)}, u32[]{:S(2)}) collective-permute-start(bf16[2,4,64,2240]{3,2,1,0:T(8,128)(2,1)S(1)} %copy-done.1), channel_id=1, source_target_pairs={{0,16},{16,32},{32,48},{48,64},{64,80},{80,96},{96,112},{112,128},... | collective-permute-start | bytes 6881288 | tf_op jit(solution)/shard_map/ppermute | solution.py:31
  147.5 2.3 %copy-start.3 = (bf16[448,448]{1,0:T(8,128)(2,1)S(1)}, bf16[448,448]{1,0:T(8,128)(2,1)}, u32[]{:S(2)}) copy-start(bf16[448,448]{1,0:T(8,128)(2,1)} %select_n.44) | copy-start | bytes 1204228
  159.6 3.1 %copy-start.2 = (bf16[2,4,64,2240]{3,2,1,0:T(8,128)(2,1)S(1)}, bf16[2,4,64,2240]{3,2,1,0:T(8,128)(2,1)}, u32[]{:S(2)}) copy-start(bf16[2,4,64,2240]{3,2,1,0:T(8,128)(2,1)} %broadcast_maximum_fusion.1) | copy-start | bytes 6881284
  159.6 3.1 %copy-start.4 = (bf16[896,896]{1,0:T(8,128)(2,1)S(1)}, bf16[896,896]{1,0:T(8,128)(2,1)}, u32[]{:S(2)}) copy-start(bf16[896,896]{1,0:T(8,128)(2,1)} %select_n.42) | copy-start | bytes 4816900
  166.9 15.7 %copy-start.6 = (f32[2240]{0:T(1024)S(1)}, f32[2240]{0:T(1024)}, u32[]{:S(2)}) copy-start(f32[2240]{0:T(1024)} %param.10) | copy-start | bytes 26884
  166.9 19.2 %slice-start = ((s8[10616832]{0:T(1024)(128)(4,1)}), s8[2228224]{0:T(1024)(128)(4,1)S(1)}, s32[]{:S(2)}) async-start(s8[10616832]{0:T(1024)(128)(4,1)} %bitcast.45), calls=%async_computation.3 | async-start | bytes 4456448
  166.9 19.2 %slice-start.1 = ((s8[10616832]{0:T(1024)(128)(4,1)}), s8[4194304]{0:T(1024)(128)(4,1)S(1)}, s32[]{:S(2)}) async-start(s8[10616832]{0:T(1024)(128)(4,1)} %bitcast.45), calls=%async_computation.4 | async-start | bytes 8388608
  182.6 3.6 %slice-start.2 = ((s8[10616832]{0:T(1024)(128)(4,1)}), s8[4194304]{0:T(1024)(128)(4,1)S(1)}, s32[]{:S(2)}) async-start(s8[10616832]{0:T(1024)(128)(4,1)} %bitcast.45), calls=%async_computation.5 | async-start | bytes 8388608
Sparse Core Ops, SparseCore 0:
  35.3 104.9 all-gather.4

commit v6 on v4

--- a/solution.py
+++ b/solution.py
@@ -102,7 +102,9 @@
     query_heads, key_heads, value_heads, head_gain, spatial_kernel, temporal_kernel, out_weight
 ):
     frame_count, row_count, col_count, model_width = query_heads.shape
-    weight_cols = lax.all_gather(out_weight, "space", axis=0, tiled=True)
+    bands = lax.axis_size("space")
+    copies = jnp.broadcast_to(out_weight[None], (bands,) + out_weight.shape)
+    weight_cols = lax.all_to_all(copies, "space", 0, 0, tiled=True).reshape(-1, out_weight.shape[1])
     weight_stack = lax.all_gather(weight_cols, "tm", axis=0)
     token_count = frame_count * row_count * col_count
     queries = query_heads.reshape(token_count, HEADS, HEAD_DIM)
@@ -115,7 +117,9 @@
     spatial = spatial_conv(padded, spatial_kernel)
     earlier_frames = from_behind(spatial, "tm", 1)
     weight_flat = weight_stack.transpose(1, 0, 2).reshape(model_width, model_width)
-    state_low, spatial, weight_flat = prefix_state(local_state, spatial, weight_flat)
+    state_low, spatial, (weight_flat, earlier_frames) = prefix_state(
+        local_state, spatial, (weight_flat, earlier_frames)
+    )
     flat_queries = jnp.maximum(query_heads.reshape(token_count, model_width), 0)
     attended = banded_attention(flat_queries, state_low)
     normed = head_norm(attended).reshape(frame_count, row_count, col_count, model_width) * head_gain

time: 205 us -> 265 us (1.29); the launches traced: 201 us -> 264 us
  waiting for transfers between devices: 37.3 us -> 86.6 us
  blocking collectives: 25 us -> 41.3 us
  matrix products: 19.8 us -> 22.7 us
  other arithmetic: 23.4 us -> 20.5 us
    all_to_all x1, waiting for transfers between devices: 12.6 us -> 69.7 us  [prefix_state(): gathered = lax.all_to_all(outgoing, axes, 0, 0, tiled=True)]
    all_to_all x0 -> x1, blocking collectives: none -> 41.3 us  [per_device(): lax.all_to_all(copies, 'space', 0, 0, tiled=True)]
    all_gather x1 -> x0, blocking collectives: 25 us -> none  [per_device(): weight_cols = lax.all_gather(out_weight, 'space', axis=0, tiled=True)]
    all_to_all x1, waiting for transfers between devices: 21.5 us -> 16.9 us  [prefix_state(): mine = lax.all_to_all(flat, axes, 0, 0, tiled=True)]
    ppermute x1, waiting for transfers between devices: 3.2 us -> 0.01 us  [from_behind(): return lax.ppermute(block, axis, route)]
    dot_general x3, matrix products: 5.73 us -> 8.67 us  [banded_attention(): jnp.dot(queries[:, first * dim:(first + count) * dim], diagonal, preferre...]
    another operation x0 -> x1, local copies, waits for them, and re-layouts: none -> 2.77 us  [per_device(): weight_stack = lax.all_gather(weight_cols, 'tm', axis=0)]
    unnamed x26 -> x21, local copies, waits for them, and re-layouts: 8.79 us -> 6.68 us
  transfers between devices with their start and end apart: 6 -> 6, of which waited for: 3 -> 2; matrix products, arithmetic and copies ran while one was open for 40% -> 20% of each run, Pallas kernels for 0% -> 0%
where the time goes in v6:
time: 265 us; the launch traced here: 264 us
  waiting for transfers between devices  86.6 us (33%)
  local copies, waits for them, and re-layouts  53.1 us (20%)
  blocking collectives  41.3 us (16%)
  starting transfers between devices  26.3 us (10%)
  matrix products  22.7 us (9%)
  other arithmetic  20.5 us (8%)
  between operations  13.8 us (5%)
    all_to_all x1, waiting for transfers between devices, prefix_state(): gathered = lax.all_to_all(outgoing, axes, 0, 0, tiled=True)  69.7 us
    all_to_all x1, blocking collectives, per_device(): lax.all_to_all(copies, 'space', 0, 0, tiled=True)  41.3 us
    all_to_all x1, waiting for transfers between devices, prefix_state(): mine = lax.all_to_all(flat, axes, 0, 0, tiled=True)  16.9 us
    reshape x1, local copies, waits for them, and re-layouts, per_device(): weight_stack.transpose(1, 0, 2).reshape(model_width, model_width)  11.9 us
    all_to_all x1, starting transfers between devices, prefix_state(): mine = lax.all_to_all(flat, axes, 0, 0, tiled=True)  9.15 us
    dot_general x3, matrix products, banded_attention(): jnp.dot(queries[:, first * dim:(first + count) * dim], diagonal, preferre...  8.67 us
    convert_element_type x1, other arithmetic, spatial_conv(): return summed.astype(jnp.bfloat16)  6.85 us
    all_to_all x1, starting transfers between devices, prefix_state(): gathered = lax.all_to_all(outgoing, axes, 0, 0, tiled=True)  6.8 us
  transfers between devices with their start and end apart: 6, of which 2 were waited for; matrix products, arithmetic and copies ran while one was open for 20% of the time, Pallas kernels for 0%

profile of v6, /device:TPU:1, one launch (start us, length us, event | category | flops | bytes accessed | tf_op | source)
XLA Modules:
  0.0 264.3 jit_solution(2757121957937944576)
XLA Ops:
  7.6 41.3 %all_to_all.30 = bf16[16,140,140]{1,2,0:T(8,128)(2,1)S(1)} all-to-all(bf16[16,140,140]{1,2,0:T(8,128)(2,1)S(1)} %broadcast_in_dim.74), channel_id=1, replica_groups=mesh['tm'=16,'space'=16] {'space'}, dimensions={0} | all-to-all | bytes 1254400 | tf_op jit(solution)/shard_map/all_to_all | solution.py:107
  49.3 2.8 %all_gather_reshape.3 = bf16[1,2240,140]{1,2,0:T(8,128)(2,1)} reshape(bf16[16,140,140]{1,0,2:T(8,128)(2,1)S(1)} %copy.51) | data formatting | bytes 1254400 | tf_op jit(solution)/shard_map/all_gather;reshape | solution.py:108
  53.3 2.0 collective-permute-start.1
  55.3 3.6 %collective-permute-start = (bf16[2,1,64,2240]{3,2,1,0:T(8,128)(2,1)}, bf16[2,1,64,2240]{3,2,1,0:T(8,128)(2,1)}, u32[]{:S(2)}, u32[]{:S(2)}) collective-permute-start(bf16[2,1,64,2240]{3,2,1,0:T(8,128)(2,1)} %get-tuple-element.27), channel_id=1, source_target_pairs={{0,1},{1,2},{2,3},{3,4},{4,5},{5,6},{6,7},{7,8},{8,9},{9,10},{10,1... | collective-permute-start | bytes 1720328 | tf_op jit(solution)/shard_map/ppermute | solution.py:20
  60.6 4.3 %reshape.111 = bf16[512,20,112]{2,1,0:T(8,128)(2,1)} reshape(bf16[2,4,64,2240]{3,2,1,0:T(8,128)(2,1)S(1)} %copy-done) | data formatting | bytes 4587520 | tf_op jit(solution)/shard_map/reshape | solution.py:112
  64.9 6.6 %max.20 = bf16[512,20,112]{2,1,0:T(8,128)(2,1)} reshape(bf16[2,4,64,2240]{3,2,1,0:T(8,128)(2,1)} %broadcast_maximum_fusion) | data formatting | bytes 4587520 | tf_op jit(solution)/shard_map/max | solution.py:114
  71.4 4.1 %fusion.8 = f32[20,112,112]{2,1,0:T(8,128)S(1)} fusion(bf16[512,20,112]{2,1,0:T(8,128)(2,1)} %reshape.111, bf16[512,20,112]{2,1,0:T(8,128)(2,1)} %max.20), kind=kOutput, calls=%fused_computation.17 | convolution fusion | flops 256901120 | bytes 5591040 | tf_op jit(solution)/shard_map/thd,the->hde/dot_general | solution.py:113
  75.5 3.6 %all_to_all.26 = f32[256,1,980]{2,1,0:T(1,128)} reshape(f32[20,112,112]{2,1,0:T(8,128)S(1)} %fusion.8) | data formatting | bytes 2007040 | tf_op jit(solution)/shard_map/all_to_all | solution.py:40
  79.1 9.2 %all-to-all-start = ((f32[256,1,980]{2,1,0:T(1,128)}), f32[256,1,980]{2,1,0:T(1,128)S(1)}, u32[]{:S(2)}, u32[]{:S(2)}) async-start(f32[256,1,980]{2,1,0:T(1,128)} %all_to_all.26), calls=%async_computation | async-start | bytes 2097152 | tf_op jit(solution)/shard_map/all_to_all | solution.py:40
  90.0 2.4 fusion.7
  92.4 6.8 %add_convert_fusion.1 = bf16[2,4,64,2240]{3,2,1,0:T(8,128)(2,1)} fusion(bf16[2,4,64,2240]{3,2,1,0:T(8,128)(2,1)S(1)} %copy-done, bf16[2,6,66,2240]{3,2,1,0:T(8,128)(2,1)S(1)} %fusion.7, bf16[2,1,64,2240]{3,2,1,0:T(8,128)(2,1)} %collective-permute-done.1, bf16[2,1,64,2240]{3,2,1,0:T(8,128)(2,1)} %collective-permute-done, f32[2240]{0:T(1024)S(1)} %get-tuple-element.22, ...), kind=kLoop, calls=%fused_computation.10 | loop fusion | flops 33259520 | bytes 19577600 | tf_op jit(solution)/shard_map/convert_element_type | solution.py:61
  99.2 4.7 %collective-permute-start.2 = (bf16[2,4,64,2240]{3,2,1,0:T(8,128)(2,1)}, bf16[2,4,64,2240]{3,2,1,0:T(8,128)(2,1)}, u32[]{:S(2)}, u32[]{:S(2)}) collective-permute-start(bf16[2,4,64,2240]{3,2,1,0:T(8,128)(2,1)} %add_convert_fusion.1), channel_id=1, source_target_pairs={{0,16},{16,32},{32,48},{48,64},{64,80},{80,96},{96,112},{112,128},... | collective-permute-start | bytes 6881288 | tf_op jit(solution)/shard_map/ppermute | solution.py:31
  103.9 16.9 %all-to-all-done = f32[256,1,980]{2,1,0:T(1,128)S(1)} async-done(((f32[256,1,980]{2,1,0:T(1,128)}), f32[256,1,980]{2,1,0:T(1,128)S(1)}, u32[]{:S(2)}, u32[]{:S(2)}) %all-to-all-start) | async-done | bytes 1003552 | tf_op jit(solution)/shard_map/all_to_all | solution.py:40
  125.6 6.8 %all-to-all-start.1 = ((bf16[256,2,490]{2,1,0:T(2,128)(2,1)}), bf16[256,2,490]{2,1,0:T(2,128)(2,1)}, u32[]{:S(2)}, u32[]{:S(2)}) async-start(bf16[256,2,490]{2,1,0:T(2,128)(2,1)} %reshape.130), calls=%async_computation.1 | async-start | bytes 1048576 | tf_op jit(solution)/shard_map/all_to_all | solution.py:45
  134.1 69.7 %all-to-all-done.1 = bf16[256,2,490]{2,1,0:T(2,128)(2,1)} async-done(((bf16[256,2,490]{2,1,0:T(2,128)(2,1)}), bf16[256,2,490]{2,1,0:T(2,128)(2,1)}, u32[]{:S(2)}, u32[]{:S(2)}) %all-to-all-start.1) | async-done | bytes 501792 | tf_op jit(solution)/shard_map/all_to_all | solution.py:45
  203.8 4.0 %reshape.131 = bf16[256,1,980]{2,1,0:T(2,128)(2,1)S(1)} reshape(bf16[256,2,490]{2,1,0:T(2,128)(2,1)} %all-to-all-done.1) | data formatting | bytes 1003520
  208.9 11.9 %reshape.113 = bf16[2240,2240]{0,1:T(8,128)(2,1)} reshape(bf16[2240,16,140]{0,2,1:T(8,128)(2,1)} %bitcast.28) | data formatting | bytes 20070400 | tf_op jit(solution)/shard_map/reshape | solution.py:119
  224.6 4.1 %select_n.42 = bf16[896,896]{1,0:T(8,128)(2,1)} reshape(bf16[8,112,8,112]{3,2,1,0:T(8,128)(2,1)} %get-tuple-element.32) | data formatting | bytes 3211264 | tf_op jit(solution)/shard_map/jit(_where)/select_n | solution.py:72
  230.1 4.2 %fusion.27 = f32[512,896]{1,0:T(8,128)} fusion(bf16[896,896]{1,0:T(8,128)(2,1)} %select_n.42, bf16[512,2240]{1,0:T(8,128)(2,1)} %bitcast.33), kind=kOutput, calls=%fused_computation.36 | convolution fusion | flops 822083584 | bytes 4358144 | tf_op jit(solution)/shard_map/dot_general | solution.py:76
  234.3 2.4 select_n.40
  236.7 3.0 %fusion.29 = f32[512,896]{1,0:T(8,128)S(1)} fusion(bf16[896,896]{1,0:T(8,128)(2,1)} %select_n.40, bf16[512,2240]{1,0:T(8,128)(2,1)} %bitcast.34), kind=kOutput, calls=%fused_computation.38 | convolution fusion | flops 822083584 | bytes 4358144 | tf_op jit(solution)/shard_map/dot_general | solution.py:76
  243.9 4.8 %add_convert_fusion = bf16[2,4,64,2240]{3,2,1,0:T(8,128)(2,1)S(1)} fusion(bf16[2,4,64,2240]{3,2,1,0:T(8,128)(2,1)} %collective-permute-done.2, bf16[2,4,64,2240]{3,2,1,0:T(8,128)(2,1)} %add_convert_fusion.1, f32[2,4,64,2240]{3,2,1,0:T(8,128)S(1)} %bitcast.27, f32[2240]{0:T(1024)S(1)} %get-tuple-element.25, f32[2240]{0:T(1024)S(1)} %get-tuple-element.26, ...), kind=kLoop, calls=%fused_computation.9 | loop fusion | flops 13762560 | bytes 11504640 | tf_op jit(solution)/shard_map/convert_element_type | solution.py:132
  249.1 5.8 %convolution_convert_fusion = bf16[512,2240]{0,1:T(8,128)(2,1)S(1)} fusion(bf16[512,2240]{1,0:T(8,128)(2,1)S(1)} %bitcast.35, bf16[2240,2240]{0,1:T(8,128)(2,1)S(1)} %bitcast.30), kind=kOutput, calls=%fused_computation.14 | convolution fusion | flops 5139169280 | bytes 14622720 | tf_op jit(solution)/shard_map/dot_general | solution.py:133
  255.0 2.5 copy.56
  (57 shorter events, 23.2 us)
Async XLA Ops:
  6.5 202.4 %all-gather.2.cloned.1.call-start = ((), (), s32[]{:S(2)}) async-start(), calls=%async_computation.3 | async-start | bytes 11280384 | tf_op jit(solution)/shard_map/all_gather | solution.py:108
  7.6 44.5 %copy-start = (bf16[2,4,64,2240]{3,2,1,0:T(8,128)(2,1)S(1)}, bf16[2,4,64,2240]{3,2,1,0:T(8,128)(2,1)}, u32[]{:S(2)}) copy-start(bf16[2,4,64,2240]{3,2,1,0:T(8,128)(2,1)} %param.9) | copy-start | bytes 6881284
  52.2 6.8 %copy-start.1 = (bf16[2,4,64,2240]{3,2,1,0:T(8,128)(2,1)S(1)}, bf16[2,4,64,2240]{3,2,1,0:T(8,128)(2,1)}, u32[]{:S(2)}) copy-start(bf16[2,4,64,2240]{3,2,1,0:T(8,128)(2,1)} %param.8) | copy-start | bytes 6881284
  53.3 36.7 %collective-permute-start.1 = (bf16[2,1,64,2240]{3,2,1,0:T(8,128)(2,1)}, bf16[2,1,64,2240]{3,2,1,0:T(8,128)(2,1)}, u32[]{:S(2)}, u32[]{:S(2)}) collective-permute-start(bf16[2,1,64,2240]{3,2,1,0:T(8,128)(2,1)} %get-tuple-element.28), channel_id=1, source_target_pairs={{1,0},{2,1},{3,2},{4,3},{5,4},{6,5},{7,6},{8,7},{9,8},{10,9},{11,1... | collective-permute-start | bytes 1720328 | tf_op jit(solution)/shard_map/ppermute | solution.py:23
  55.3 34.7 %collective-permute-start = (bf16[2,1,64,2240]{3,2,1,0:T(8,128)(2,1)}, bf16[2,1,64,2240]{3,2,1,0:T(8,128)(2,1)}, u32[]{:S(2)}, u32[]{:S(2)}) collective-permute-start(bf16[2,1,64,2240]{3,2,1,0:T(8,128)(2,1)} %get-tuple-element.27), channel_id=1, source_target_pairs={{0,1},{1,2},{2,3},{3,4},{4,5},{5,6},{6,7},{7,8},{8,9},{9,10},{10,1... | collective-permute-start | bytes 1720328 | tf_op jit(solution)/shard_map/ppermute | solution.py:20
  79.1 41.7 %all-to-all-start = ((f32[256,1,980]{2,1,0:T(1,128)}), f32[256,1,980]{2,1,0:T(1,128)S(1)}, u32[]{:S(2)}, u32[]{:S(2)}) async-start(f32[256,1,980]{2,1,0:T(1,128)} %all_to_all.26), calls=%async_computation | async-start | bytes 2097152 | tf_op jit(solution)/shard_map/all_to_all | solution.py:40
  99.2 121.6 %collective-permute-start.2 = (bf16[2,4,64,2240]{3,2,1,0:T(8,128)(2,1)}, bf16[2,4,64,2240]{3,2,1,0:T(8,128)(2,1)}, u32[]{:S(2)}, u32[]{:S(2)}) collective-permute-start(bf16[2,4,64,2240]{3,2,1,0:T(8,128)(2,1)} %add_convert_fusion.1), channel_id=1, source_target_pairs={{0,16},{16,32},{32,48},{48,64},{64,80},{80,96},{96,112},{112,128},... | collective-permute-start | bytes 6881288 | tf_op jit(solution)/shard_map/ppermute | solution.py:31
  122.0 10.4 %copy-start.4 = (f32[3,2240]{1,0:T(4,128)S(1)}, f32[3,2240]{1,0:T(4,128)}, u32[]{:S(2)}) copy-start(f32[3,2240]{1,0:T(4,128)} %param.12) | copy-start | bytes 80644
  122.3 10.2 %copy-start.2 = (bf16[2,4,64,2240]{3,2,1,0:T(8,128)(2,1)S(1)}, bf16[2,4,64,2240]{3,2,1,0:T(8,128)(2,1)}, u32[]{:S(2)}) copy-start(bf16[2,4,64,2240]{3,2,1,0:T(8,128)(2,1)} %param.7) | copy-start | bytes 6881284
  125.6 78.2 %all-to-all-start.1 = ((bf16[256,2,490]{2,1,0:T(2,128)(2,1)}), bf16[256,2,490]{2,1,0:T(2,128)(2,1)}, u32[]{:S(2)}, u32[]{:S(2)}) async-start(bf16[256,2,490]{2,1,0:T(2,128)(2,1)} %reshape.130), calls=%async_computation.1 | async-start | bytes 1048576 | tf_op jit(solution)/shard_map/all_to_all | solution.py:45
  236.7 3.0 %copy-start.3 = (f32[512,896]{1,0:T(8,128)S(1)}, f32[512,896]{1,0:T(8,128)}, u32[]{:S(2)}) copy-start(f32[512,896]{1,0:T(8,128)} %fusion.27) | copy-start | bytes 5505028
  242.8 1.1 copy-start.5
  242.8 6.0 %slice-start = ((s8[10321920]{0:T(1024)(128)(4,1)}), s8[4194304]{0:T(1024)(128)(4,1)S(1)}, s32[]{:S(2)}) async-start(s8[10321920]{0:T(1024)(128)(4,1)} %bitcast.29), calls=%async_computation.4 | async-start | bytes 8388608
  242.8 6.0 %slice-start.1 = ((s8[10321920]{0:T(1024)(128)(4,1)}), s8[1933312]{0:T(1024)(128)(4,1)S(1)}, s32[]{:S(2)}) async-start(s8[10321920]{0:T(1024)(128)(4,1)} %bitcast.29), calls=%async_computation.5 | async-start | bytes 3866624
  243.9 5.2 %slice-start.2 = ((s8[10321920]{0:T(1024)(128)(4,1)}), s8[4194304]{0:T(1024)(128)(4,1)S(1)}, s32[]{:S(2)}) async-start(s8[10321920]{0:T(1024)(128)(4,1)} %bitcast.29), calls=%async_computation.6 | async-start | bytes 8388608
Sparse Core Ops, SparseCore 0:
  52.3 132.3 all-gather.1

commit v7 on v4

--- a/solution.py
+++ b/solution.py
@@ -68,10 +68,9 @@
     for first in range(0, heads, group):
         count = min(group, heads - first)
         blocks = state_low[first : first + count]
-        eye = jnp.eye(count, dtype=bool)
-        diagonal = jnp.where(
-            eye[:, None, :, None], blocks[:, :, None, :], jnp.zeros((), blocks.dtype)
-        ).reshape(count * dim, count * dim)
+        diagonal = jnp.zeros((count * dim, count * dim), blocks.dtype)
+        for head in range(count):
+            diagonal = lax.dynamic_update_slice(diagonal, blocks[head], (head * dim, head * dim))
         pieces.append(
             jnp.dot(
                 queries[:, first * dim : (first + count) * dim],

time: 205 us -> 240 us (1.17)
  local copies, waits for them, and re-layouts: 55.4 us -> 98.1 us
  waiting for transfers between devices: 37.3 us -> 33 us
  other arithmetic: 23.4 us -> 19.9 us
    dynamic_update_slice x0 -> x20, local copies, waits for them, and re-layouts: none -> 49 us  [banded_attention(): lax.dynamic_update_slice(diagonal, blocks[head], (head * dim, head * dim))]
    select_n x3 -> x0, local copies, waits for them, and re-layouts: 9.26 us -> none  [banded_attention(): jnp.where(eye[:, None, :, None], blocks[:, :, None, :], jnp.zeros((), blo...]
    ppermute x1, waiting for transfers between devices: 3.2 us -> 0.01 us  [from_behind(): return lax.ppermute(block, axis, route)]
    select_n x2 -> x0, other arithmetic: 2.62 us -> none  [banded_attention(): jnp.where(eye[:, None, :, None], blocks[:, :, None, :], jnp.zeros((), blo...]
    unnamed x26 -> x40, local copies, waits for them, and re-layouts: 8.79 us -> 9.75 us
  transfers between devices with their start and end apart: 6 -> 6, of which waited for: 3 -> 2; matrix products, arithmetic and copies ran while one was open for 40% -> 50% of each run, Pallas kernels for 0% -> 0%
where the time goes in v7:
time: 240 us; the launch traced here: 236 us
  local copies, waits for them, and re-layouts  98.1 us (41%)
  waiting for transfers between devices  33 us (14%)
  starting transfers between devices  26.7 us (11%)
  blocking collectives  25 us (10%)
  other arithmetic  19.9 us (8%)
  matrix products  19.9 us (8%)
  between operations  13.8 us (6%)
    dynamic_update_slice x20, local copies, waits for them, and re-layouts, banded_attention(): lax.dynamic_update_slice(diagonal, blocks[head], (head * dim, head * dim))  49 us
    all_gather x1, blocking collectives, per_device(): weight_cols = lax.all_gather(out_weight, 'space', axis=0, tiled=True)  25 us
    all_to_all x1, waiting for transfers between devices, prefix_state(): mine = lax.all_to_all(flat, axes, 0, 0, tiled=True)  21.6 us
    reshape x1, local copies, waits for them, and re-layouts, per_device(): weight_stack.transpose(1, 0, 2).reshape(model_width, model_width)  11.9 us
    all_to_all x1, waiting for transfers between devices, prefix_state(): gathered = lax.all_to_all(outgoing, axes, 0, 0, tiled=True)  11.4 us
    all_to_all x1, starting transfers between devices, prefix_state(): mine = lax.all_to_all(flat, axes, 0, 0, tiled=True)  11.1 us
    unnamed x40, local copies, waits for them, and re-layouts  9.75 us
    all_to_all x1, starting transfers between devices, prefix_state(): gathered = lax.all_to_all(outgoing, axes, 0, 0, tiled=True)  7.12 us
  transfers between devices with their start and end apart: 6, of which 2 were waited for; matrix products, arithmetic and copies ran while one was open for 50% of the time, Pallas kernels for 0%

profile of v7, /device:TPU:1, one launch (start us, length us, event | category | flops | bytes accessed | tf_op | source)
XLA Modules:
  0.0 236.5 jit_solution(14402592967247731377)
XLA Ops:
  6.5 25.0 %all-gather.1 = bf16[16,140,140]{2,1,0:T(8,128)(2,1)S(1)} all-gather(bf16[1,140,140]{2,1,0:T(8,128)(2,1)} %bitcast.73), channel_id=1, replica_groups=mesh['tm'=16,'space'=16] {'space'}, dimensions={0}, use_global_device_ids=true | all-gather | bytes 666400 | tf_op jit(solution)/shard_map/all_gather | solution.py:104
  38.2 3.2 %collective-permute-start.1 = (bf16[2,1,64,2240]{3,2,1,0:T(8,128)(2,1)}, bf16[2,1,64,2240]{3,2,1,0:T(8,128)(2,1)}, u32[]{:S(2)}, u32[]{:S(2)}) collective-permute-start(bf16[2,1,64,2240]{3,2,1,0:T(8,128)(2,1)} %get-tuple-element.26), channel_id=1, source_target_pairs={{1,0},{2,1},{3,2},{4,3},{5,4},{6,5},{7,6},{8,7},{9,8},{10,9},{11,1... | collective-permute-start | bytes 1720328 | tf_op jit(solution)/shard_map/ppermute | solution.py:23
  43.0 4.3 %reshape.78 = bf16[512,20,112]{2,1,0:T(8,128)(2,1)} reshape(bf16[2,4,64,2240]{3,2,1,0:T(8,128)(2,1)S(1)} %copy-done) | data formatting | bytes 4587520 | tf_op jit(solution)/shard_map/reshape | solution.py:109
  47.3 6.5 %max.20 = bf16[512,20,112]{2,1,0:T(8,128)(2,1)} reshape(bf16[2,4,64,2240]{3,2,1,0:T(8,128)(2,1)} %broadcast_maximum_fusion) | data formatting | bytes 4587520 | tf_op jit(solution)/shard_map/max | solution.py:111
  53.9 4.1 %fusion.8 = f32[20,112,112]{2,1,0:T(8,128)S(1)} fusion(bf16[512,20,112]{2,1,0:T(8,128)(2,1)} %reshape.78, bf16[512,20,112]{2,1,0:T(8,128)(2,1)} %max.20), kind=kOutput, calls=%fused_computation.17 | convolution fusion | flops 256901120 | bytes 5591040 | tf_op jit(solution)/shard_map/thd,the->hde/dot_general | solution.py:110
  58.0 3.6 %all_to_all.22 = f32[256,1,980]{2,1,0:T(1,128)} reshape(f32[20,112,112]{2,1,0:T(8,128)S(1)} %fusion.8) | data formatting | bytes 2007040 | tf_op jit(solution)/shard_map/all_to_all | solution.py:40
  61.6 11.1 %all-to-all-start = ((f32[256,1,980]{2,1,0:T(1,128)}), f32[256,1,980]{2,1,0:T(1,128)S(1)}, u32[]{:S(2)}, u32[]{:S(2)}) async-start(f32[256,1,980]{2,1,0:T(1,128)} %all_to_all.22), calls=%async_computation | async-start | bytes 2097152 | tf_op jit(solution)/shard_map/all_to_all | solution.py:40
  76.8 6.8 %add_convert_fusion.1 = bf16[2,4,64,2240]{3,2,1,0:T(8,128)(2,1)} fusion(bf16[2,4,64,2240]{3,2,1,0:T(8,128)(2,1)S(1)} %copy-done, bf16[2,6,66,2240]{3,2,1,0:T(8,128)(2,1)S(1)} %fusion.7, bf16[2,1,64,2240]{3,2,1,0:T(8,128)(2,1)} %collective-permute-done.1, bf16[2,1,64,2240]{3,2,1,0:T(8,128)(2,1)} %collective-permute-done, f32[2240]{0:T(1024)S(1)} %get-tuple-element.20, ...), kind=kLoop, calls=%fused_computation.10 | loop fusion | flops 33259520 | bytes 19577600 | tf_op jit(solution)/shard_map/convert_element_type | solution.py:61
  83.6 21.6 %all-to-all-done = f32[256,1,980]{2,1,0:T(1,128)S(1)} async-done(((f32[256,1,980]{2,1,0:T(1,128)}), f32[256,1,980]{2,1,0:T(1,128)S(1)}, u32[]{:S(2)}, u32[]{:S(2)}) %all-to-all-start) | async-done | bytes 1003552 | tf_op jit(solution)/shard_map/all_to_all | solution.py:40
  110.0 7.1 %all-to-all-start.1 = ((bf16[256,2,490]{2,1,0:T(2,128)(2,1)}), bf16[256,2,490]{2,1,0:T(2,128)(2,1)}, u32[]{:S(2)}, u32[]{:S(2)}) async-start(bf16[256,2,490]{2,1,0:T(2,128)(2,1)} %reshape.105), calls=%async_computation.1 | async-start | bytes 1048576 | tf_op jit(solution)/shard_map/all_to_all | solution.py:45
  118.4 3.3 %broadcast_maximum_fusion.1 = bf16[2,4,64,2240]{3,2,1,0:T(8,128)(2,1)} fusion(bf16[2,4,64,2240]{3,2,1,0:T(8,128)(2,1)} %param.7), kind=kLoop, calls=%fused_computation.26 | loop fusion | flops 1146880 | bytes 4587520 | tf_op jit(solution)/shard_map/max | solution.py:118
  121.7 3.3 %collective-permute-start.2 = (bf16[2,4,64,2240]{3,2,1,0:T(8,128)(2,1)S(1)}, bf16[2,4,64,2240]{3,2,1,0:T(8,128)(2,1)}, u32[]{:S(2)}, u32[]{:S(2)}) collective-permute-start(bf16[2,4,64,2240]{3,2,1,0:T(8,128)(2,1)S(1)} %copy-done.1), channel_id=1, source_target_pairs={{0,16},{16,32},{32,48},{48,64},{64,80},{80,96},{96,112},{112,128},... | collective-permute-start | bytes 6881288 | tf_op jit(solution)/shard_map/ppermute | solution.py:31
  125.0 11.4 %all-to-all-done.1 = bf16[256,2,490]{2,1,0:T(2,128)(2,1)} async-done(((bf16[256,2,490]{2,1,0:T(2,128)(2,1)}), bf16[256,2,490]{2,1,0:T(2,128)(2,1)}, u32[]{:S(2)}, u32[]{:S(2)}) %all-to-all-start.1) | async-done | bytes 501792 | tf_op jit(solution)/shard_map/all_to_all | solution.py:45
  136.4 4.0 %reshape.106 = bf16[256,1,980]{2,1,0:T(2,128)(2,1)S(1)} reshape(bf16[256,2,490]{2,1,0:T(2,128)(2,1)} %all-to-all-done.1) | data formatting | bytes 1003520
  142.3 11.9 %reshape.80 = bf16[2240,2240]{0,1:T(8,128)(2,1)} reshape(bf16[2240,16,140]{0,2,1:T(8,128)(2,1)} %bitcast.63) | data formatting | bytes 20070400 | tf_op jit(solution)/shard_map/reshape | solution.py:116
  168.5 3.0 %dynamic_update_slice.61 = bf16[896,896]{1,0:T(8,128)(2,1)} dynamic-update-slice(bf16[896,896]{1,0:T(8,128)(2,1)} %dynamic_update_slice.60, bf16[112,112]{1,0:T(8,128)(2,1)} %get-tuple-element.45, s32[]{:T(128)} %constant.8.clone.1, s32[]{:T(128)} %constant.8.clone.1) | dynamic-update-slice | bytes 50180 | tf_op jit(solution)/shard_map/dynamic_update_slice | solution.py:73
  171.6 3.0 %dynamic_update_slice.62 = bf16[896,896]{1,0:T(8,128)(2,1)} dynamic-update-slice(bf16[896,896]{1,0:T(8,128)(2,1)} %dynamic_update_slice.61, bf16[112,112]{1,0:T(8,128)(2,1)} %get-tuple-element.44, s32[]{:T(128)} %constant.17.clone.1, s32[]{:T(128)} %constant.17.clone.1) | dynamic-update-slice | bytes 50180 | tf_op jit(solution)/shard_map/dynamic_update_slice | solution.py:73
  177.6 3.0 %dynamic_update_slice.69 = bf16[896,896]{1,0:T(8,128)(2,1)} dynamic-update-slice(bf16[896,896]{1,0:T(8,128)(2,1)} %dynamic_update_slice.68, bf16[112,112]{1,0:T(8,128)(2,1)} %get-tuple-element.38, s32[]{:T(128)} %constant.8.clone.1, s32[]{:T(128)} %constant.8.clone.1) | dynamic-update-slice | bytes 50180 | tf_op jit(solution)/shard_map/dynamic_update_slice | solution.py:73
  180.6 3.0 %dynamic_update_slice.70 = bf16[896,896]{1,0:T(8,128)(2,1)} dynamic-update-slice(bf16[896,896]{1,0:T(8,128)(2,1)} %dynamic_update_slice.69, bf16[112,112]{1,0:T(8,128)(2,1)} %get-tuple-element.37, s32[]{:T(128)} %constant.17.clone.1, s32[]{:T(128)} %constant.17.clone.1) | dynamic-update-slice | bytes 50180 | tf_op jit(solution)/shard_map/dynamic_update_slice | solution.py:73
  183.6 3.0 %dynamic_update_slice.71 = bf16[896,896]{1,0:T(8,128)(2,1)} dynamic-update-slice(bf16[896,896]{1,0:T(8,128)(2,1)} %dynamic_update_slice.70, bf16[112,112]{1,0:T(8,128)(2,1)} %get-tuple-element.36, s32[]{:T(128)} %constant.18.clone.1, s32[]{:T(128)} %constant.18.clone.1) | dynamic-update-slice | bytes 50180 | tf_op jit(solution)/shard_map/dynamic_update_slice | solution.py:73
  189.7 3.0 %dynamic_update_slice.72 = bf16[896,896]{1,0:T(8,128)(2,1)} dynamic-update-slice(bf16[896,896]{1,0:T(8,128)(2,1)} %dynamic_update_slice.71, bf16[112,112]{1,0:T(8,128)(2,1)} %get-tuple-element.35, s32[]{:T(128)} %constant.9.clone.1, s32[]{:T(128)} %constant.9.clone.1) | dynamic-update-slice | bytes 50180 | tf_op jit(solution)/shard_map/dynamic_update_slice | solution.py:73
  208.6 3.1 %fusion.29 = f32[512,896]{1,0:T(8,128)S(1)} fusion(bf16[896,896]{1,0:T(8,128)(2,1)} %dynamic_update_slice.67, bf16[512,2240]{1,0:T(8,128)(2,1)} %bitcast.68), kind=kOutput, calls=%fused_computation.36 | convolution fusion | flops 822083584 | bytes 4358144 | tf_op jit(solution)/shard_map/dot_general | solution.py:75
  217.2 4.0 %add_convert_fusion = bf16[2,4,64,2240]{3,2,1,0:T(8,128)(2,1)S(1)} fusion(bf16[2,4,64,2240]{3,2,1,0:T(8,128)(2,1)} %collective-permute-done.2, bf16[2,4,64,2240]{3,2,1,0:T(8,128)(2,1)S(1)} %copy-done.1, f32[2,4,64,2240]{3,2,1,0:T(8,128)S(1)} %bitcast.62, f32[2240]{0:T(1024)S(1)} %copy-done.11, f32[2240]{0:T(1024)S(1)} %copy-done.12, f32[2240]{0:T(1024)S(1)} %copy-done.10, ...), kind=kLoop, calls=%fused_computation.9 | loop fusion | flops 13762560 | bytes 11504640 | tf_op jit(solution)/shard_map/convert_element_type | solution.py:127
  221.4 5.8 %convolution_convert_fusion = bf16[512,2240]{0,1:T(8,128)(2,1)S(1)} fusion(bf16[512,2240]{1,0:T(8,128)(2,1)S(1)} %bitcast.70, bf16[2240,2240]{0,1:T(8,128)(2,1)S(1)} %bitcast.65), kind=kOutput, calls=%fused_computation.14 | convolution fusion | flops 5139169280 | bytes 14622720 | tf_op jit(solution)/shard_map/dot_general | solution.py:128
  (86 shorter events, 64.5 us)
Async XLA Ops:
  6.5 28.5 %copy-start = (bf16[2,4,64,2240]{3,2,1,0:T(8,128)(2,1)S(1)}, bf16[2,4,64,2240]{3,2,1,0:T(8,128)(2,1)}, u32[]{:S(2)}) copy-start(bf16[2,4,64,2240]{3,2,1,0:T(8,128)(2,1)} %param.9) | copy-start | bytes 6881284
  6.5 135.8 %all-gather.5.cloned.1.call-start = ((), (), s32[]{:S(2)}) async-start(), calls=%async_computation.2 | async-start | bytes 11280384 | tf_op jit(solution)/shard_map/all_gather | solution.py:105
  35.1 6.4 %copy-start.3 = (bf16[2,4,64,2240]{3,2,1,0:T(8,128)(2,1)S(1)}, bf16[2,4,64,2240]{3,2,1,0:T(8,128)(2,1)}, u32[]{:S(2)}) copy-start(bf16[2,4,64,2240]{3,2,1,0:T(8,128)(2,1)} %param.8) | copy-start | bytes 6881284
  36.2 38.2 %collective-permute-start = (bf16[2,1,64,2240]{3,2,1,0:T(8,128)(2,1)}, bf16[2,1,64,2240]{3,2,1,0:T(8,128)(2,1)}, u32[]{:S(2)}, u32[]{:S(2)}) collective-permute-start(bf16[2,1,64,2240]{3,2,1,0:T(8,128)(2,1)} %get-tuple-element.25), channel_id=1, source_target_pairs={{0,1},{1,2},{2,3},{3,4},{4,5},{5,6},{6,7},{7,8},{8,9},{9,10},{10,1... | collective-permute-start | bytes 1720328 | tf_op jit(solution)/shard_map/ppermute | solution.py:20
  38.2 36.2 %collective-permute-start.1 = (bf16[2,1,64,2240]{3,2,1,0:T(8,128)(2,1)}, bf16[2,1,64,2240]{3,2,1,0:T(8,128)(2,1)}, u32[]{:S(2)}, u32[]{:S(2)}) collective-permute-start(bf16[2,1,64,2240]{3,2,1,0:T(8,128)(2,1)} %get-tuple-element.26), channel_id=1, source_target_pairs={{1,0},{2,1},{3,2},{4,3},{5,4},{6,5},{7,6},{8,7},{9,8},{10,9},{11,1... | collective-permute-start | bytes 1720328 | tf_op jit(solution)/shard_map/ppermute | solution.py:23
  61.6 43.6 %all-to-all-start = ((f32[256,1,980]{2,1,0:T(1,128)}), f32[256,1,980]{2,1,0:T(1,128)S(1)}, u32[]{:S(2)}, u32[]{:S(2)}) async-start(f32[256,1,980]{2,1,0:T(1,128)} %all_to_all.22), calls=%async_computation | async-start | bytes 2097152 | tf_op jit(solution)/shard_map/all_to_all | solution.py:40
  106.4 11.4 %copy-start.13 = (f32[3,2240]{1,0:T(4,128)S(1)}, f32[3,2240]{1,0:T(4,128)}, u32[]{:S(2)}) copy-start(f32[3,2240]{1,0:T(4,128)} %param.12) | copy-start | bytes 80644
  110.0 11.7 %copy-start.1 = (bf16[2,4,64,2240]{3,2,1,0:T(8,128)(2,1)S(1)}, bf16[2,4,64,2240]{3,2,1,0:T(8,128)(2,1)}, u32[]{:S(2)}) copy-start(bf16[2,4,64,2240]{3,2,1,0:T(8,128)(2,1)} %add_convert_fusion.1) | copy-start | bytes 6881284
  110.0 26.3 %all-to-all-start.1 = ((bf16[256,2,490]{2,1,0:T(2,128)(2,1)}), bf16[256,2,490]{2,1,0:T(2,128)(2,1)}, u32[]{:S(2)}, u32[]{:S(2)}) async-start(bf16[256,2,490]{2,1,0:T(2,128)(2,1)} %reshape.105), calls=%async_computation.1 | async-start | bytes 1048576 | tf_op jit(solution)/shard_map/all_to_all | solution.py:45
  121.7 95.4 %collective-permute-start.2 = (bf16[2,4,64,2240]{3,2,1,0:T(8,128)(2,1)S(1)}, bf16[2,4,64,2240]{3,2,1,0:T(8,128)(2,1)}, u32[]{:S(2)}, u32[]{:S(2)}) collective-permute-start(bf16[2,4,64,2240]{3,2,1,0:T(8,128)(2,1)S(1)} %copy-done.1), channel_id=1, source_target_pairs={{0,16},{16,32},{32,48},{48,64},{64,80},{80,96},{96,112},{112,128},... | collective-permute-start | bytes 6881288 | tf_op jit(solution)/shard_map/ppermute | solution.py:31
  142.3 11.9 %copy-start.5 = (bf16[256,1,980]{0,2,1:T(8,128)(2,1)S(1)}, bf16[256,1,980]{0,2,1:T(8,128)(2,1)}, u32[]{:S(2)}) copy-start(bf16[256,1,980]{0,2,1:T(8,128)(2,1)} %copy.47) | copy-start | bytes 1505284
  155.7 7.2 %copy-start.4 = (bf16[20,112,112]{2,1,0:T(8,128)(2,1)}, bf16[20,112,112]{2,1,0:T(8,128)(2,1)S(1)}, u32[]{:S(2)}) copy-start(bf16[20,112,112]{2,1,0:T(8,128)(2,1)S(1)} %reshape.81) | copy-start | bytes 1505284
  162.8 0.8 copy-start.6
  163.6 3.7 %copy-start.8 = (bf16[112,112]{1,0:T(8,128)(2,1)S(1)}, bf16[112,112]{1,0:T(8,128)(2,1)}, u32[]{:S(2)}) copy-start(bf16[112,112]{1,0:T(8,128)(2,1)} %get-tuple-element.39) | copy-start | bytes 75268
  208.6 3.1 %copy-start.2 = (bf16[2,4,64,2240]{3,2,1,0:T(8,128)(2,1)S(1)}, bf16[2,4,64,2240]{3,2,1,0:T(8,128)(2,1)}, u32[]{:S(2)}) copy-start(bf16[2,4,64,2240]{3,2,1,0:T(8,128)(2,1)} %broadcast_maximum_fusion.1) | copy-start | bytes 6881284
  208.6 3.1 %copy-start.7 = (bf16[896,896]{1,0:T(8,128)(2,1)S(1)}, bf16[896,896]{1,0:T(8,128)(2,1)}, u32[]{:S(2)}) copy-start(bf16[896,896]{1,0:T(8,128)(2,1)} %dynamic_update_slice.75) | copy-start | bytes 4816900
  211.7 1.2 copy-start.9
  216.0 1.2 copy-start.10
  216.0 1.2 copy-start.11
  216.0 1.2 copy-start.12
  216.0 1.2 copy-start.14
  216.0 5.2 %slice-start = ((s8[10321920]{0:T(1024)(128)(4,1)}), s8[4194304]{0:T(1024)(128)(4,1)S(1)}, s32[]{:S(2)}) async-start(s8[10321920]{0:T(1024)(128)(4,1)} %bitcast.64), calls=%async_computation.3 | async-start | bytes 8388608
  216.0 5.2 %slice-start.1 = ((s8[10321920]{0:T(1024)(128)(4,1)}), s8[1933312]{0:T(1024)(128)(4,1)S(1)}, s32[]{:S(2)}) async-start(s8[10321920]{0:T(1024)(128)(4,1)} %bitcast.64), calls=%async_computation.4 | async-start | bytes 3866624
  217.2 4.2 %slice-start.2 = ((s8[10321920]{0:T(1024)(128)(4,1)}), s8[4194304]{0:T(1024)(128)(4,1)S(1)}, s32[]{:S(2)}) async-start(s8[10321920]{0:T(1024)(128)(4,1)} %bitcast.64), calls=%async_computation.5 | async-start | bytes 8388608
Sparse Core Ops, SparseCore 0:
  35.2 105.4 all-gather.4

commit v8 on v5

--- a/solution.py
+++ b/solution.py
@@ -117,7 +117,9 @@
     earlier_frames = from_behind(spatial, "tm", 1)
     blocks, _, padded_width = weight_stack.shape
     weight_flat = weight_stack.transpose(1, 0, 2).reshape(model_width, blocks * padded_width)
-    state_low, spatial, weight_flat = prefix_state(local_state, spatial, weight_flat)
+    state_low, spatial, (weight_flat, earlier_frames) = prefix_state(
+        local_state, spatial, (weight_flat, earlier_frames)
+    )
     flat_queries = jnp.maximum(query_heads.reshape(token_count, model_width), 0)
     attended = banded_attention(flat_queries, state_low)
     normed = head_norm(attended).reshape(frame_count, row_count, col_count, model_width) * head_gain

time: 215 us -> 246 us (1.14); the launches traced: 211 us -> 245 us
  waiting for transfers between devices: 48.5 us -> 86.6 us
  local copies, waits for them, and re-layouts: 54 us -> 50.4 us
  other arithmetic: 23.3 us -> 20.3 us
  matrix products: 20.2 us -> 22.9 us
    all_to_all x1, waiting for transfers between devices: 12.4 us -> 69.9 us  [prefix_state(): gathered = lax.all_to_all(outgoing, axes, 0, 0, tiled=True)]
    ppermute x1, waiting for transfers between devices: 14.6 us -> 0.01 us  [from_behind(): return lax.ppermute(block, axis, route)]
    all_to_all x1, waiting for transfers between devices: 21.5 us -> 16.7 us  [prefix_state(): mine = lax.all_to_all(flat, axes, 0, 0, tiled=True)]
    dot_general x3, matrix products: 5.73 us -> 8.66 us  [banded_attention(): jnp.dot(queries[:, first * dim:(first + count) * dim], diagonal, preferre...]
    unnamed x25 -> x23, local copies, waits for them, and re-layouts: 9.05 us -> 9.82 us
  transfers between devices with their start and end apart: 6 -> 6, of which waited for: 3 -> 2; matrix products, arithmetic and copies ran while one was open for 33% -> 16% of each run, Pallas kernels for 0% -> 0%
where the time goes in v8:
time: 246 us; the launch traced here: 245 us
  waiting for transfers between devices  86.6 us (35%)
  local copies, waits for them, and re-layouts  50.4 us (20%)
  starting transfers between devices  26.6 us (11%)
  blocking collectives  24.9 us (10%)
  matrix products  22.9 us (9%)
  other arithmetic  20.3 us (8%)
  between operations  13.8 us (6%)
    all_to_all x1, waiting for transfers between devices, prefix_state(): gathered = lax.all_to_all(outgoing, axes, 0, 0, tiled=True)  69.9 us
    all_gather x1, blocking collectives, per_device(): weight_cols = lax.all_gather(out_weight, 'space', axis=0, tiled=True)  24.9 us
    all_to_all x1, waiting for transfers between devices, prefix_state(): mine = lax.all_to_all(flat, axes, 0, 0, tiled=True)  16.7 us
    reshape x2, local copies, waits for them, and re-layouts, per_device(): projected.astype(jnp.bfloat16)  11.6 us
    unnamed x23, local copies, waits for them, and re-layouts  9.82 us
    all_to_all x1, starting transfers between devices, prefix_state(): mine = lax.all_to_all(flat, axes, 0, 0, tiled=True)  9.45 us
    dot_general x3, matrix products, banded_attention(): jnp.dot(queries[:, first * dim:(first + count) * dim], diagonal, preferre...  8.66 us
    convert_element_type x1, other arithmetic, spatial_conv(): return summed.astype(jnp.bfloat16)  6.85 us
  transfers between devices with their start and end apart: 6, of which 2 were waited for; matrix products, arithmetic and copies ran while one was open for 16% of the time, Pallas kernels for 0%

profile of v8, /device:TPU:1, one launch (start us, length us, event | category | flops | bytes accessed | tf_op | source)
XLA Modules:
  0.0 245.4 jit_solution(1383079277800385607)
XLA Ops:
  6.5 24.9 %all-gather.1 = bf16[16,140,140]{2,1,0:T(8,128)(2,1)S(1)} all-gather(bf16[1,140,140]{2,1,0:T(8,128)(2,1)} %bitcast.44), channel_id=1, replica_groups=mesh['tm'=16,'space'=16] {'space'}, dimensions={0}, use_global_device_ids=true | all-gather | bytes 666400 | tf_op jit(solution)/shard_map/all_gather | solution.py:105
  36.4 2.2 collective-permute-start.1
  38.6 3.5 %collective-permute-start = (bf16[2,1,64,2240]{3,2,1,0:T(8,128)(2,1)}, bf16[2,1,64,2240]{3,2,1,0:T(8,128)(2,1)}, u32[]{:S(2)}, u32[]{:S(2)}) collective-permute-start(bf16[2,1,64,2240]{3,2,1,0:T(8,128)(2,1)} %get-tuple-element.27), channel_id=1, source_target_pairs={{0,1},{1,2},{2,3},{3,4},{4,5},{5,6},{6,7},{7,8},{8,9},{9,10},{10,1... | collective-permute-start | bytes 1720328 | tf_op jit(solution)/shard_map/ppermute | solution.py:20
  43.6 4.3 %reshape.112 = bf16[512,20,112]{2,1,0:T(8,128)(2,1)} reshape(bf16[2,4,64,2240]{3,2,1,0:T(8,128)(2,1)S(1)} %copy-done) | data formatting | bytes 4587520 | tf_op jit(solution)/shard_map/reshape | solution.py:111
  47.9 6.5 %max.20 = bf16[512,20,112]{2,1,0:T(8,128)(2,1)} reshape(bf16[2,4,64,2240]{3,2,1,0:T(8,128)(2,1)} %broadcast_maximum_fusion) | data formatting | bytes 4587520 | tf_op jit(solution)/shard_map/max | solution.py:113
  54.5 4.1 %fusion.8 = f32[20,112,112]{2,1,0:T(8,128)S(1)} fusion(bf16[512,20,112]{2,1,0:T(8,128)(2,1)} %reshape.112, bf16[512,20,112]{2,1,0:T(8,128)(2,1)} %max.20), kind=kOutput, calls=%fused_computation.17 | convolution fusion | flops 256901120 | bytes 5591040 | tf_op jit(solution)/shard_map/thd,the->hde/dot_general | solution.py:112
  58.6 3.6 %all_to_all.22 = f32[256,1,980]{2,1,0:T(1,128)} reshape(f32[20,112,112]{2,1,0:T(8,128)S(1)} %fusion.8) | data formatting | bytes 2007040 | tf_op jit(solution)/shard_map/all_to_all | solution.py:40
  62.2 9.4 %all-to-all-start = ((f32[256,1,980]{2,1,0:T(1,128)}), f32[256,1,980]{2,1,0:T(1,128)S(1)}, u32[]{:S(2)}, u32[]{:S(2)}) async-start(f32[256,1,980]{2,1,0:T(1,128)} %all_to_all.22), calls=%async_computation | async-start | bytes 2097152 | tf_op jit(solution)/shard_map/all_to_all | solution.py:40
  71.7 1.8 slice_reduce_fusion.11
  73.5 2.5 %fusion.7 = bf16[2,6,66,2240]{3,2,1,0:T(8,128)(2,1)S(1)} fusion(bf16[2,1,64,2240]{3,2,1,0:T(8,128)(2,1)} %collective-permute-done.1, bf16[2,4,64,2240]{3,2,1,0:T(8,128)(2,1)S(1)} %copy-done, bf16[2,1,64,2240]{3,2,1,0:T(8,128)(2,1)} %collective-permute-done), kind=kLoop, calls=%fused_computation.16 | loop fusion | flops 21288960 | bytes 6988800 | tf_op jit(solution)/shard_map/concatenate | solution.py:24
  76.0 6.8 %add_convert_fusion.1 = bf16[2,4,64,2240]{3,2,1,0:T(8,128)(2,1)} fusion(bf16[2,4,64,2240]{3,2,1,0:T(8,128)(2,1)S(1)} %copy-done, bf16[2,6,66,2240]{3,2,1,0:T(8,128)(2,1)S(1)} %fusion.7, bf16[2,1,64,2240]{3,2,1,0:T(8,128)(2,1)} %collective-permute-done.1, bf16[2,1,64,2240]{3,2,1,0:T(8,128)(2,1)} %collective-permute-done, f32[2240]{0:T(1024)S(1)} %get-tuple-element.22, ...), kind=kLoop, calls=%fused_computation.11 | loop fusion | flops 33259520 | bytes 19577600 | tf_op jit(solution)/shard_map/convert_element_type | solution.py:61
  82.8 4.7 %collective-permute-start.2 = (bf16[2,4,64,2240]{3,2,1,0:T(8,128)(2,1)}, bf16[2,4,64,2240]{3,2,1,0:T(8,128)(2,1)}, u32[]{:S(2)}, u32[]{:S(2)}) collective-permute-start(bf16[2,4,64,2240]{3,2,1,0:T(8,128)(2,1)} %add_convert_fusion.1), channel_id=1, source_target_pairs={{0,16},{16,32},{32,48},{48,64},{64,80},{80,96},{96,112},{112,128},... | collective-permute-start | bytes 6881288 | tf_op jit(solution)/shard_map/ppermute | solution.py:31
  87.5 16.7 %all-to-all-done = f32[256,1,980]{2,1,0:T(1,128)S(1)} async-done(((f32[256,1,980]{2,1,0:T(1,128)}), f32[256,1,980]{2,1,0:T(1,128)S(1)}, u32[]{:S(2)}, u32[]{:S(2)}) %all-to-all-start) | async-done | bytes 1003552 | tf_op jit(solution)/shard_map/all_to_all | solution.py:40
  109.0 6.8 %all-to-all-start.1 = ((bf16[256,2,490]{2,1,0:T(2,128)(2,1)}), bf16[256,2,490]{2,1,0:T(2,128)(2,1)}, u32[]{:S(2)}, u32[]{:S(2)}) async-start(bf16[256,2,490]{2,1,0:T(2,128)(2,1)} %reshape.140), calls=%async_computation.1 | async-start | bytes 1048576 | tf_op jit(solution)/shard_map/all_to_all | solution.py:45
  117.5 69.9 %all-to-all-done.1 = bf16[256,2,490]{2,1,0:T(2,128)(2,1)} async-done(((bf16[256,2,490]{2,1,0:T(2,128)(2,1)}), bf16[256,2,490]{2,1,0:T(2,128)(2,1)}, u32[]{:S(2)}, u32[]{:S(2)}) %all-to-all-start.1) | async-done | bytes 501792 | tf_op jit(solution)/shard_map/all_to_all | solution.py:45
  187.3 4.0 %reshape.141 = bf16[256,1,980]{2,1,0:T(2,128)(2,1)S(1)} reshape(bf16[256,2,490]{2,1,0:T(2,128)(2,1)} %all-to-all-done.1) | data formatting | bytes 1003520
  196.2 4.1 %select_n.42 = bf16[896,896]{1,0:T(8,128)(2,1)} reshape(bf16[8,112,8,112]{3,2,1,0:T(8,128)(2,1)} %get-tuple-element.32) | data formatting | bytes 3211264 | tf_op jit(solution)/shard_map/jit(_where)/select_n | solution.py:72
  201.8 4.2 %fusion.27 = f32[512,896]{1,0:T(8,128)} fusion(bf16[896,896]{1,0:T(8,128)(2,1)} %select_n.42, bf16[512,2240]{1,0:T(8,128)(2,1)} %bitcast.38), kind=kOutput, calls=%fused_computation.36 | convolution fusion | flops 822083584 | bytes 4358144 | tf_op jit(solution)/shard_map/dot_general | solution.py:76
  206.0 2.4 select_n.40
  208.4 3.0 %fusion.29 = f32[512,896]{1,0:T(8,128)S(1)} fusion(bf16[896,896]{1,0:T(8,128)(2,1)} %select_n.40, bf16[512,2240]{1,0:T(8,128)(2,1)} %bitcast.39), kind=kOutput, calls=%fused_computation.38 | convolution fusion | flops 822083584 | bytes 4358144 | tf_op jit(solution)/shard_map/dot_general | solution.py:76
  215.6 4.5 %add_convert_fusion = bf16[2,4,64,2240]{3,2,1,0:T(8,128)(2,1)S(1)} fusion(bf16[2,4,64,2240]{3,2,1,0:T(8,128)(2,1)} %collective-permute-done.2, bf16[2,4,64,2240]{3,2,1,0:T(8,128)(2,1)} %add_convert_fusion.1, f32[2,4,64,2240]{3,2,1,0:T(8,128)S(1)} %bitcast.35, f32[2240]{0:T(1024)S(1)} %get-tuple-element.25, f32[2240]{0:T(1024)S(1)} %get-tuple-element.26, ...), kind=kLoop, calls=%fused_computation.10 | loop fusion | flops 13762560 | bytes 11504640 | tf_op jit(solution)/shard_map/convert_element_type | solution.py:132
  220.9 6.0 %fusion.46 = bf16[512,16,144]{0,2,1:T(8,128)(2,1)S(1)} fusion(bf16[512,2240,1]{1,0,2:T(8,128)(2,1)S(1)} %bitcast.41, bf16[16,144,2240]{2,1,0:T(8,128)(2,1)S(1)} %bitcast.47), kind=kOutput, calls=%fused_computation.76 | convolution fusion | flops 5284823040 | bytes 14974976 | tf_op jit(solution)/shard_map/dot_general | solution.py:133
  226.9 3.8 %reshape.127 = bf16[2,4,64,2240]{2,1,0,3:T(4,128)(2,1)} reshape(bf16[512,16,140]{0,2,1:T(8,128)(2,1)S(1)} %bitcast.40) | data formatting | bytes 4587520 | tf_op jit(solution)/shard_map/reshape | solution.py:135
  230.8 7.8 %copy.65 = bf16[2,4,64,2240]{3,2,1,0:T(8,128)(2,1)} copy(bf16[2,4,64,2240]{2,1,0,3:T(4,128)(2,1)} %reshape.127) | data formatting | bytes 4587520 | tf_op jit(solution)/shard_map/reshape | solution.py:135
  (56 shorter events, 24.1 us)
Async XLA Ops:
  6.5 185.9 %all-gather.5.cloned.1.call-start = ((), (), s32[]{:S(2)}) async-start(), calls=%async_computation.2 | async-start | bytes 11280384 | tf_op jit(solution)/shard_map/all_gather | solution.py:107
  31.4 3.8 %copy-start = (bf16[2,4,64,2240]{3,2,1,0:T(8,128)(2,1)S(1)}, bf16[2,4,64,2240]{3,2,1,0:T(8,128)(2,1)}, u32[]{:S(2)}) copy-start(bf16[2,4,64,2240]{3,2,1,0:T(8,128)(2,1)} %param.9) | copy-start | bytes 6881284
  35.2 6.8 %copy-start.1 = (bf16[2,4,64,2240]{3,2,1,0:T(8,128)(2,1)S(1)}, bf16[2,4,64,2240]{3,2,1,0:T(8,128)(2,1)}, u32[]{:S(2)}) copy-start(bf16[2,4,64,2240]{3,2,1,0:T(8,128)(2,1)} %param.8) | copy-start | bytes 6881284
  36.4 37.1 %collective-permute-start.1 = (bf16[2,1,64,2240]{3,2,1,0:T(8,128)(2,1)}, bf16[2,1,64,2240]{3,2,1,0:T(8,128)(2,1)}, u32[]{:S(2)}, u32[]{:S(2)}) collective-permute-start(bf16[2,1,64,2240]{3,2,1,0:T(8,128)(2,1)} %get-tuple-element.28), channel_id=1, source_target_pairs={{1,0},{2,1},{3,2},{4,3},{5,4},{6,5},{7,6},{8,7},{9,8},{10,9},{11,1... | collective-permute-start | bytes 1720328 | tf_op jit(solution)/shard_map/ppermute | solution.py:23
  38.6 34.9 %collective-permute-start = (bf16[2,1,64,2240]{3,2,1,0:T(8,128)(2,1)}, bf16[2,1,64,2240]{3,2,1,0:T(8,128)(2,1)}, u32[]{:S(2)}, u32[]{:S(2)}) collective-permute-start(bf16[2,1,64,2240]{3,2,1,0:T(8,128)(2,1)} %get-tuple-element.27), channel_id=1, source_target_pairs={{0,1},{1,2},{2,3},{3,4},{4,5},{5,6},{6,7},{7,8},{8,9},{9,10},{10,1... | collective-permute-start | bytes 1720328 | tf_op jit(solution)/shard_map/ppermute | solution.py:20
  62.2 42.0 %all-to-all-start = ((f32[256,1,980]{2,1,0:T(1,128)}), f32[256,1,980]{2,1,0:T(1,128)S(1)}, u32[]{:S(2)}, u32[]{:S(2)}) async-start(f32[256,1,980]{2,1,0:T(1,128)} %all_to_all.22), calls=%async_computation | async-start | bytes 2097152 | tf_op jit(solution)/shard_map/all_to_all | solution.py:40
  82.8 109.6 %collective-permute-start.2 = (bf16[2,4,64,2240]{3,2,1,0:T(8,128)(2,1)}, bf16[2,4,64,2240]{3,2,1,0:T(8,128)(2,1)}, u32[]{:S(2)}, u32[]{:S(2)}) collective-permute-start(bf16[2,4,64,2240]{3,2,1,0:T(8,128)(2,1)} %add_convert_fusion.1), channel_id=1, source_target_pairs={{0,16},{16,32},{32,48},{48,64},{64,80},{80,96},{96,112},{112,128},... | collective-permute-start | bytes 6881288 | tf_op jit(solution)/shard_map/ppermute | solution.py:31
  105.4 10.4 %copy-start.4 = (f32[3,2240]{1,0:T(4,128)S(1)}, f32[3,2240]{1,0:T(4,128)}, u32[]{:S(2)}) copy-start(f32[3,2240]{1,0:T(4,128)} %param.12) | copy-start | bytes 80644
  105.7 10.2 %copy-start.2 = (bf16[2,4,64,2240]{3,2,1,0:T(8,128)(2,1)S(1)}, bf16[2,4,64,2240]{3,2,1,0:T(8,128)(2,1)}, u32[]{:S(2)}) copy-start(bf16[2,4,64,2240]{3,2,1,0:T(8,128)(2,1)} %param.7) | copy-start | bytes 6881284
  109.0 78.4 %all-to-all-start.1 = ((bf16[256,2,490]{2,1,0:T(2,128)(2,1)}), bf16[256,2,490]{2,1,0:T(2,128)(2,1)}, u32[]{:S(2)}, u32[]{:S(2)}) async-start(bf16[256,2,490]{2,1,0:T(2,128)(2,1)} %reshape.140), calls=%async_computation.1 | async-start | bytes 1048576 | tf_op jit(solution)/shard_map/all_to_all | solution.py:45
  208.4 3.0 %copy-start.3 = (f32[512,896]{1,0:T(8,128)S(1)}, f32[512,896]{1,0:T(8,128)}, u32[]{:S(2)}) copy-start(f32[512,896]{1,0:T(8,128)} %fusion.27) | copy-start | bytes 5505028
  214.5 1.1 copy-start.5
  214.5 5.6 %slice-start = ((s8[10616832]{0:T(1024)(128)(4,1)}), s8[2228224]{0:T(1024)(128)(4,1)S(1)}, s32[]{:S(2)}) async-start(s8[10616832]{0:T(1024)(128)(4,1)} %bitcast.45), calls=%async_computation.3 | async-start | bytes 4456448
  214.5 5.6 %slice-start.1 = ((s8[10616832]{0:T(1024)(128)(4,1)}), s8[4194304]{0:T(1024)(128)(4,1)S(1)}, s32[]{:S(2)}) async-start(s8[10616832]{0:T(1024)(128)(4,1)} %bitcast.45), calls=%async_computation.4 | async-start | bytes 8388608
  215.6 5.3 %slice-start.2 = ((s8[10616832]{0:T(1024)(128)(4,1)}), s8[4194304]{0:T(1024)(128)(4,1)S(1)}, s32[]{:S(2)}) async-start(s8[10616832]{0:T(1024)(128)(4,1)} %bitcast.45), calls=%async_computation.5 | async-start | bytes 8388608
Sparse Core Ops, SparseCore 0:
  35.3 132.4 all-gather.4

commit v9 on v4

--- a/solution.py
+++ b/solution.py
@@ -61,6 +61,21 @@
     return summed.astype(jnp.bfloat16)
 
 
+def banded_state(keys, values):
+    group = math.lcm(HEAD_DIM, 128) // HEAD_DIM
+    blocks = []
+    for first in range(0, HEADS, group):
+        count = min(group, HEADS - first)
+        span = slice(first * HEAD_DIM, (first + count) * HEAD_DIM)
+        product = lax.dot_general(
+            keys[:, span], values[:, span], (((0,), (0,)), ((), ())), preferred_element_type=jnp.float32
+        )
+        for head in range(count):
+            rows = slice(head * HEAD_DIM, (head + 1) * HEAD_DIM)
+            blocks.append(product[rows, rows])
+    return jnp.stack(blocks)
+
+
 def banded_attention(queries, state_low):
     heads, dim, _ = state_low.shape
     group = math.lcm(dim, 128) // dim
@@ -108,8 +123,9 @@
     queries = query_heads.reshape(token_count, HEADS, HEAD_DIM)
     key_rows = key_heads.reshape(token_count, HEADS, HEAD_DIM)
     value_rows = value_heads.reshape(token_count, HEADS, HEAD_DIM)
-    local_state = jnp.einsum(
-        "thd,the->hde", jnp.maximum(key_rows, 0), value_rows, preferred_element_type=jnp.float32
+    local_state = banded_state(
+        jnp.maximum(key_heads.reshape(token_count, model_width), 0),
+        value_heads.reshape(token_count, model_width),
     )
     padded = extended(value_heads, (("space", 1),), 1)
     spatial = spatial_conv(padded, spatial_kernel)

time: 205 us -> 199 us (0.971); the launches traced: 201 us -> 198 us
  waiting for transfers between devices: 37.3 us -> 47.1 us
  local copies, waits for them, and re-layouts: 55.4 us -> 46.2 us
  other arithmetic: 23.4 us -> 20.7 us
    all_gather x1, waiting for transfers between devices: 0.01 us -> 13.4 us  [per_device(): weight_stack = lax.all_gather(weight_cols, 'tm', axis=0)]
    max x1 -> x0, local copies, waits for them, and re-layouts: 6.55 us -> none  [per_device(): jnp.maximum(key_rows, 0)]
    reshape x1 -> x0, local copies, waits for them, and re-layouts: 4.32 us -> none  [per_device(): value_rows = value_heads.reshape(token_count, HEADS, HEAD_DIM)]
    max x1, other arithmetic: 3.38 us -> 0.15 us  [per_device(): jnp.maximum(key_heads.reshape(token_count, model_width), 0)]
    ppermute x1, waiting for transfers between devices: 3.2 us -> 0.01 us  [from_behind(): return lax.ppermute(block, axis, route)]
    unnamed x26 -> x47, local copies, waits for them, and re-layouts: 8.79 us -> 10.3 us
    dot_general x1 -> x3, matrix products: 4.13 us -> 2.75 us  [banded_state(): lax.dot_general(keys[:, span], values[:, span], (((0,), (0,)), ((), ())),...]
  transfers between devices with their start and end apart: 6 -> 6, of which waited for: 3 -> 3; matrix products, arithmetic and copies ran while one was open for 40% -> 33% of each run, Pallas kernels for 0% -> 0%
where the time goes in v9:
time: 199 us; the launch traced here: 198 us
  waiting for transfers between devices  47.1 us (24%)
  local copies, waits for them, and re-layouts  46.2 us (23%)
  starting transfers between devices  26.5 us (13%)
  blocking collectives  24.9 us (13%)
  other arithmetic  20.7 us (10%)
  matrix products  18.4 us (9%)
  between operations  13.8 us (7%)
    all_gather x1, blocking collectives, per_device(): weight_cols = lax.all_gather(out_weight, 'space', axis=0, tiled=True)  24.9 us
    all_to_all x1, waiting for transfers between devices, prefix_state(): mine = lax.all_to_all(flat, axes, 0, 0, tiled=True)  21.5 us
    all_gather x1, waiting for transfers between devices, per_device(): weight_stack = lax.all_gather(weight_cols, 'tm', axis=0)  13.4 us
    all_to_all x1, waiting for transfers between devices, prefix_state(): gathered = lax.all_to_all(outgoing, axes, 0, 0, tiled=True)  12.1 us
    reshape x1, local copies, waits for them, and re-layouts, per_device(): weight_stack.transpose(1, 0, 2).reshape(model_width, model_width)  11.9 us
    all_to_all x1, starting transfers between devices, prefix_state(): mine = lax.all_to_all(flat, axes, 0, 0, tiled=True)  11 us
    unnamed x47, local copies, waits for them, and re-layouts  10.3 us
    select_n x3, local copies, waits for them, and re-layouts, banded_attention(): jnp.where(eye[:, None, :, None], blocks[:, :, None, :], jnp.zeros((), blo...  9.26 us
  transfers between devices with their start and end apart: 6, of which 3 were waited for; matrix products, arithmetic and copies ran while one was open for 33% of the time, Pallas kernels for 0%

profile of v9, /device:TPU:1, one launch (start us, length us, event | category | flops | bytes accessed | tf_op | source)
XLA Modules:
  0.0 197.5 jit_solution(14108335645041693496)
XLA Ops:
  6.5 24.9 %all-gather.1 = bf16[16,140,140]{2,1,0:T(8,128)(2,1)S(1)} all-gather(bf16[1,140,140]{2,1,0:T(8,128)(2,1)} %bitcast.121), channel_id=1, replica_groups=mesh['tm'=16,'space'=16] {'space'}, dimensions={0}, use_global_device_ids=true | all-gather | bytes 666400 | tf_op jit(solution)/shard_map/all_gather | solution.py:120
  32.7 2.3 %copy.47 = bf16[1,2240,140]{1,2,0:T(8,128)(2,1)} copy(bf16[1,2240,140]{2,1,0:T(8,128)(2,1)} %reshape.124) | data formatting | bytes 1254400
  36.1 2.0 %collective-permute-start = (bf16[2,1,64,2240]{3,2,1,0:T(8,128)(2,1)}, bf16[2,1,64,2240]{3,2,1,0:T(8,128)(2,1)}, u32[]{:S(2)}, u32[]{:S(2)}) collective-permute-start(bf16[2,1,64,2240]{3,2,1,0:T(8,128)(2,1)} %get-tuple-element.25), channel_id=1, source_target_pairs={{0,1},{1,2},{2,3},{3,4},{4,5},{5,6},{6,7},{7,8},{8,9},{9,10},{10,1... | collective-permute-start | bytes 1720328 | tf_op jit(solution)/shard_map/ppermute | solution.py:20
  38.1 3.2 %collective-permute-start.1 = (bf16[2,1,64,2240]{3,2,1,0:T(8,128)(2,1)}, bf16[2,1,64,2240]{3,2,1,0:T(8,128)(2,1)}, u32[]{:S(2)}, u32[]{:S(2)}) collective-permute-start(bf16[2,1,64,2240]{3,2,1,0:T(8,128)(2,1)} %get-tuple-element.26), channel_id=1, source_target_pairs={{1,0},{2,1},{3,2},{4,3},{5,4},{6,5},{7,6},{8,7},{9,8},{10,9},{11,1... | collective-permute-start | bytes 1720328 | tf_op jit(solution)/shard_map/ppermute | solution.py:23
  45.7 3.6 %all_to_all.22 = f32[256,1,980]{2,1,0:T(1,128)} reshape(f32[20,112,112]{2,1,0:T(8,128)S(1)} %fusion.43) | data formatting | bytes 2007040 | tf_op jit(solution)/shard_map/all_to_all | solution.py:40
  49.3 11.0 %all-to-all-start = ((f32[256,1,980]{2,1,0:T(1,128)}), f32[256,1,980]{2,1,0:T(1,128)S(1)}, u32[]{:S(2)}, u32[]{:S(2)}) async-start(f32[256,1,980]{2,1,0:T(1,128)} %all_to_all.22), calls=%async_computation | async-start | bytes 2097152 | tf_op jit(solution)/shard_map/all_to_all | solution.py:40
  62.1 2.4 %fusion.7 = bf16[2,6,66,2240]{3,2,1,0:T(8,128)(2,1)S(1)} fusion(bf16[2,1,64,2240]{3,2,1,0:T(8,128)(2,1)} %collective-permute-done.1, bf16[2,4,64,2240]{3,2,1,0:T(8,128)(2,1)S(1)} %copy-done, bf16[2,1,64,2240]{3,2,1,0:T(8,128)(2,1)} %collective-permute-done), kind=kLoop, calls=%fused_computation.16 | loop fusion | flops 21288960 | bytes 6988800 | tf_op jit(solution)/shard_map/concatenate | solution.py:24
  64.5 6.8 %add_convert_fusion.1 = bf16[2,4,64,2240]{3,2,1,0:T(8,128)(2,1)} fusion(bf16[2,4,64,2240]{3,2,1,0:T(8,128)(2,1)S(1)} %copy-done, bf16[2,6,66,2240]{3,2,1,0:T(8,128)(2,1)S(1)} %fusion.7, bf16[2,1,64,2240]{3,2,1,0:T(8,128)(2,1)} %collective-permute-done.1, bf16[2,1,64,2240]{3,2,1,0:T(8,128)(2,1)} %collective-permute-done, f32[2240]{0:T(1024)S(1)} %get-tuple-element.20, ...), kind=kLoop, calls=%fused_computation.10 | loop fusion | flops 33259520 | bytes 19577600 | tf_op jit(solution)/shard_map/convert_element_type | solution.py:61
  71.3 21.5 %all-to-all-done = f32[256,1,980]{2,1,0:T(1,128)S(1)} async-done(((f32[256,1,980]{2,1,0:T(1,128)}), f32[256,1,980]{2,1,0:T(1,128)S(1)}, u32[]{:S(2)}, u32[]{:S(2)}) %all-to-all-start) | async-done | bytes 1003552 | tf_op jit(solution)/shard_map/all_to_all | solution.py:40
  97.7 6.8 %all-to-all-start.1 = ((bf16[256,2,490]{2,1,0:T(2,128)(2,1)}), bf16[256,2,490]{2,1,0:T(2,128)(2,1)}, u32[]{:S(2)}, u32[]{:S(2)}) async-start(bf16[256,2,490]{2,1,0:T(2,128)(2,1)} %reshape.137), calls=%async_computation.1 | async-start | bytes 1048576 | tf_op jit(solution)/shard_map/all_to_all | solution.py:45
  104.6 3.5 %broadcast_maximum_fusion.1 = bf16[2,4,64,2240]{3,2,1,0:T(8,128)(2,1)} fusion(bf16[2,4,64,2240]{3,2,1,0:T(8,128)(2,1)} %param.7), kind=kLoop, calls=%fused_computation.25 | loop fusion | flops 1146880 | bytes 4587520 | tf_op jit(solution)/shard_map/max | solution.py:135
  108.0 3.5 %collective-permute-start.2 = (bf16[2,4,64,2240]{3,2,1,0:T(8,128)(2,1)S(1)}, bf16[2,4,64,2240]{3,2,1,0:T(8,128)(2,1)}, u32[]{:S(2)}, u32[]{:S(2)}) collective-permute-start(bf16[2,4,64,2240]{3,2,1,0:T(8,128)(2,1)S(1)} %copy-done.1), channel_id=1, source_target_pairs={{0,16},{16,32},{32,48},{48,64},{64,80},{80,96},{96,112},{112,128},... | collective-permute-start | bytes 6881288 | tf_op jit(solution)/shard_map/ppermute | solution.py:31
  111.5 12.1 %all-to-all-done.1 = bf16[256,2,490]{2,1,0:T(2,128)(2,1)} async-done(((bf16[256,2,490]{2,1,0:T(2,128)(2,1)}), bf16[256,2,490]{2,1,0:T(2,128)(2,1)}, u32[]{:S(2)}, u32[]{:S(2)}) %all-to-all-start.1) | async-done | bytes 501792 | tf_op jit(solution)/shard_map/all_to_all | solution.py:45
  123.6 4.0 %reshape.138 = bf16[256,1,980]{2,1,0:T(2,128)(2,1)S(1)} reshape(bf16[256,2,490]{2,1,0:T(2,128)(2,1)} %all-to-all-done.1) | data formatting | bytes 1003520
  127.6 2.0 %copy.37 = bf16[256,1,980]{0,2,1:T(8,128)(2,1)} copy(bf16[256,1,980]{2,1,0:T(2,128)(2,1)S(1)} %reshape.138) | data formatting | bytes 1003520 | tf_op jit(solution)/shard_map/all_to_all | solution.py:45
  129.6 13.4 %all-gather.5.cloned.1.call-done = bf16[16,2240,140]{1,2,0:T(8,128)(2,1)} async-done(((bf16[1,2240,140]{1,2,0:T(8,128)(2,1)}), bf16[16,2240,140]{1,2,0:T(8,128)(2,1)}) %all-gather.5.cloned.1.call-update) | async-done | bytes 10035216 | tf_op jit(solution)/shard_map/all_gather | solution.py:121
  142.9 11.9 %reshape.112 = bf16[2240,2240]{0,1:T(8,128)(2,1)} reshape(bf16[2240,16,140]{0,2,1:T(8,128)(2,1)} %bitcast.111) | data formatting | bytes 20070400 | tf_op jit(solution)/shard_map/reshape | solution.py:133
  157.7 2.4 %broadcast_select_fusion.1 = (bf16[8,112,8,112]{3,2,1,0:T(8,128)(2,1)}, bf16[8,112,8,112]{3,2,1,0:T(8,128)(2,1)}) fusion(pred[8,8]{1,0:T(8,128)(4,1)S(1)} %iota_compare_fusion.15, bf16[8,112,112]{2,1,0:T(8,128)(2,1)S(1)} %get-tuple-element.27, bf16[8,112,112]{2,1,0:T(8,128)(2,1)S(1)} %get-tuple-element.28), kind=kLoop, calls=%fused_computation.23 | loop fusion | flops 1605632 | bytes 3612736 | tf_op jit(solution)/shard_map/jit(_where)/select_n | solution.py:87
  161.5 4.1 %select_n.40 = bf16[896,896]{1,0:T(8,128)(2,1)} reshape(bf16[8,112,8,112]{3,2,1,0:T(8,128)(2,1)} %get-tuple-element.29) | data formatting | bytes 3211264 | tf_op jit(solution)/shard_map/jit(_where)/select_n | solution.py:87
  165.6 4.1 %select_n.42 = bf16[896,896]{1,0:T(8,128)(2,1)} reshape(bf16[8,112,8,112]{3,2,1,0:T(8,128)(2,1)} %get-tuple-element.30) | data formatting | bytes 3211264 | tf_op jit(solution)/shard_map/jit(_where)/select_n | solution.py:87
  169.7 3.0 %fusion.32 = f32[512,896]{1,0:T(8,128)S(1)} fusion(bf16[896,896]{1,0:T(8,128)(2,1)} %select_n.40, bf16[512,2240]{1,0:T(8,128)(2,1)} %bitcast.116), kind=kOutput, calls=%fused_computation.41 | convolution fusion | flops 822083584 | bytes 4358144 | tf_op jit(solution)/shard_map/dot_general | solution.py:91
  178.2 4.0 %add_convert_fusion = bf16[2,4,64,2240]{3,2,1,0:T(8,128)(2,1)S(1)} fusion(bf16[2,4,64,2240]{3,2,1,0:T(8,128)(2,1)} %collective-permute-done.2, bf16[2,4,64,2240]{3,2,1,0:T(8,128)(2,1)S(1)} %copy-done.1, f32[2,4,64,2240]{3,2,1,0:T(8,128)S(1)} %bitcast.107, f32[2240]{0:T(1024)S(1)} %get-tuple-element.23, f32[2240]{0:T(1024)S(1)} %get-tuple-element.24, ...), kind=kLoop, calls=%fused_computation.9 | loop fusion | flops 13762560 | bytes 11504640 | tf_op jit(solution)/shard_map/convert_element_type | solution.py:144
  182.4 5.8 %convolution_convert_fusion = bf16[512,2240]{0,1:T(8,128)(2,1)S(1)} fusion(bf16[512,2240]{1,0:T(8,128)(2,1)S(1)} %bitcast.118, bf16[2240,2240]{0,1:T(8,128)(2,1)S(1)} %bitcast.113), kind=kOutput, calls=%fused_computation.14 | convolution fusion | flops 5139169280 | bytes 14622720 | tf_op jit(solution)/shard_map/dot_general | solution.py:145
  188.2 2.5 %copy.43 = bf16[512,2240]{1,0:T(8,128)(2,1)} copy(bf16[512,2240]{0,1:T(8,128)(2,1)S(1)} %convolution_convert_fusion) | data formatting | bytes 4587520 | tf_op jit(solution)/shard_map/convert_element_type | solution.py:148
  (81 shorter events, 23.1 us)
Async XLA Ops:
  6.5 136.4 %all-gather.5.cloned.1.call-start = ((), (), s32[]{:S(2)}) async-start(), calls=%async_computation.2 | async-start | bytes 11280384 | tf_op jit(solution)/shard_map/all_gather | solution.py:121
  31.4 3.5 %copy-start = (bf16[2,4,64,2240]{3,2,1,0:T(8,128)(2,1)S(1)}, bf16[2,4,64,2240]{3,2,1,0:T(8,128)(2,1)}, u32[]{:S(2)}) copy-start(bf16[2,4,64,2240]{3,2,1,0:T(8,128)(2,1)} %param.9) | copy-start | bytes 6881284
  35.0 6.4 %copy-start.3 = (bf16[2,4,64,2240]{3,2,1,0:T(8,128)(2,1)S(1)}, bf16[2,4,64,2240]{3,2,1,0:T(8,128)(2,1)}, u32[]{:S(2)}) copy-start(bf16[2,4,64,2240]{3,2,1,0:T(8,128)(2,1)} %param.8) | copy-start | bytes 6881284
  36.1 26.0 %collective-permute-start = (bf16[2,1,64,2240]{3,2,1,0:T(8,128)(2,1)}, bf16[2,1,64,2240]{3,2,1,0:T(8,128)(2,1)}, u32[]{:S(2)}, u32[]{:S(2)}) collective-permute-start(bf16[2,1,64,2240]{3,2,1,0:T(8,128)(2,1)} %get-tuple-element.25), channel_id=1, source_target_pairs={{0,1},{1,2},{2,3},{3,4},{4,5},{5,6},{6,7},{7,8},{8,9},{9,10},{10,1... | collective-permute-start | bytes 1720328 | tf_op jit(solution)/shard_map/ppermute | solution.py:20
  38.1 24.0 %collective-permute-start.1 = (bf16[2,1,64,2240]{3,2,1,0:T(8,128)(2,1)}, bf16[2,1,64,2240]{3,2,1,0:T(8,128)(2,1)}, u32[]{:S(2)}, u32[]{:S(2)}) collective-permute-start(bf16[2,1,64,2240]{3,2,1,0:T(8,128)(2,1)} %get-tuple-element.26), channel_id=1, source_target_pairs={{1,0},{2,1},{3,2},{4,3},{5,4},{6,5},{7,6},{8,7},{9,8},{10,9},{11,1... | collective-permute-start | bytes 1720328 | tf_op jit(solution)/shard_map/ppermute | solution.py:23
  49.3 43.6 %all-to-all-start = ((f32[256,1,980]{2,1,0:T(1,128)}), f32[256,1,980]{2,1,0:T(1,128)S(1)}, u32[]{:S(2)}, u32[]{:S(2)}) async-start(f32[256,1,980]{2,1,0:T(1,128)} %all_to_all.22), calls=%async_computation | async-start | bytes 2097152 | tf_op jit(solution)/shard_map/all_to_all | solution.py:40
  94.4 10.1 %copy-start.7 = (f32[3,2240]{1,0:T(4,128)S(1)}, f32[3,2240]{1,0:T(4,128)}, u32[]{:S(2)}) copy-start(f32[3,2240]{1,0:T(4,128)} %param.12) | copy-start | bytes 80644
  97.7 26.0 %all-to-all-start.1 = ((bf16[256,2,490]{2,1,0:T(2,128)(2,1)}), bf16[256,2,490]{2,1,0:T(2,128)(2,1)}, u32[]{:S(2)}, u32[]{:S(2)}) async-start(bf16[256,2,490]{2,1,0:T(2,128)(2,1)} %reshape.137), calls=%async_computation.1 | async-start | bytes 1048576 | tf_op jit(solution)/shard_map/all_to_all | solution.py:45
  104.6 3.5 %copy-start.1 = (bf16[2,4,64,2240]{3,2,1,0:T(8,128)(2,1)S(1)}, bf16[2,4,64,2240]{3,2,1,0:T(8,128)(2,1)}, u32[]{:S(2)}) copy-start(bf16[2,4,64,2240]{3,2,1,0:T(8,128)(2,1)} %add_convert_fusion.1) | copy-start | bytes 6881284
  108.0 70.1 %collective-permute-start.2 = (bf16[2,4,64,2240]{3,2,1,0:T(8,128)(2,1)S(1)}, bf16[2,4,64,2240]{3,2,1,0:T(8,128)(2,1)}, u32[]{:S(2)}, u32[]{:S(2)}) collective-permute-start(bf16[2,4,64,2240]{3,2,1,0:T(8,128)(2,1)S(1)} %copy-done.1), channel_id=1, source_target_pairs={{0,16},{16,32},{32,48},{48,64},{64,80},{80,96},{96,112},{112,128},... | collective-permute-start | bytes 6881288 | tf_op jit(solution)/shard_map/ppermute | solution.py:31
  142.9 11.9 %copy-start.4 = (bf16[256,1,980]{0,2,1:T(8,128)(2,1)S(1)}, bf16[256,1,980]{0,2,1:T(8,128)(2,1)}, u32[]{:S(2)}) copy-start(bf16[256,1,980]{0,2,1:T(8,128)(2,1)} %copy.37) | copy-start | bytes 1505284
  157.7 2.4 %copy-start.5 = (bf16[448,448]{1,0:T(8,128)(2,1)S(1)}, bf16[448,448]{1,0:T(8,128)(2,1)}, u32[]{:S(2)}) copy-start(bf16[448,448]{1,0:T(8,128)(2,1)} %select_n.44) | copy-start | bytes 1204228
  169.7 3.1 %copy-start.2 = (bf16[2,4,64,2240]{3,2,1,0:T(8,128)(2,1)S(1)}, bf16[2,4,64,2240]{3,2,1,0:T(8,128)(2,1)}, u32[]{:S(2)}) copy-start(bf16[2,4,64,2240]{3,2,1,0:T(8,128)(2,1)} %broadcast_maximum_fusion.1) | copy-start | bytes 6881284
  169.7 3.1 %copy-start.6 = (bf16[896,896]{1,0:T(8,128)(2,1)S(1)}, bf16[896,896]{1,0:T(8,128)(2,1)}, u32[]{:S(2)}) copy-start(bf16[896,896]{1,0:T(8,128)(2,1)} %select_n.42) | copy-start | bytes 4816900
  177.0 1.1 copy-start.8
  177.1 5.1 %slice-start = ((s8[10321920]{0:T(1024)(128)(4,1)}), s8[4194304]{0:T(1024)(128)(4,1)S(1)}, s32[]{:S(2)}) async-start(s8[10321920]{0:T(1024)(128)(4,1)} %bitcast.112), calls=%async_computation.3 | async-start | bytes 8388608
  177.1 5.1 %slice-start.1 = ((s8[10321920]{0:T(1024)(128)(4,1)}), s8[1933312]{0:T(1024)(128)(4,1)S(1)}, s32[]{:S(2)}) async-start(s8[10321920]{0:T(1024)(128)(4,1)} %bitcast.112), calls=%async_computation.4 | async-start | bytes 3866624
  178.2 4.2 %slice-start.2 = ((s8[10321920]{0:T(1024)(128)(4,1)}), s8[4194304]{0:T(1024)(128)(4,1)S(1)}, s32[]{:S(2)}) async-start(s8[10321920]{0:T(1024)(128)(4,1)} %bitcast.112), calls=%async_computation.5 | async-start | bytes 8388608
Sparse Core Ops, SparseCore 0:
  35.1 107.8 all-gather.4

commit v10 on v9

--- a/solution.py
+++ b/solution.py
@@ -117,8 +117,8 @@
     query_heads, key_heads, value_heads, head_gain, spatial_kernel, temporal_kernel, out_weight
 ):
     frame_count, row_count, col_count, model_width = query_heads.shape
-    weight_cols = lax.all_gather(out_weight, "space", axis=0, tiled=True)
-    weight_stack = lax.all_gather(weight_cols, "tm", axis=0)
+    weight_band = lax.all_gather(out_weight, "tm", axis=1, tiled=True)
+    weight_stack = lax.all_gather(weight_band, "space", axis=0)
     token_count = frame_count * row_count * col_count
     queries = query_heads.reshape(token_count, HEADS, HEAD_DIM)
     key_rows = key_heads.reshape(token_count, HEADS, HEAD_DIM)
@@ -130,7 +130,7 @@
     padded = extended(value_heads, (("space", 1),), 1)
     spatial = spatial_conv(padded, spatial_kernel)
     earlier_frames = from_behind(spatial, "tm", 1)
-    weight_flat = weight_stack.transpose(1, 0, 2).reshape(model_width, model_width)
+    weight_flat = weight_stack.reshape(model_width, model_width)
     state_low, spatial, weight_flat = prefix_state(local_state, spatial, weight_flat)
     flat_queries = jnp.maximum(query_heads.reshape(token_count, model_width), 0)
     attended = banded_attention(flat_queries, state_low)

time: 199 us -> 208 us (1.045)
  starting transfers between devices: 26.5 us -> 34.6 us
  blocking collectives: 24.9 us -> 21.3 us
  matrix products: 18.4 us -> 21.7 us
    all_gather x1, waiting for transfers between devices: 13.4 us -> 0.01 us  [per_device(): weight_stack = lax.all_gather(weight_band, 'space', axis=0)]
    optimization_barrier x1 -> x2, local copies, waits for them, and re-layouts: 0.21 us -> 12.1 us  [prefix_state(): gathered, beside_back = lax.optimization_barrier((gathered, beside_back))]
    reshape x1 -> x0, local copies, waits for them, and re-layouts: 11.9 us -> none  [per_device(): weight_stack.transpose(1, 0, 2).reshape(model_width, model_width)]
    all_to_all x1, waiting for transfers between devices: 21.5 us -> 32.9 us  [prefix_state(): mine = lax.all_to_all(flat, axes, 0, 0, tiled=True)]
    ppermute x1, starting transfers between devices: 2.04 us -> 9.11 us  [extended(): lax.ppermute(lax.slice_in_dim(block, block.shape[dim] - width, None, axis...]
    all_gather x1, blocking collectives: 24.9 us -> 21.3 us  [per_device(): weight_band = lax.all_gather(out_weight, 'tm', axis=1, tiled=True)]
    dot_general x1, matrix products: 5.81 us -> 9.04 us  [per_device(): projected = jnp.dot(mixed, weight_flat, preferred_element_type=jnp.float32)]
    all_to_all x1, starting transfers between devices: 11 us -> 13.4 us  [prefix_state(): mine = lax.all_to_all(flat, axes, 0, 0, tiled=True)]
  transfers between devices with their start and end apart: 6 -> 6, of which waited for: 3 -> 2; matrix products, arithmetic and copies ran while one was open for 33% -> 32% of each run, Pallas kernels for 0% -> 0%
where the time goes in v10:
time: 208 us; the launch traced here: 207 us
  waiting for transfers between devices  47.4 us (23%)
  local copies, waits for them, and re-layouts  47 us (23%)
  starting transfers between devices  34.6 us (17%)
  matrix products  21.7 us (10%)
  blocking collectives  21.3 us (10%)
  other arithmetic  20.8 us (10%)
  between operations  13.8 us (7%)
    all_to_all x1, waiting for transfers between devices, prefix_state(): mine = lax.all_to_all(flat, axes, 0, 0, tiled=True)  32.9 us
    all_gather x1, blocking collectives, per_device(): weight_band = lax.all_gather(out_weight, 'tm', axis=1, tiled=True)  21.3 us
    all_to_all x1, waiting for transfers between devices, prefix_state(): gathered = lax.all_to_all(outgoing, axes, 0, 0, tiled=True)  14.5 us
    all_to_all x1, starting transfers between devices, prefix_state(): mine = lax.all_to_all(flat, axes, 0, 0, tiled=True)  13.4 us
    optimization_barrier x2, local copies, waits for them, and re-layouts, prefix_state(): gathered, beside_back = lax.optimization_barrier((gathered, beside_back))  12.1 us
    unnamed x48, local copies, waits for them, and re-layouts  11.2 us
    select_n x3, local copies, waits for them, and re-layouts, banded_attention(): jnp.where(eye[:, None, :, None], blocks[:, :, None, :], jnp.zeros((), blo...  9.26 us
    ppermute x1, starting transfers between devices, extended(): lax.ppermute(lax.slice_in_dim(block, block.shape[dim] - width, None, axis...  9.11 us
  transfers between devices with their start and end apart: 6, of which 2 were waited for; matrix products, arithmetic and copies ran while one was open for 32% of the time, Pallas kernels for 0%

profile of v10, /device:TPU:1, one launch (start us, length us, event | category | flops | bytes accessed | tf_op | source)
XLA Modules:
  0.0 206.7 jit_solution(6681729459693451776)
XLA Ops:
  7.5 21.3 %all-gather.1 = bf16[16,140,140]{2,1,0:T(8,128)(2,1)S(1)} all-gather(bf16[1,140,140]{2,1,0:T(8,128)(2,1)S(1)} %bitcast.123), channel_id=1, replica_groups=mesh['tm'=16,'space'=16] {'tm'}, dimensions={0}, use_global_device_ids=true | all-gather | bytes 666400 | tf_op jit(solution)/shard_map/all_gather | solution.py:120
  30.1 2.3 %copy.50 = bf16[2240,140]{0,1:T(8,128)(2,1)} copy(bf16[2240,140]{1,0:T(8,128)(2,1)} %reshape.123) | data formatting | bytes 1254400
  33.5 9.1 %collective-permute-start = (bf16[2,1,64,2240]{3,2,1,0:T(8,128)(2,1)}, bf16[2,1,64,2240]{3,2,1,0:T(8,128)(2,1)}, u32[]{:S(2)}, u32[]{:S(2)}) collective-permute-start(bf16[2,1,64,2240]{3,2,1,0:T(8,128)(2,1)} %get-tuple-element.25), channel_id=1, source_target_pairs={{0,1},{1,2},{2,3},{3,4},{4,5},{5,6},{6,7},{7,8},{8,9},{9,10},{10,1... | collective-permute-start | bytes 1720328 | tf_op jit(solution)/shard_map/ppermute | solution.py:20
  42.7 1.9 collective-permute-start.1
  49.0 3.6 %all_to_all.22 = f32[256,1,980]{2,1,0:T(1,128)} reshape(f32[20,112,112]{2,1,0:T(8,128)S(1)} %fusion.43) | data formatting | bytes 2007040 | tf_op jit(solution)/shard_map/all_to_all | solution.py:40
  52.6 13.4 %all-to-all-start = ((f32[256,1,980]{2,1,0:T(1,128)}), f32[256,1,980]{2,1,0:T(1,128)S(1)}, u32[]{:S(2)}, u32[]{:S(2)}) async-start(f32[256,1,980]{2,1,0:T(1,128)} %all_to_all.22), calls=%async_computation | async-start | bytes 2097152 | tf_op jit(solution)/shard_map/all_to_all | solution.py:40
  66.0 1.7 slice_reduce_fusion.11
  67.7 2.4 %fusion.7 = bf16[2,6,66,2240]{3,2,1,0:T(8,128)(2,1)S(1)} fusion(bf16[2,1,64,2240]{3,2,1,0:T(8,128)(2,1)} %collective-permute-done.1, bf16[2,4,64,2240]{3,2,1,0:T(8,128)(2,1)S(1)} %copy-done, bf16[2,1,64,2240]{3,2,1,0:T(8,128)(2,1)} %collective-permute-done), kind=kLoop, calls=%fused_computation.16 | loop fusion | flops 21288960 | bytes 6988800 | tf_op jit(solution)/shard_map/concatenate | solution.py:24
  70.1 6.8 %add_convert_fusion.1 = bf16[2,4,64,2240]{3,2,1,0:T(8,128)(2,1)} fusion(bf16[2,4,64,2240]{3,2,1,0:T(8,128)(2,1)S(1)} %copy-done, bf16[2,6,66,2240]{3,2,1,0:T(8,128)(2,1)S(1)} %fusion.7, bf16[2,1,64,2240]{3,2,1,0:T(8,128)(2,1)} %collective-permute-done.1, bf16[2,1,64,2240]{3,2,1,0:T(8,128)(2,1)} %collective-permute-done, f32[2240]{0:T(1024)S(1)} %get-tuple-element.20, ...), kind=kLoop, calls=%fused_computation.10 | loop fusion | flops 33259520 | bytes 19577600 | tf_op jit(solution)/shard_map/convert_element_type | solution.py:61
  76.9 32.9 %all-to-all-done = f32[256,1,980]{2,1,0:T(1,128)S(1)} async-done(((f32[256,1,980]{2,1,0:T(1,128)}), f32[256,1,980]{2,1,0:T(1,128)S(1)}, u32[]{:S(2)}, u32[]{:S(2)}) %all-to-all-start) | async-done | bytes 1003552 | tf_op jit(solution)/shard_map/all_to_all | solution.py:40
  114.7 6.8 %all-to-all-start.1 = ((bf16[256,2,490]{2,1,0:T(2,128)(2,1)}), bf16[256,2,490]{2,1,0:T(2,128)(2,1)}, u32[]{:S(2)}, u32[]{:S(2)}) async-start(bf16[256,2,490]{2,1,0:T(2,128)(2,1)} %reshape.136), calls=%async_computation.1 | async-start | bytes 1048576 | tf_op jit(solution)/shard_map/all_to_all | solution.py:45
  121.6 3.5 %broadcast_maximum_fusion.1 = bf16[2,4,64,2240]{3,2,1,0:T(8,128)(2,1)} fusion(bf16[2,4,64,2240]{3,2,1,0:T(8,128)(2,1)} %param.7), kind=kLoop, calls=%fused_computation.25 | loop fusion | flops 1146880 | bytes 4587520 | tf_op jit(solution)/shard_map/max | solution.py:135
  125.1 3.5 %collective-permute-start.2 = (bf16[2,4,64,2240]{3,2,1,0:T(8,128)(2,1)S(1)}, bf16[2,4,64,2240]{3,2,1,0:T(8,128)(2,1)}, u32[]{:S(2)}, u32[]{:S(2)}) collective-permute-start(bf16[2,4,64,2240]{3,2,1,0:T(8,128)(2,1)S(1)} %copy-done.1), channel_id=1, source_target_pairs={{0,16},{16,32},{32,48},{48,64},{64,80},{80,96},{96,112},{112,128},... | collective-permute-start | bytes 6881288 | tf_op jit(solution)/shard_map/ppermute | solution.py:31
  128.5 14.5 %all-to-all-done.1 = bf16[256,2,490]{2,1,0:T(2,128)(2,1)} async-done(((bf16[256,2,490]{2,1,0:T(2,128)(2,1)}), bf16[256,2,490]{2,1,0:T(2,128)(2,1)}, u32[]{:S(2)}, u32[]{:S(2)}) %all-to-all-start.1) | async-done | bytes 501792 | tf_op jit(solution)/shard_map/all_to_all | solution.py:45
  143.0 4.0 %reshape.137 = bf16[256,1,980]{2,1,0:T(2,128)(2,1)S(1)} reshape(bf16[256,2,490]{2,1,0:T(2,128)(2,1)} %all-to-all-done.1) | data formatting | bytes 1003520
  147.0 2.0 copy.39
  148.9 11.9 %reshape.122 = bf16[2240,2240]{1,0:T(8,128)(2,1)} reshape(bf16[16,140,2240]{2,1,0:T(8,128)(2,1)} %all-gather.5.cloned.1.call-done) | data formatting | bytes 20070400 | tf_op jit(solution)/shard_map/optimization_barrier | solution.py:46
  163.7 2.4 %broadcast_select_fusion.1 = (bf16[8,112,8,112]{3,2,1,0:T(8,128)(2,1)}, bf16[8,112,8,112]{3,2,1,0:T(8,128)(2,1)}) fusion(pred[8,8]{1,0:T(8,128)(4,1)S(1)} %iota_compare_fusion.15, bf16[8,112,112]{2,1,0:T(8,128)(2,1)S(1)} %get-tuple-element.27, bf16[8,112,112]{2,1,0:T(8,128)(2,1)S(1)} %get-tuple-element.28), kind=kLoop, calls=%fused_computation.23 | loop fusion | flops 1605632 | bytes 3612736 | tf_op jit(solution)/shard_map/jit(_where)/select_n | solution.py:87
  167.5 4.1 %select_n.40 = bf16[896,896]{1,0:T(8,128)(2,1)} reshape(bf16[8,112,8,112]{3,2,1,0:T(8,128)(2,1)} %get-tuple-element.29) | data formatting | bytes 3211264 | tf_op jit(solution)/shard_map/jit(_where)/select_n | solution.py:87
  171.6 4.1 %select_n.42 = bf16[896,896]{1,0:T(8,128)(2,1)} reshape(bf16[8,112,8,112]{3,2,1,0:T(8,128)(2,1)} %get-tuple-element.30) | data formatting | bytes 3211264 | tf_op jit(solution)/shard_map/jit(_where)/select_n | solution.py:87
  175.7 3.0 %fusion.32 = f32[512,896]{1,0:T(8,128)S(1)} fusion(bf16[896,896]{1,0:T(8,128)(2,1)} %select_n.40, bf16[512,2240]{1,0:T(8,128)(2,1)} %bitcast.117), kind=kOutput, calls=%fused_computation.41 | convolution fusion | flops 822083584 | bytes 4358144 | tf_op jit(solution)/shard_map/dot_general | solution.py:91
  184.3 4.0 %add_convert_fusion = bf16[2,4,64,2240]{3,2,1,0:T(8,128)(2,1)S(1)} fusion(bf16[2,4,64,2240]{3,2,1,0:T(8,128)(2,1)} %collective-permute-done.2, bf16[2,4,64,2240]{3,2,1,0:T(8,128)(2,1)S(1)} %copy-done.1, f32[2,4,64,2240]{3,2,1,0:T(8,128)S(1)} %bitcast.109, f32[2240]{0:T(1024)S(1)} %get-tuple-element.23, f32[2240]{0:T(1024)S(1)} %get-tuple-element.24, ...), kind=kLoop, calls=%fused_computation.9 | loop fusion | flops 13762560 | bytes 11504640 | tf_op jit(solution)/shard_map/convert_element_type | solution.py:144
  188.3 9.0 %convolution_convert_fusion = bf16[512,2240]{0,1:T(8,128)(2,1)S(1)} fusion(bf16[512,2240]{1,0:T(8,128)(2,1)S(1)} %bitcast.120, bf16[2240,2240]{1,0:T(8,128)(2,1)S(1)} %bitcast.114), kind=kOutput, calls=%fused_computation.14 | convolution fusion | flops 5139169280 | bytes 14622720 | tf_op jit(solution)/shard_map/dot_general | solution.py:145
  197.4 2.5 %copy.46 = bf16[512,2240]{1,0:T(8,128)(2,1)} copy(bf16[512,2240]{0,1:T(8,128)(2,1)S(1)} %convolution_convert_fusion) | data formatting | bytes 4587520 | tf_op jit(solution)/shard_map/convert_element_type | solution.py:148
  (82 shorter events, 22.3 us)
Async XLA Ops:
  6.5 142.4 %all-gather.5.cloned.1.call-start = ((), (), s32[]{:S(2)}) async-start(), calls=%async_computation.2 | async-start | bytes 11280384 | tf_op jit(solution)/shard_map/all_gather | solution.py:121
  28.9 3.5 %copy-start = (bf16[2,4,64,2240]{3,2,1,0:T(8,128)(2,1)S(1)}, bf16[2,4,64,2240]{3,2,1,0:T(8,128)(2,1)}, u32[]{:S(2)}) copy-start(bf16[2,4,64,2240]{3,2,1,0:T(8,128)(2,1)} %param.9) | copy-start | bytes 6881284
  32.4 12.2 %copy-start.3 = (bf16[2,4,64,2240]{3,2,1,0:T(8,128)(2,1)S(1)}, bf16[2,4,64,2240]{3,2,1,0:T(8,128)(2,1)}, u32[]{:S(2)}) copy-start(bf16[2,4,64,2240]{3,2,1,0:T(8,128)(2,1)} %param.8) | copy-start | bytes 6881284
  33.5 34.2 %collective-permute-start = (bf16[2,1,64,2240]{3,2,1,0:T(8,128)(2,1)}, bf16[2,1,64,2240]{3,2,1,0:T(8,128)(2,1)}, u32[]{:S(2)}, u32[]{:S(2)}) collective-permute-start(bf16[2,1,64,2240]{3,2,1,0:T(8,128)(2,1)} %get-tuple-element.25), channel_id=1, source_target_pairs={{0,1},{1,2},{2,3},{3,4},{4,5},{5,6},{6,7},{7,8},{8,9},{9,10},{10,1... | collective-permute-start | bytes 1720328 | tf_op jit(solution)/shard_map/ppermute | solution.py:20
  42.7 25.1 %collective-permute-start.1 = (bf16[2,1,64,2240]{3,2,1,0:T(8,128)(2,1)}, bf16[2,1,64,2240]{3,2,1,0:T(8,128)(2,1)}, u32[]{:S(2)}, u32[]{:S(2)}) collective-permute-start(bf16[2,1,64,2240]{3,2,1,0:T(8,128)(2,1)} %get-tuple-element.26), channel_id=1, source_target_pairs={{1,0},{2,1},{3,2},{4,3},{5,4},{6,5},{7,6},{8,7},{9,8},{10,9},{11,1... | collective-permute-start | bytes 1720328 | tf_op jit(solution)/shard_map/ppermute | solution.py:23
  52.6 57.3 %all-to-all-start = ((f32[256,1,980]{2,1,0:T(1,128)}), f32[256,1,980]{2,1,0:T(1,128)S(1)}, u32[]{:S(2)}, u32[]{:S(2)}) async-start(f32[256,1,980]{2,1,0:T(1,128)} %all_to_all.22), calls=%async_computation | async-start | bytes 2097152 | tf_op jit(solution)/shard_map/all_to_all | solution.py:40
  111.4 10.1 %copy-start.7 = (f32[3,2240]{1,0:T(4,128)S(1)}, f32[3,2240]{1,0:T(4,128)}, u32[]{:S(2)}) copy-start(f32[3,2240]{1,0:T(4,128)} %param.12) | copy-start | bytes 80644
  114.7 28.3 %all-to-all-start.1 = ((bf16[256,2,490]{2,1,0:T(2,128)(2,1)}), bf16[256,2,490]{2,1,0:T(2,128)(2,1)}, u32[]{:S(2)}, u32[]{:S(2)}) async-start(bf16[256,2,490]{2,1,0:T(2,128)(2,1)} %reshape.136), calls=%async_computation.1 | async-start | bytes 1048576 | tf_op jit(solution)/shard_map/all_to_all | solution.py:45
  121.6 3.5 %copy-start.1 = (bf16[2,4,64,2240]{3,2,1,0:T(8,128)(2,1)S(1)}, bf16[2,4,64,2240]{3,2,1,0:T(8,128)(2,1)}, u32[]{:S(2)}) copy-start(bf16[2,4,64,2240]{3,2,1,0:T(8,128)(2,1)} %add_convert_fusion.1) | copy-start | bytes 6881284
  125.1 59.2 %collective-permute-start.2 = (bf16[2,4,64,2240]{3,2,1,0:T(8,128)(2,1)S(1)}, bf16[2,4,64,2240]{3,2,1,0:T(8,128)(2,1)}, u32[]{:S(2)}, u32[]{:S(2)}) collective-permute-start(bf16[2,4,64,2240]{3,2,1,0:T(8,128)(2,1)S(1)} %copy-done.1), channel_id=1, source_target_pairs={{0,16},{16,32},{32,48},{48,64},{64,80},{80,96},{96,112},{112,128},... | collective-permute-start | bytes 6881288 | tf_op jit(solution)/shard_map/ppermute | solution.py:31
  148.9 11.9 %copy-start.4 = (bf16[256,1,980]{0,2,1:T(8,128)(2,1)S(1)}, bf16[256,1,980]{0,2,1:T(8,128)(2,1)}, u32[]{:S(2)}) copy-start(bf16[256,1,980]{0,2,1:T(8,128)(2,1)} %copy.39) | copy-start | bytes 1505284
  163.7 2.4 %copy-start.5 = (bf16[448,448]{1,0:T(8,128)(2,1)S(1)}, bf16[448,448]{1,0:T(8,128)(2,1)}, u32[]{:S(2)}) copy-start(bf16[448,448]{1,0:T(8,128)(2,1)} %select_n.44) | copy-start | bytes 1204228
  175.7 3.1 %copy-start.2 = (bf16[2,4,64,2240]{3,2,1,0:T(8,128)(2,1)S(1)}, bf16[2,4,64,2240]{3,2,1,0:T(8,128)(2,1)}, u32[]{:S(2)}) copy-start(bf16[2,4,64,2240]{3,2,1,0:T(8,128)(2,1)} %broadcast_maximum_fusion.1) | copy-start | bytes 6881284
  175.7 3.1 %copy-start.6 = (bf16[896,896]{1,0:T(8,128)(2,1)S(1)}, bf16[896,896]{1,0:T(8,128)(2,1)}, u32[]{:S(2)}) copy-start(bf16[896,896]{1,0:T(8,128)(2,1)} %select_n.42) | copy-start | bytes 4816900
  183.0 1.2 copy-start.8
  183.0 5.2 %slice-start = ((s8[10321920]{0:T(1024)(128)(4,1)}), s8[4194304]{0:T(1024)(128)(4,1)S(1)}, s32[]{:S(2)}) async-start(s8[10321920]{0:T(1024)(128)(4,1)} %bitcast.113), calls=%async_computation.3 | async-start | bytes 8388608
  183.1 5.2 %slice-start.1 = ((s8[10321920]{0:T(1024)(128)(4,1)}), s8[4194304]{0:T(1024)(128)(4,1)S(1)}, s32[]{:S(2)}) async-start(s8[10321920]{0:T(1024)(128)(4,1)} %bitcast.113), calls=%async_computation.4 | async-start | bytes 8388608
  184.3 4.1 %slice-start.2 = ((s8[10321920]{0:T(1024)(128)(4,1)}), s8[1933312]{0:T(1024)(128)(4,1)S(1)}, s32[]{:S(2)}) async-start(s8[10321920]{0:T(1024)(128)(4,1)} %bitcast.113), calls=%async_computation.5 | async-start | bytes 3866624
Sparse Core Ops, SparseCore 0:
  32.5 106.9 all-gather.4

commit v11 on v9

--- a/solution.py
+++ b/solution.py
@@ -130,10 +130,11 @@
     padded = extended(value_heads, (("space", 1),), 1)
     spatial = spatial_conv(padded, spatial_kernel)
     earlier_frames = from_behind(spatial, "tm", 1)
-    weight_flat = weight_stack.transpose(1, 0, 2).reshape(model_width, model_width)
-    state_low, spatial, weight_flat = prefix_state(local_state, spatial, weight_flat)
+    state_low, spatial, _ = prefix_state(local_state, spatial, ())
     flat_queries = jnp.maximum(query_heads.reshape(token_count, model_width), 0)
     attended = banded_attention(flat_queries, state_low)
+    attended, weight_stack = lax.optimization_barrier((attended, weight_stack))
+    weight_flat = weight_stack.transpose(1, 0, 2).reshape(model_width, model_width)
     normed = head_norm(attended).reshape(frame_count, row_count, col_count, model_width) * head_gain
     window = jnp.concatenate([earlier_frames, spatial], axis=0)
     temporal = jnp.zeros(normed.shape, jnp.float32)

time: 199 us -> 199 us (level); the launches traced: 198 us -> 195 us
  waiting for transfers between devices: 47.1 us -> 41.1 us
  other arithmetic: 20.7 us -> 22.8 us
    all_gather x1, waiting for transfers between devices: 13.4 us -> 0.01 us  [per_device(): weight_stack = lax.all_gather(weight_cols, 'tm', axis=0)]
    ppermute x1, waiting for transfers between devices: 0.01 us -> 7.09 us  [from_behind(): return lax.ppermute(block, axis, route)]
    concatenate x0 -> x1, other arithmetic: none -> 2.53 us  [banded_attention(): return jnp.concatenate(pieces, axis=1)]
    dot_general x2, matrix products: 1.94 us -> 4.28 us  [split_dot(): jnp.dot(high.astype(jnp.bfloat16), matrix, preferred_element_type=jnp.flo...]
  transfers between devices with their start and end apart: 6 -> 6, of which waited for: 3 -> 3; matrix products, arithmetic and copies ran while one was open for 33% -> 36% of each run, Pallas kernels for 0% -> 0%
where the time goes in v11:
time: 199 us; the launch traced here: 195 us
  local copies, waits for them, and re-layouts  46.4 us (23%)
  waiting for transfers between devices  41.1 us (21%)
  starting transfers between devices  26.6 us (13%)
  blocking collectives  24.9 us (13%)
  other arithmetic  22.8 us (11%)
  matrix products  19.7 us (10%)
  between operations  13.8 us (7%)
    all_gather x1, blocking collectives, per_device(): weight_cols = lax.all_gather(out_weight, 'space', axis=0, tiled=True)  24.9 us
    all_to_all x1, waiting for transfers between devices, prefix_state(): mine = lax.all_to_all(flat, axes, 0, 0, tiled=True)  21.8 us
    all_to_all x1, waiting for transfers between devices, prefix_state(): gathered = lax.all_to_all(outgoing, axes, 0, 0, tiled=True)  12.2 us
    reshape x1, local copies, waits for them, and re-layouts, per_device(): weight_stack.transpose(1, 0, 2).reshape(model_width, model_width)  11.9 us
    all_to_all x1, starting transfers between devices, prefix_state(): mine = lax.all_to_all(flat, axes, 0, 0, tiled=True)  11 us
    unnamed x47, local copies, waits for them, and re-layouts  10.6 us
    select_n x3, local copies, waits for them, and re-layouts, banded_attention(): jnp.where(eye[:, None, :, None], blocks[:, :, None, :], jnp.zeros((), blo...  8.51 us
    ppermute x1, waiting for transfers between devices, from_behind(): return lax.ppermute(block, axis, route)  7.09 us
  transfers between devices with their start and end apart: 6, of which 3 were waited for; matrix products, arithmetic and copies ran while one was open for 36% of the time, Pallas kernels for 0%

profile of v11, /device:TPU:1, one launch (start us, length us, event | category | flops | bytes accessed | tf_op | source)
XLA Modules:
  0.0 195.2 jit_solution(931594104160273636)
XLA Ops:
  6.5 24.9 %all-gather.1 = bf16[16,140,140]{2,1,0:T(8,128)(2,1)S(1)} all-gather(bf16[1,140,140]{2,1,0:T(8,128)(2,1)} %bitcast.121), channel_id=1, replica_groups=mesh['tm'=16,'space'=16] {'space'}, dimensions={0}, use_global_device_ids=true | all-gather | bytes 666400 | tf_op jit(solution)/shard_map/all_gather | solution.py:120
  32.7 2.2 %copy.47 = bf16[1,2240,140]{1,2,0:T(8,128)(2,1)} copy(bf16[1,2240,140]{2,1,0:T(8,128)(2,1)} %reshape.124) | data formatting | bytes 1254400
  38.1 3.3 %collective-permute-start.1 = (bf16[2,1,64,2240]{3,2,1,0:T(8,128)(2,1)}, bf16[2,1,64,2240]{3,2,1,0:T(8,128)(2,1)}, u32[]{:S(2)}, u32[]{:S(2)}) collective-permute-start(bf16[2,1,64,2240]{3,2,1,0:T(8,128)(2,1)} %get-tuple-element.26), channel_id=1, source_target_pairs={{1,0},{2,1},{3,2},{4,3},{5,4},{6,5},{7,6},{8,7},{9,8},{10,9},{11,1... | collective-permute-start | bytes 1720328 | tf_op jit(solution)/shard_map/ppermute | solution.py:23
  45.7 3.6 %all_to_all.22 = f32[256,1,980]{2,1,0:T(1,128)} reshape(f32[20,112,112]{2,1,0:T(8,128)S(1)} %fusion.43) | data formatting | bytes 2007040 | tf_op jit(solution)/shard_map/all_to_all | solution.py:40
  49.4 11.0 %all-to-all-start = ((f32[256,1,980]{2,1,0:T(1,128)}), f32[256,1,980]{2,1,0:T(1,128)S(1)}, u32[]{:S(2)}, u32[]{:S(2)}) async-start(f32[256,1,980]{2,1,0:T(1,128)} %all_to_all.22), calls=%async_computation | async-start | bytes 2097152 | tf_op jit(solution)/shard_map/all_to_all | solution.py:40
  61.9 2.4 %fusion.7 = bf16[2,6,66,2240]{3,2,1,0:T(8,128)(2,1)S(1)} fusion(bf16[2,1,64,2240]{3,2,1,0:T(8,128)(2,1)} %collective-permute-done.1, bf16[2,4,64,2240]{3,2,1,0:T(8,128)(2,1)S(1)} %copy-done.1, bf16[2,1,64,2240]{3,2,1,0:T(8,128)(2,1)} %collective-permute-done), kind=kLoop, calls=%fused_computation.16 | loop fusion | flops 21288960 | bytes 6988800 | tf_op jit(solution)/shard_map/concatenate | solution.py:24
  64.3 6.8 %add_convert_fusion.1 = bf16[2,4,64,2240]{3,2,1,0:T(8,128)(2,1)} fusion(bf16[2,4,64,2240]{3,2,1,0:T(8,128)(2,1)S(1)} %copy-done.1, bf16[2,6,66,2240]{3,2,1,0:T(8,128)(2,1)S(1)} %fusion.7, bf16[2,1,64,2240]{3,2,1,0:T(8,128)(2,1)} %collective-permute-done.1, bf16[2,1,64,2240]{3,2,1,0:T(8,128)(2,1)} %collective-permute-done, f32[2240]{0:T(1024)S(1)} %get-tuple-element.20, ...), kind=kLoop, calls=%fused_computation.10 | loop fusion | flops 33259520 | bytes 19577600 | tf_op jit(solution)/shard_map/convert_element_type | solution.py:61
  71.1 21.8 %all-to-all-done = f32[256,1,980]{2,1,0:T(1,128)S(1)} async-done(((f32[256,1,980]{2,1,0:T(1,128)}), f32[256,1,980]{2,1,0:T(1,128)S(1)}, u32[]{:S(2)}, u32[]{:S(2)}) %all-to-all-start) | async-done | bytes 1003552 | tf_op jit(solution)/shard_map/all_to_all | solution.py:40
  97.6 6.8 %all-to-all-start.1 = ((bf16[256,2,490]{2,1,0:T(2,128)(2,1)}), bf16[256,2,490]{2,1,0:T(2,128)(2,1)}, u32[]{:S(2)}, u32[]{:S(2)}) async-start(bf16[256,2,490]{2,1,0:T(2,128)(2,1)} %reshape.137), calls=%async_computation.1 | async-start | bytes 1048576 | tf_op jit(solution)/shard_map/all_to_all | solution.py:45
  104.6 3.4 %broadcast_maximum_fusion.1 = bf16[2,4,64,2240]{3,2,1,0:T(8,128)(2,1)} fusion(bf16[2,4,64,2240]{3,2,1,0:T(8,128)(2,1)} %param.7), kind=kLoop, calls=%fused_computation.25 | loop fusion | flops 1146880 | bytes 4587520 | tf_op jit(solution)/shard_map/max | solution.py:134
  108.0 3.5 %collective-permute-start.2 = (bf16[2,4,64,2240]{3,2,1,0:T(8,128)(2,1)S(1)}, bf16[2,4,64,2240]{3,2,1,0:T(8,128)(2,1)}, u32[]{:S(2)}, u32[]{:S(2)}) collective-permute-start(bf16[2,4,64,2240]{3,2,1,0:T(8,128)(2,1)S(1)} %copy-done.2), channel_id=1, source_target_pairs={{0,16},{16,32},{32,48},{48,64},{64,80},{80,96},{96,112},{112,128},... | collective-permute-start | bytes 6881288 | tf_op jit(solution)/shard_map/ppermute | solution.py:31
  111.5 12.2 %all-to-all-done.1 = bf16[256,2,490]{2,1,0:T(2,128)(2,1)} async-done(((bf16[256,2,490]{2,1,0:T(2,128)(2,1)}), bf16[256,2,490]{2,1,0:T(2,128)(2,1)}, u32[]{:S(2)}, u32[]{:S(2)}) %all-to-all-start.1) | async-done | bytes 501792 | tf_op jit(solution)/shard_map/all_to_all | solution.py:45
  123.7 4.0 %reshape.138 = bf16[256,1,980]{2,1,0:T(2,128)(2,1)S(1)} reshape(bf16[256,2,490]{2,1,0:T(2,128)(2,1)} %all-to-all-done.1) | data formatting | bytes 1003520
  132.1 2.4 %broadcast_select_fusion.1 = (bf16[8,112,8,112]{3,2,1,0:T(8,128)(2,1)}, bf16[8,112,8,112]{3,2,1,0:T(8,128)(2,1)}) fusion(pred[8,8]{1,0:T(8,128)(4,1)S(1)} %iota_compare_fusion.15, bf16[8,112,112]{2,1,0:T(8,128)(2,1)S(1)} %get-tuple-element.27, bf16[8,112,112]{2,1,0:T(8,128)(2,1)S(1)} %get-tuple-element.28), kind=kLoop, calls=%fused_computation.23 | loop fusion | flops 1605632 | bytes 3612736 | tf_op jit(solution)/shard_map/jit(_where)/select_n | solution.py:87
  134.5 4.1 %select_n.40 = bf16[896,896]{1,0:T(8,128)(2,1)} reshape(bf16[8,112,8,112]{3,2,1,0:T(8,128)(2,1)} %get-tuple-element.29) | data formatting | bytes 3211264 | tf_op jit(solution)/shard_map/jit(_where)/select_n | solution.py:87
  138.6 4.1 %select_n.42 = bf16[896,896]{1,0:T(8,128)(2,1)} reshape(bf16[8,112,8,112]{3,2,1,0:T(8,128)(2,1)} %get-tuple-element.30) | data formatting | bytes 3211264 | tf_op jit(solution)/shard_map/jit(_where)/select_n | solution.py:87
  143.3 3.1 %fusion.32 = f32[512,896]{1,0:T(8,128)S(1)} fusion(bf16[896,896]{1,0:T(8,128)(2,1)} %select_n.40, bf16[512,2240]{1,0:T(8,128)(2,1)} %bitcast.115), kind=kOutput, calls=%fused_computation.41 | convolution fusion | flops 822083584 | bytes 4358144 | tf_op jit(solution)/shard_map/dot_general | solution.py:91
  148.1 2.5 %pad_maximum_fusion = f32[512,2240]{1,0:T(8,128)} fusion(f32[512,448]{1,0:T(8,128)S(1)} %fusion.38, f32[512,896]{1,0:T(8,128)S(1)} %fusion.24, f32[512,896]{1,0:T(8,128)S(1)} %fusion.32), kind=kLoop, calls=%fused_computation.8 | loop fusion | flops 2293760 | bytes 9175040 | tf_op jit(solution)/shard_map/concatenate | solution.py:97
  150.6 11.9 %reshape.115 = bf16[2240,2240]{0,1:T(8,128)(2,1)} reshape(bf16[2240,16,140]{0,2,1:T(8,128)(2,1)} %bitcast.111) | data formatting | bytes 20070400 | tf_op jit(solution)/shard_map/reshape | solution.py:137
  162.5 3.3 %fusion.8 = f32[512,20]{0,1:T(8,128)S(1)} fusion(f32[512,2240]{1,0:T(8,128)} %pad_maximum_fusion, s32[2240]{0:T(1024)S(1)} %add_select_fusion), kind=kOutput, calls=%fused_computation.17 | convolution fusion | flops 49360640 | bytes 4637440 | tf_op jit(solution)/shard_map/dot_general | solution.py:103
  169.5 7.1 %collective-permute-done.2 = bf16[2,4,64,2240]{3,2,1,0:T(8,128)(2,1)} collective-permute-done((bf16[2,4,64,2240]{3,2,1,0:T(8,128)(2,1)S(1)}, bf16[2,4,64,2240]{3,2,1,0:T(8,128)(2,1)}, u32[]{:S(2)}, u32[]{:S(2)}) %collective-permute-start.2) | collective-permute-done | bytes 2293792 | tf_op jit(solution)/shard_map/ppermute | solution.py:31
  176.6 3.5 %add_convert_fusion = bf16[2,4,64,2240]{3,2,1,0:T(8,128)(2,1)S(1)} fusion(bf16[2,4,64,2240]{3,2,1,0:T(8,128)(2,1)} %collective-permute-done.2, bf16[2,4,64,2240]{3,2,1,0:T(8,128)(2,1)S(1)} %copy-done.2, f32[2,4,64,2240]{3,2,1,0:T(8,128)S(1)} %bitcast.107, f32[2240]{0:T(1024)S(1)} %get-tuple-element.23, f32[2240]{0:T(1024)S(1)} %get-tuple-element.24, ...), kind=kLoop, calls=%fused_computation.9 | loop fusion | flops 13762560 | bytes 11504640 | tf_op jit(solution)/shard_map/convert_element_type | solution.py:145
  180.1 5.8 %convolution_convert_fusion = bf16[512,2240]{0,1:T(8,128)(2,1)S(1)} fusion(bf16[512,2240]{1,0:T(8,128)(2,1)S(1)} %bitcast.118, bf16[2240,2240]{0,1:T(8,128)(2,1)S(1)} %bitcast.113), kind=kOutput, calls=%fused_computation.14 | convolution fusion | flops 5139169280 | bytes 14622720 | tf_op jit(solution)/shard_map/dot_general | solution.py:146
  185.9 2.5 %copy.43 = bf16[512,2240]{1,0:T(8,128)(2,1)} copy(bf16[512,2240]{0,1:T(8,128)(2,1)S(1)} %convolution_convert_fusion) | data formatting | bytes 4587520 | tf_op jit(solution)/shard_map/convert_element_type | solution.py:149
  (83 shorter events, 25.4 us)
Async XLA Ops:
  6.5 144.1 %all-gather.5.cloned.1.call-start = ((), (), s32[]{:S(2)}) async-start(), calls=%async_computation.2 | async-start | bytes 11280384 | tf_op jit(solution)/shard_map/all_gather | solution.py:121
  31.4 3.5 %copy-start.1 = (bf16[2,4,64,2240]{3,2,1,0:T(8,128)(2,1)S(1)}, bf16[2,4,64,2240]{3,2,1,0:T(8,128)(2,1)}, u32[]{:S(2)}) copy-start(bf16[2,4,64,2240]{3,2,1,0:T(8,128)(2,1)} %param.9) | copy-start | bytes 6881284
  34.9 6.4 %copy-start.4 = (bf16[2,4,64,2240]{3,2,1,0:T(8,128)(2,1)S(1)}, bf16[2,4,64,2240]{3,2,1,0:T(8,128)(2,1)}, u32[]{:S(2)}) copy-start(bf16[2,4,64,2240]{3,2,1,0:T(8,128)(2,1)} %param.8) | copy-start | bytes 6881284
  36.0 25.8 %collective-permute-start = (bf16[2,1,64,2240]{3,2,1,0:T(8,128)(2,1)}, bf16[2,1,64,2240]{3,2,1,0:T(8,128)(2,1)}, u32[]{:S(2)}, u32[]{:S(2)}) collective-permute-start(bf16[2,1,64,2240]{3,2,1,0:T(8,128)(2,1)} %get-tuple-element.25), channel_id=1, source_target_pairs={{0,1},{1,2},{2,3},{3,4},{4,5},{5,6},{6,7},{7,8},{8,9},{9,10},{10,1... | collective-permute-start | bytes 1720328 | tf_op jit(solution)/shard_map/ppermute | solution.py:20
  38.1 23.8 %collective-permute-start.1 = (bf16[2,1,64,2240]{3,2,1,0:T(8,128)(2,1)}, bf16[2,1,64,2240]{3,2,1,0:T(8,128)(2,1)}, u32[]{:S(2)}, u32[]{:S(2)}) collective-permute-start(bf16[2,1,64,2240]{3,2,1,0:T(8,128)(2,1)} %get-tuple-element.26), channel_id=1, source_target_pairs={{1,0},{2,1},{3,2},{4,3},{5,4},{6,5},{7,6},{8,7},{9,8},{10,9},{11,1... | collective-permute-start | bytes 1720328 | tf_op jit(solution)/shard_map/ppermute | solution.py:23
  49.4 43.5 %all-to-all-start = ((f32[256,1,980]{2,1,0:T(1,128)}), f32[256,1,980]{2,1,0:T(1,128)S(1)}, u32[]{:S(2)}, u32[]{:S(2)}) async-start(f32[256,1,980]{2,1,0:T(1,128)} %all_to_all.22), calls=%async_computation | async-start | bytes 2097152 | tf_op jit(solution)/shard_map/all_to_all | solution.py:40
  94.4 10.1 %copy-start.7 = (f32[3,2240]{1,0:T(4,128)S(1)}, f32[3,2240]{1,0:T(4,128)}, u32[]{:S(2)}) copy-start(f32[3,2240]{1,0:T(4,128)} %param.12) | copy-start | bytes 80644
  97.6 26.0 %all-to-all-start.1 = ((bf16[256,2,490]{2,1,0:T(2,128)(2,1)}), bf16[256,2,490]{2,1,0:T(2,128)(2,1)}, u32[]{:S(2)}, u32[]{:S(2)}) async-start(bf16[256,2,490]{2,1,0:T(2,128)(2,1)} %reshape.137), calls=%async_computation.1 | async-start | bytes 1048576 | tf_op jit(solution)/shard_map/all_to_all | solution.py:45
  104.6 3.4 %copy-start.2 = (bf16[2,4,64,2240]{3,2,1,0:T(8,128)(2,1)S(1)}, bf16[2,4,64,2240]{3,2,1,0:T(8,128)(2,1)}, u32[]{:S(2)}) copy-start(bf16[2,4,64,2240]{3,2,1,0:T(8,128)(2,1)} %add_convert_fusion.1) | copy-start | bytes 6881284
  108.0 68.6 %collective-permute-start.2 = (bf16[2,4,64,2240]{3,2,1,0:T(8,128)(2,1)S(1)}, bf16[2,4,64,2240]{3,2,1,0:T(8,128)(2,1)}, u32[]{:S(2)}, u32[]{:S(2)}) collective-permute-start(bf16[2,4,64,2240]{3,2,1,0:T(8,128)(2,1)S(1)} %copy-done.2), channel_id=1, source_target_pairs={{0,16},{16,32},{32,48},{48,64},{64,80},{80,96},{96,112},{112,128},... | collective-permute-start | bytes 6881288 | tf_op jit(solution)/shard_map/ppermute | solution.py:31
  132.0 2.5 %copy-start.5 = (bf16[20,112,112]{2,1,0:T(8,128)(2,1)}, bf16[20,112,112]{2,1,0:T(8,128)(2,1)S(1)}, u32[]{:S(2)}) copy-start(bf16[20,112,112]{2,1,0:T(8,128)(2,1)S(1)} %reshape.112) | copy-start | bytes 1505284
  138.6 4.1 %slice-start.3 = ((bf16[20,112,112]{2,1,0:T(8,128)(2,1)}), bf16[4,112,112]{2,1,0:T(8,128)(2,1)S(1)}, s32[]{:S(2)}) async-start(bf16[20,112,112]{2,1,0:T(8,128)(2,1)} %copy-done.5), calls=%async_computation.6 | async-start | bytes 229376 | tf_op jit(solution)/shard_map/slice | solution.py:85
  143.3 3.1 %copy-start.3 = (bf16[2,4,64,2240]{3,2,1,0:T(8,128)(2,1)S(1)}, bf16[2,4,64,2240]{3,2,1,0:T(8,128)(2,1)}, u32[]{:S(2)}) copy-start(bf16[2,4,64,2240]{3,2,1,0:T(8,128)(2,1)} %broadcast_maximum_fusion.1) | copy-start | bytes 6881284
  143.3 3.1 %copy-start.6 = (bf16[896,896]{1,0:T(8,128)(2,1)S(1)}, bf16[896,896]{1,0:T(8,128)(2,1)}, u32[]{:S(2)}) copy-start(bf16[896,896]{1,0:T(8,128)(2,1)} %select_n.42) | copy-start | bytes 4816900
  162.5 3.8 %copy-start = (f32[512,2240]{1,0:T(8,128)S(1)}, f32[512,2240]{1,0:T(8,128)}, u32[]{:S(2)}) copy-start(f32[512,2240]{1,0:T(8,128)} %pad_maximum_fusion) | copy-start | bytes 13762564
  168.3 8.3 %copy-start.8 = (f32[2240]{0:T(1024)S(1)}, f32[2240]{0:T(1024)}, u32[]{:S(2)}) copy-start(f32[2240]{0:T(1024)} %param.10) | copy-start | bytes 26884
  168.3 11.8 %slice-start = ((s8[10321920]{0:T(1024)(128)(4,1)}), s8[4194304]{0:T(1024)(128)(4,1)S(1)}, s32[]{:S(2)}) async-start(s8[10321920]{0:T(1024)(128)(4,1)} %bitcast.112), calls=%async_computation.3 | async-start | bytes 8388608
  168.3 11.8 %slice-start.1 = ((s8[10321920]{0:T(1024)(128)(4,1)}), s8[1933312]{0:T(1024)(128)(4,1)S(1)}, s32[]{:S(2)}) async-start(s8[10321920]{0:T(1024)(128)(4,1)} %bitcast.112), calls=%async_computation.4 | async-start | bytes 3866624
  176.6 3.5 %slice-start.2 = ((s8[10321920]{0:T(1024)(128)(4,1)}), s8[4194304]{0:T(1024)(128)(4,1)S(1)}, s32[]{:S(2)}) async-start(s8[10321920]{0:T(1024)(128)(4,1)} %bitcast.112), calls=%async_computation.5 | async-start | bytes 8388608
Sparse Core Ops, SparseCore 0:
  35.1 108.0 all-gather.4
